TPU v7x, 256 devices: a whole 4x4x8 slice. The times are simulated.
256 devices in a mesh: dom: 128 (over y, x, z), col: 2 (over core).
Axes of the slice: x: 4, y: 4, z: 8, core: 2. Of those that a mesh axis runs over, the one named last changes fastest.
Arguments:
- src_local: int32 [262144], P('dom'), may hold values from 0 to 4095
- dst_local: int32 [262144], P('dom'), may hold values from 0 to 4095
- edge_weight: float32 [262144], P('dom'), may hold values from 0.25 to 4
- send_counts: int32 [128, 128], P('dom'), may hold values from 1 to 16, as said below
- sketch: bfloat16 [128, 262144], P('col', 'dom'), may hold values from -6 to 6
Outputs:
- solution: float32 [128, 524288], P('col', 'dom')
- resistance: float32 [262144], P('dom')
Inputs may be any that keep to these rules, and one draw needn't show every extreme that they name: Each row of send_counts reaches 16 for some peer, and one peer receives 16 live slots from every partition.
All inputs are finite; a program needn't handle non-finite values.
Results may differ from a plain program's by a relative error of at most 0.0003.
Values sent between devices are 32-bit elements; how exact they have to be, the bound alone decides.
No kernel may reach another device: no remote copies, remote signals or barrier semaphores. Data moves between devices by JAX's collectives and lax.ppermute only.
A program may use at most 64 MiB of HBM per device.

v0:
```python
import jax
import jax.numpy as jnp
from jax import lax
from jax.sharding import PartitionSpec as P

SKETCH = 128
VERT_DEV = 4096
SWEEPS = 3


ground_shift = 1.0
degree_boost = 0.25


def local(src_local, dst_local, edge_weight, send_counts, sketch):
    peers = lax.axis_size("dom")
    edges = src_local.shape[0]
    cap = edges // peers
    width = sketch.shape[0]
    live = (jnp.arange(cap)[None, :] < send_counts.reshape(peers, 1)).astype(jnp.float32)
    w_out = (edge_weight.reshape(peers, cap) * live).reshape(-1)
    root = jnp.sqrt(w_out)[:, None] * sketch.astype(jnp.float32).T
    payload = jnp.concatenate(
        [root, w_out[:, None], dst_local.astype(jnp.float32)[:, None]], axis=1
    )
    arrived = lax.all_to_all(payload, "dom", split_axis=0, concat_axis=0, tiled=True)
    arrived_root = arrived[:, :width]
    w_in = arrived[:, width]
    wanted = arrived[:, width + 1].astype(jnp.int32)

    both = jnp.stack(
        [src_local.reshape(peers, cap), wanted.reshape(peers, cap)], axis=1
    ).reshape(-1)
    zero_rows = jnp.zeros((VERT_DEV, width), jnp.float32)
    rhs = zero_rows.at[both].add(
        jnp.stack(
            [root.reshape(peers, cap, width), -arrived_root.reshape(peers, cap, width)],
            axis=1,
        ).reshape(-1, width)
    )
    w_both = jnp.stack([w_out.reshape(peers, cap), w_in.reshape(peers, cap)], axis=1).reshape(-1)
    degree = jnp.zeros((VERT_DEV,), jnp.float32).at[both].add(w_both)
    diag = ((1.0 + degree_boost) * degree + ground_shift)[:, None]
    extra = (degree_boost * degree + ground_shift)[:, None]

    def apply(field):
        here = field[both].reshape(peers, 2, cap, width)
        there = lax.all_to_all(here, "dom", split_axis=0, concat_axis=0, tiled=True)
        flow_out = w_out.reshape(peers, cap, 1) * (here[:, 0] - there[:, 1])
        flow_in = w_in.reshape(peers, cap, 1) * (there[:, 0] - here[:, 1])
        flows = jnp.stack([flow_out, -flow_in], axis=1).reshape(-1, width)
        return zero_rows.at[both].add(flows) + extra * field

    sigma = 1.25
    delta = 0.8
    coeff = 1.0 / sigma
    resid = rhs
    direction = resid / diag
    solution = zero_rows
    for sweep in range(SWEEPS):
        solution = solution + direction
        if sweep < SWEEPS - 1:
            resid = resid - apply(direction)
            newer = 1.0 / (2.0 * sigma - coeff)
            direction = newer * coeff * direction + 2.0 * newer / delta * resid / diag
            coeff = newer
    far = lax.all_to_all(
        solution[wanted], "dom", split_axis=0, concat_axis=0, tiled=True
    )
    diff = solution[src_local] - far
    partial_sum = jnp.sum(diff * diff, axis=1) * live.reshape(-1)
    resistance = lax.psum(partial_sum, "col") / SKETCH
    return (solution.T, resistance)


def solution(mesh):
    in_specs = (P("dom"), P("dom"), P("dom"), P("dom", None), P("col", "dom"))
    out_specs = (P("col", "dom"), P("dom"))
    return jax.shard_map(local, mesh=mesh, in_specs=in_specs, out_specs=out_specs, check_vma=False)
```

profile of v0, /device:TPU:1, one launch (start us, length us, event | category | flops | bytes accessed | tf_op | source)
XLA Modules:
  0.0 337.0 jit_solution(13985790518361709083)
XLA Ops:
  0.6 0.7 convert_element_type.23
  1.3 1.8 concatenate.11
  3.2 1.6 reshape.287
  4.9 0.2 fusion.9
  5.2 0.8 multiply_bitcast_fusion
  6.1 1.4 copy.38
  7.4 1.6 pad_maximum_fusion.3
  9.0 16.5 %all-to-all-start = ((f32[128,16,66]{2,1,0:T(8,128)}), f32[128,16,66]{2,1,0:T(8,128)S(1)}, u32[]{:S(2)}, u32[]{:S(2)}) async-start(f32[128,16,66]{2,1,0:T(8,128)} %pad_maximum_fusion.3), calls=%async_computation | async-start | bytes 2097152 | tf_op jit(solution)/shard_map/all_to_all | solution.py:26
  25.8 30.0 %all-to-all-done = f32[128,16,66]{2,1,0:T(8,128)S(1)} async-done(((f32[128,16,66]{2,1,0:T(8,128)}), f32[128,16,66]{2,1,0:T(8,128)S(1)}, u32[]{:S(2)}, u32[]{:S(2)}) %all-to-all-start) | async-done | bytes 540704 | tf_op jit(solution)/shard_map/all_to_all | solution.py:26
  55.7 0.9 fusion
  56.6 0.6 slice_reduce_fusion
  58.2 21.9 %scatter_custom_fusion.1 = f32[4096]{0:T(1024)S(1)} fusion(s32[4096]{0:T(1024)S(1)} %bitcast.33, f32[4096]{0:T(1024)S(1)} %reshape.266, f32[]{:T(128)} %constant.11.clone.1), kind=kCustom, calls=%fused_computation.51 | custom fusion | flops 4096 | bytes 16388 | tf_op jit(solution)/shard_map/scatter-add | solution.py:42
  80.3 0.2 copy.43
  80.5 23.8 %scatter_custom_fusion = f32[4096,64]{1,0:T(8,128)} fusion(s32[4096]{0:T(1024)S(1)} %bitcast.34, f32[4096,64]{1,0:T(8,128)S(1)} %bitcast.31, f32[]{:T(128)} %constant.11.clone.1), kind=kCustom, calls=%fused_computation.34 | custom fusion | flops 262144 | bytes 1048580 | tf_op jit(solution)/shard_map/scatter-add | solution.py:35
  104.3 4.9 %broadcast_multiply_fusion.1 = (f32[4096,64]{1,0:T(8,128)}, f32[4096,64]{1,0:T(8,128)S(1)}) fusion(f32[4096]{0:T(1024)S(1)} %get-tuple-element.24, f32[4096,64]{1,0:T(8,128)} %scatter_custom_fusion, f32[4096]{0:T(1024)S(1)} %get-tuple-element.23), kind=kLoop, calls=%fused_computation.31 | loop fusion | flops 524288 | bytes 3178496 | tf_op jit(solution)/shard_map/mul | solution.py:52
  109.2 14.1 %gather_fusion = f32[4096,64]{1,0:T(8,128)} fusion(f32[4096,64]{1,0:T(8,128)S(1)} %get-tuple-element.18, s32[4096]{0:T(1024)S(1)} %broadcast_clamp_fusion), kind=kCustom, calls=%fused_computation | custom fusion | bytes 2113536 | tf_op jit(solution)/shard_map/gather | solution.py:47
  123.3 3.4 %reshape.296 = f32[128,1,2048]{2,1,0:T(1,128)} reshape(f32[128,2,16,64]{3,2,1,0:T(8,128)} %bitcast.17) | data formatting | bytes 2097152
  126.7 6.2 %all-to-all-start.1 = ((f32[128,1,2048]{2,1,0:T(1,128)}), f32[128,1,2048]{2,1,0:T(1,128)S(1)}, u32[]{:S(2)}, u32[]{:S(2)}) async-start(f32[128,1,2048]{2,1,0:T(1,128)} %reshape.296), calls=%async_computation.1 | async-start | bytes 2097152 | tf_op jit(solution)/shard_map/all_to_all | solution.py:48
  133.2 28.2 %all-to-all-done.1 = f32[128,1,2048]{2,1,0:T(1,128)S(1)} async-done(((f32[128,1,2048]{2,1,0:T(1,128)}), f32[128,1,2048]{2,1,0:T(1,128)S(1)}, u32[]{:S(2)}, u32[]{:S(2)}) %all-to-all-start.1) | async-done | bytes 1048608 | tf_op jit(solution)/shard_map/all_to_all | solution.py:48
  161.5 1.0 copy-done.1
  162.4 0.5 broadcast.164
  162.9 4.4 %reduce.8 = f32[128,2048]{1,0:T(8,128)S(1)} reduce(f32[128,1,2048]{2,1,0:T(1,128)} %copy-done.1, f32[]{:T(128)} %broadcast.164), dimensions={1}, to_apply=%all_to_all.20.reduce_sub_computation | reduce | bytes 2097156 | tf_op jit(solution)/shard_map/all_to_all | solution.py:48
  167.3 2.1 reshape.297
  169.4 2.5 fusion.6
  172.0 1.5 pad_maximum_fusion.1
  173.5 23.3 %scatter_fusion = f32[4096,64]{1,0:T(8,128)} fusion(f32[4096,64]{1,0:T(8,128)} %get-tuple-element.17, s32[4096]{0:T(1024)S(1)} %bitcast.35, f32[4096,64]{1,0:T(8,128)} %bitcast.26), kind=kCustom, calls=%fused_computation.6 | custom fusion | flops 262144 | bytes 3162112 | tf_op jit(solution)/shard_map/scatter-add | solution.py:52
  196.8 4.7 %broadcast_multiply_fusion = (f32[4096,64]{1,0:T(8,128)}, f32[4096,64]{1,0:T(8,128)}, f32[4096,64]{1,0:T(8,128)}) fusion(f32[4096]{0:T(1024)S(1)} %get-tuple-element.24, f32[4096]{0:T(1024)S(1)} %get-tuple-element.23, f32[4096,64]{1,0:T(8,128)S(1)} %get-tuple-element.18, f32[4096,64]{1,0:T(8,128)} %scatter_custom_fusion, f32[4096,64]{1,0:T(8,128)} %scatter_fusion), kind=kLoop, calls=%fused_computation.30 | loop fusion | flops 1572864 | bytes 6324224 | tf_op jit(solution)/shard_map/mul | solution.py:52
  201.5 15.7 %gather_fusion.1 = f32[4096,64]{1,0:T(8,128)} fusion(f32[4096,64]{1,0:T(8,128)} %get-tuple-element.15, s32[4096]{0:T(1024)S(1)} %broadcast_clamp_fusion), kind=kCustom, calls=%fused_computation.1 | custom fusion | bytes 2113536 | tf_op jit(solution)/shard_map/gather | solution.py:47
  217.1 3.4 %reshape.298 = f32[128,1,2048]{2,1,0:T(1,128)} reshape(f32[128,2,16,64]{3,2,1,0:T(8,128)} %bitcast.19) | data formatting | bytes 2097152
  220.6 7.3 %all-to-all-start.2 = ((f32[128,1,2048]{2,1,0:T(1,128)}), f32[128,1,2048]{2,1,0:T(1,128)}, u32[]{:S(2)}, u32[]{:S(2)}) async-start(f32[128,1,2048]{2,1,0:T(1,128)} %reshape.298), calls=%async_computation.2 | async-start | bytes 2097152 | tf_op jit(solution)/shard_map/all_to_all | solution.py:48
  227.9 26.1 %all-to-all-done.2 = f32[128,1,2048]{2,1,0:T(1,128)} async-done(((f32[128,1,2048]{2,1,0:T(1,128)}), f32[128,1,2048]{2,1,0:T(1,128)}, u32[]{:S(2)}, u32[]{:S(2)}) %all-to-all-start.2) | async-done | bytes 1048608 | tf_op jit(solution)/shard_map/all_to_all | solution.py:48
  254.0 4.4 %reduce.9 = f32[128,2048]{1,0:T(8,128)S(1)} reduce(f32[128,1,2048]{2,1,0:T(1,128)} %all-to-all-done.2, f32[]{:T(128)} %broadcast.164), dimensions={1}, to_apply=%all_to_all.21.reduce_sub_computation | reduce | bytes 2097156 | tf_op jit(solution)/shard_map/all_to_all | solution.py:48
  258.4 2.2 reshape.299
  260.6 2.5 fusion.3
  263.1 1.5 pad_maximum_fusion.2
  264.6 23.3 %scatter_fusion.1 = f32[4096,64]{1,0:T(8,128)} fusion(f32[4096,64]{1,0:T(8,128)} %get-tuple-element.14, s32[4096]{0:T(1024)S(1)} %bitcast.36, f32[4096,64]{1,0:T(8,128)} %bitcast.27), kind=kCustom, calls=%fused_computation.7 | custom fusion | flops 262144 | bytes 3162112 | tf_op jit(solution)/shard_map/scatter-add | solution.py:52
  287.9 4.1 %add_add_fusion = f32[4096,64]{1,0:T(8,128)} fusion(f32[4096,64]{1,0:T(8,128)} %get-tuple-element.16, f32[4096,64]{1,0:T(8,128)} %scatter_fusion.1, f32[4096,64]{1,0:T(8,128)} %get-tuple-element.15, f32[4096,64]{1,0:T(8,128)S(1)} %get-tuple-element.18, f32[4096]{0:T(1024)S(1)} %get-tuple-element.23), kind=kLoop, calls=%fused_computation.12 | loop fusion | flops 1835008 | bytes 5259264 | tf_op jit(solution)/shard_map/add | solution.py:61
  292.0 7.0 %gather_fusion.3 = f32[2048,64]{1,0:T(8,128)S(1)} fusion(f32[4096,64]{1,0:T(8,128)} %add_add_fusion, s32[2048]{0:T(1024)S(1)} %broadcast_clamp_fusion.1), kind=kCustom, calls=%fused_computation.3 | custom fusion | bytes 1056768 | tf_op jit(solution)/shard_map/gather | solution.py:68
  299.1 1.5 reshape.300
  300.6 7.6 %all-to-all-start.3 = ((f32[128,1,1024]{2,1,0:T(1,128)}), f32[128,1,1024]{2,1,0:T(1,128)}, u32[]{:S(2)}, u32[]{:S(2)}) async-start(f32[128,1,1024]{2,1,0:T(1,128)} %reshape.300), calls=%async_computation.3 | async-start | bytes 1048576 | tf_op jit(solution)/shard_map/all_to_all | solution.py:67
  308.2 1.6 copy.45
  309.7 5.5 %gather_fusion.2 = f32[2048,64]{1,0:T(8,128)S(1)} fusion(f32[4096,64]{1,0:T(8,128)S(1)} %copy-done, s32[2048]{0:T(1024)S(1)} %fusion.12), kind=kCustom, calls=%fused_computation.2 | custom fusion | bytes 1056768 | tf_op jit(solution)/shard_map/gather | solution.py:70
  315.2 7.9 %all-to-all-done.3 = f32[128,1,1024]{2,1,0:T(1,128)} async-done(((f32[128,1,1024]{2,1,0:T(1,128)}), f32[128,1,1024]{2,1,0:T(1,128)}, u32[]{:S(2)}, u32[]{:S(2)}) %all-to-all-start.3) | async-done | bytes 524320 | tf_op jit(solution)/shard_map/all_to_all | solution.py:67
  323.1 2.9 reduce.10
  326.0 0.3 reshape.301
  326.3 0.3 multiply_reduce_fusion
  326.7 9.7 %psum.7 = f32[2048]{0:T(1024)S(1)} all-reduce(f32[2048]{0:T(1024)S(1)} %broadcast_select_fusion.1), channel_id=1, replica_groups=mesh['dom'=128,'col'=2] {'col'}, use_global_device_ids=true, to_apply=%region_5.0 | all-reduce | flops 2048 | bytes 16384 | tf_op jit(solution)/shard_map/psum | solution.py:72
  336.4 0.6 broadcast_multiply_fusion.2
  (39 shorter events, 1.8 us)
Async XLA Ops:
  0.6 4.1 %copy-start.6 = (s32[1,128]{1,0:T(1,128)S(1)}, s32[1,128]{1,0:T(1,128)}, u32[]{:S(2)}) copy-start(s32[1,128]{1,0:T(1,128)} %param.8) | copy-start | bytes 1540
  1.3 3.8 %copy-start.4 = (f32[2048]{0:T(1024)S(1)}, f32[2048]{0:T(1024)}, u32[]{:S(2)}) copy-start(f32[2048]{0:T(1024)} %param.7) | copy-start | bytes 24580
  1.3 3.9 %copy-start.3 = (bf16[64,2048]{1,0:T(8,128)(2,1)S(1)}, bf16[64,2048]{1,0:T(8,128)(2,1)}, u32[]{:S(2)}) copy-start(bf16[64,2048]{1,0:T(8,128)(2,1)} %param.9) | copy-start | bytes 786436
  5.1 2.4 copy-start.2
  9.0 16.6 %copy-start.5 = (s32[2048]{0:T(1024)S(1)}, s32[2048]{0:T(1024)}, u32[]{:S(2)}) copy-start(s32[2048]{0:T(1024)} %param.5) | copy-start | bytes 24580
  9.0 46.7 %all-to-all-start = ((f32[128,16,66]{2,1,0:T(8,128)}), f32[128,16,66]{2,1,0:T(8,128)S(1)}, u32[]{:S(2)}, u32[]{:S(2)}) async-start(f32[128,16,66]{2,1,0:T(8,128)} %pad_maximum_fusion.3), calls=%async_computation | async-start | bytes 2097152 | tf_op jit(solution)/shard_map/all_to_all | solution.py:26
  126.7 34.7 %all-to-all-start.1 = ((f32[128,1,2048]{2,1,0:T(1,128)}), f32[128,1,2048]{2,1,0:T(1,128)S(1)}, u32[]{:S(2)}, u32[]{:S(2)}) async-start(f32[128,1,2048]{2,1,0:T(1,128)} %reshape.296), calls=%async_computation.1 | async-start | bytes 2097152 | tf_op jit(solution)/shard_map/all_to_all | solution.py:48
  161.5 1.0 copy-start.1
  220.6 33.4 %all-to-all-start.2 = ((f32[128,1,2048]{2,1,0:T(1,128)}), f32[128,1,2048]{2,1,0:T(1,128)}, u32[]{:S(2)}, u32[]{:S(2)}) async-start(f32[128,1,2048]{2,1,0:T(1,128)} %reshape.298), calls=%async_computation.2 | async-start | bytes 2097152 | tf_op jit(solution)/shard_map/all_to_all | solution.py:48
  299.1 9.1 %copy-start = (f32[4096,64]{1,0:T(8,128)S(1)}, f32[4096,64]{1,0:T(8,128)}, u32[]{:S(2)}) copy-start(f32[4096,64]{1,0:T(8,128)} %add_add_fusion) | copy-start | bytes 3145732
  300.6 22.5 %all-to-all-start.3 = ((f32[128,1,1024]{2,1,0:T(1,128)}), f32[128,1,1024]{2,1,0:T(1,128)}, u32[]{:S(2)}, u32[]{:S(2)}) async-start(f32[128,1,1024]{2,1,0:T(1,128)} %reshape.300), calls=%async_computation.3 | async-start | bytes 1048576 | tf_op jit(solution)/shard_map/all_to_all | solution.py:67
where the time goes:
time: 338 us; the launch traced here: 337 us
  other arithmetic  131 us (39%)
  waiting for transfers between devices  92.2 us (27%)
  local copies, waits for them, and re-layouts  65.2 us (19%)
  starting transfers between devices  37.5 us (11%)
  blocking collectives  9.66 us (3%)
    all_to_all x2, waiting for transfers between devices, apply(): there = lax.all_to_all(here, 'dom', split_axis=0, concat_axis=0, tiled=True)  54.3 us
    scatter-add x2, other arithmetic, apply(): return zero_rows.at[both].add(flows) + extra * field  46.6 us
    all_to_all x1, waiting for transfers between devices, local(): lax.all_to_all(payload, 'dom', split_axis=0, concat_axis=0, tiled=True)  30 us
    gather x2, local copies, waits for them, and re-layouts, apply(): here = field[both].reshape(peers, 2, cap, width)  29.7 us
    scatter-add x1, other arithmetic, local(): zero_rows.at[both]  23.8 us
    scatter-add x1, other arithmetic, local(): degree = jnp.zeros((VERT_DEV,), jnp.float32).at[both].add(w_both)  21.9 us
    all_to_all x1, starting transfers between devices, local(): lax.all_to_all(payload, 'dom', split_axis=0, concat_axis=0, tiled=True)  16.5 us
    unnamed x21, local copies, waits for them, and re-layouts  15.5 us
  transfers between devices with their start and end apart: 4, of which 4 were waited for; matrix products, arithmetic and copies ran while one was open for 2% of the time, Pallas kernels for 0%

commit v1 on v0

v1 whole, which is shorter than its diff:
```python
import functools

import jax
import jax.numpy as jnp
from jax import lax
from jax.experimental import pallas as pl
from jax.experimental.pallas import tpu as pltpu
from jax.sharding import PartitionSpec as P

SKETCH = 128
VERT_DEV = 4096
SWEEPS = 3
BLOCK = 16


ground_shift = 1.0
degree_boost = 0.25


def _pair_gather_kernel(a_ref, b_ref, x_ref, o_ref):
    lanes = x_ref.shape[2]
    low = lax.broadcasted_iota(jnp.int32, (1, lanes), 1) < lanes // 2

    def body(t, carry):
        base = t * BLOCK
        rows = [(x_ref[a_ref[base + r]], x_ref[b_ref[base + r]]) for r in range(BLOCK)]
        for r in range(BLOCK):
            o_ref[base + r] = jnp.where(low, rows[r][0], rows[r][1])
        return carry

    lax.fori_loop(0, o_ref.shape[0] // BLOCK, body, 0)


def pair_gather(a, b, x):
    return pl.pallas_call(
        _pair_gather_kernel,
        out_shape=jax.ShapeDtypeStruct((a.shape[0],) + x.shape[1:], x.dtype),
        in_specs=[
            pl.BlockSpec(memory_space=pltpu.SMEM),
            pl.BlockSpec(memory_space=pltpu.SMEM),
            pl.BlockSpec(memory_space=pltpu.VMEM),
        ],
        out_specs=pl.BlockSpec(memory_space=pltpu.VMEM),
    )(a, b, x)


def _sorted_scatter_kernel(half, key_ref, slot_ref, side_ref, v_ref, o_ref):
    lanes = o_ref.shape[2]
    o_ref[...] = jnp.zeros(o_ref.shape, o_ref.dtype)
    group = (lax.broadcasted_iota(jnp.int32, (1, lanes), 1) // half) % 2

    def body(t, carry):
        run, prev = carry
        base = t * BLOCK
        rows = [v_ref[slot_ref[base + r]] for r in range(BLOCK)]
        for r in range(BLOCK):
            i = base + r
            k = key_ref[i]
            mine = jnp.where(group == side_ref[i], rows[r], jnp.zeros_like(rows[r]))
            run = jnp.where(k == prev, run, jnp.zeros_like(run)) + mine
            o_ref[k] = run
            prev = k
        return run, prev

    lax.fori_loop(
        0,
        key_ref.shape[0] // BLOCK,
        body,
        (jnp.zeros((1, lanes), jnp.float32), jnp.int32(-1)),
    )


def sorted_scatter(half, key, slot, side, vals, rows):
    return pl.pallas_call(
        functools.partial(_sorted_scatter_kernel, half),
        out_shape=jax.ShapeDtypeStruct((rows,) + vals.shape[1:], vals.dtype),
        in_specs=[
            pl.BlockSpec(memory_space=pltpu.SMEM),
            pl.BlockSpec(memory_space=pltpu.SMEM),
            pl.BlockSpec(memory_space=pltpu.SMEM),
            pl.BlockSpec(memory_space=pltpu.VMEM),
        ],
        out_specs=pl.BlockSpec(memory_space=pltpu.VMEM),
    )(key, slot, side, vals)


def local(src_local, dst_local, edge_weight, send_counts, sketch):
    peers = lax.axis_size("dom")
    edges = src_local.shape[0]
    cap = edges // peers
    width = sketch.shape[0]

    def a2a(x):
        return lax.all_to_all(x, "dom", split_axis=0, concat_axis=0, tiled=True)

    live = (jnp.arange(cap)[None, :] < send_counts.reshape(peers, 1)).astype(jnp.float32)
    w_out = (edge_weight.reshape(peers, cap) * live).reshape(-1)
    root = jnp.sqrt(w_out)[:, None] * sketch.astype(jnp.float32).T
    payload = jnp.concatenate(
        [root, w_out[:, None], dst_local.astype(jnp.float32)[:, None]], axis=1
    )
    arrived = a2a(payload)
    arrived_root = arrived[:, :width]
    w_in = arrived[:, width]
    wanted = arrived[:, width + 1].astype(jnp.int32)

    keys = jnp.stack([src_local, wanted], axis=1).reshape(-1)
    key_s, entry_s = lax.sort(
        (keys, jnp.arange(2 * edges, dtype=jnp.int32)), num_keys=1
    )
    slot_s = entry_s // 2
    side_s = entry_s % 2

    def scatter(vals):
        return sorted_scatter(width, key_s, slot_s, side_s, vals, VERT_DEV)

    ones = jnp.ones((1, width), jnp.float32)
    first = jnp.concatenate(
        [root, -arrived_root, w_out[:, None] * ones, w_in[:, None] * ones], axis=1
    ).reshape(edges, 1, 4 * width)
    acc = scatter(first).reshape(VERT_DEV, 4 * width)
    rhs = acc[:, :width] + acc[:, width:2 * width]
    degree = acc[:, 2 * width] + acc[:, 3 * width]
    diag = ((1.0 + degree_boost) * degree + ground_shift)[:, None]
    extra = (degree_boost * degree + ground_shift)[:, None]

    def ends(field):
        doubled = jnp.concatenate([field, field], axis=1).reshape(VERT_DEV, 1, 2 * width)
        return pair_gather(src_local, wanted, doubled)

    def apply(field):
        here = ends(field)
        there = a2a(here).reshape(edges, 2 * width)
        here = here.reshape(edges, 2 * width)
        flow_out = w_out[:, None] * (here[:, :width] - there[:, width:])
        flow_in = w_in[:, None] * (there[:, :width] - here[:, width:])
        flows = jnp.concatenate([flow_out, -flow_in], axis=1).reshape(edges, 1, 2 * width)
        acc = scatter(flows).reshape(VERT_DEV, 2 * width)
        return (acc[:, :width] + acc[:, width:]) + extra * field

    sigma = 1.25
    delta = 0.8
    coeff = 1.0 / sigma
    resid = rhs
    direction = resid / diag
    solution = jnp.zeros((VERT_DEV, width), jnp.float32)
    for sweep in range(SWEEPS):
        solution = solution + direction
        if sweep < SWEEPS - 1:
            resid = resid - apply(direction)
            newer = 1.0 / (2.0 * sigma - coeff)
            direction = newer * coeff * direction + 2.0 * newer / delta * resid / diag
            coeff = newer
    here = ends(solution).reshape(edges, 2 * width)
    far = a2a(here[:, width:].reshape(edges // 2, 2 * width)).reshape(edges, width)
    diff = here[:, :width] - far
    partial_sum = jnp.sum(diff * diff, axis=1) * live.reshape(-1)
    resistance = lax.psum(partial_sum, "col") / SKETCH
    return (solution.T, resistance)


def solution(mesh):
    in_specs = (P("dom"), P("dom"), P("dom"), P("dom", None), P("col", "dom"))
    out_specs = (P("col", "dom"), P("dom"))
    return jax.shard_map(local, mesh=mesh, in_specs=in_specs, out_specs=out_specs, check_vma=False)
```

time: 338 us -> 289 us (0.86)
  other arithmetic: 131 us -> 42.4 us
  Pallas kernels: 0 us -> 75.3 us
  blocking collectives: 9.66 us -> 77.8 us
  waiting for transfers between devices: 92.2 us -> 43 us
  local copies, waits for them, and re-layouts: 65.2 us -> 24.2 us
  starting transfers between devices: 37.5 us -> 24.2 us
    scatter-add x4 -> x0, other arithmetic: 92.3 us -> none  [the longest x2 46.6 us: apply(): return zero_rows.at[both].add(flows) + extra * field]
    pallas_call x0 -> x6, Pallas kernels: none -> 75.3 us  [the longest x3 57.6 us: sorted_scatter(): pl.pallas_call(functools.partial(_sorted_scatter_kernel, half), out_shape...]
    all_to_all x0 -> x2, blocking collectives: none -> 68.1 us  [a2a(): return lax.all_to_all(x, 'dom', split_axis=0, concat_axis=0, tiled=True)]
    all_to_all x4 -> x2, waiting for transfers between devices: 92.2 us -> 43 us  [a2a(): return lax.all_to_all(x, 'dom', split_axis=0, concat_axis=0, tiled=True)]
    gather x4 -> x0, local copies, waits for them, and re-layouts: 42.2 us -> none  [the longest x2 29.7 us: apply(): here = field[both].reshape(peers, 2, cap, width)]
    all_to_all x4 -> x2, starting transfers between devices: 37.5 us -> 24.2 us  [a2a(): return lax.all_to_all(x, 'dom', split_axis=0, concat_axis=0, tiled=True)]
    mul x4 -> x2, other arithmetic: 14.7 us -> 2.48 us  [apply(): flow_out = w_out[:, None] * (here[:, :width] - there[:, width:])]
    all_to_all x3 -> x0, other arithmetic: 11.7 us -> none  [the longest x2 8.72 us: apply(): there = lax.all_to_all(here, 'dom', split_axis=0, concat_axis=0, tiled=True)]
  transfers between devices with their start and end apart: 4 -> 2, of which waited for: 4 -> 2; matrix products, arithmetic and copies ran while one was open for 2% -> 1% of each run, Pallas kernels for 0% -> 0%
where the time goes in v1:
time: 289 us; the launch traced here: 288 us
  blocking collectives  77.8 us (27%)
  Pallas kernels  75.3 us (26%)
  waiting for transfers between devices  43 us (15%)
  other arithmetic  42.4 us (15%)
  local copies, waits for them, and re-layouts  24.2 us (8%)
  starting transfers between devices  24.2 us (8%)
    all_to_all x2, blocking collectives, a2a(): return lax.all_to_all(x, 'dom', split_axis=0, concat_axis=0, tiled=True)  68.1 us
    pallas_call x3, Pallas kernels, sorted_scatter(): pl.pallas_call(functools.partial(_sorted_scatter_kernel, half), out_shape...  57.6 us
    all_to_all x2, waiting for transfers between devices, a2a(): return lax.all_to_all(x, 'dom', split_axis=0, concat_axis=0, tiled=True)  43 us
    all_to_all x2, starting transfers between devices, a2a(): return lax.all_to_all(x, 'dom', split_axis=0, concat_axis=0, tiled=True)  24.2 us
    pallas_call x3, Pallas kernels, pair_gather(): pl.pallas_call(_pair_gather_kernel, out_shape=jax.ShapeDtypeStruct((a.sha...  17.6 us
    reshape x1, local copies, waits for them, and re-layouts, local(): first = jnp.concatenate([root, -arrived_root, w_out[:, None] * ones, w_in...  10 us
    psum x1, blocking collectives, local(): resistance = lax.psum(partial_sum, 'col') / SKETCH  9.66 us
    unnamed x21, local copies, waits for them, and re-layouts  6.21 us
  transfers between devices with their start and end apart: 2, of which 2 were waited for; matrix products, arithmetic and copies ran while one was open for 1% of the time, Pallas kernels for 0%

profile of v1, /device:TPU:1, one launch (start us, length us, event | category | flops | bytes accessed | tf_op | source)
XLA Modules:
  0.0 287.7 jit_solution(7504708441622712293)
XLA Ops:
  0.6 0.7 convert_element_type.14
  1.3 0.7 iota_compare_fusion.1
  2.2 0.8 reshape.127
  3.0 0.7 fusion.21
  3.7 0.7 fusion.16
  4.4 2.0 copy.45
  6.4 0.8 copy.47
  7.2 0.9 concatenate.35
  8.1 1.4 fusion.19
  9.4 1.6 pad_maximum_fusion.3
  11.0 16.6 %all-to-all-start = ((f32[128,16,66]{2,1,0:T(8,128)}), f32[128,16,66]{2,1,0:T(8,128)S(1)}, u32[]{:S(2)}, u32[]{:S(2)}) async-start(f32[128,16,66]{2,1,0:T(8,128)} %pad_maximum_fusion.3), calls=%async_computation | async-start | bytes 2097152 | tf_op jit(solution)/shard_map/all_to_all | solution.py:94
  28.1 29.7 %all-to-all-done = f32[128,16,66]{2,1,0:T(8,128)S(1)} async-done(((f32[128,16,66]{2,1,0:T(8,128)}), f32[128,16,66]{2,1,0:T(8,128)S(1)}, u32[]{:S(2)}, u32[]{:S(2)}) %all-to-all-start) | async-done | bytes 540704 | tf_op jit(solution)/shard_map/all_to_all | solution.py:94
  57.8 1.2 fusion.20.b_ref
  59.0 1.0 slice_negate_fusion
  60.0 0.9 slice_reduce_fusion
  61.3 0.5 reshape.128
  61.8 5.8 %sort.15 = (s32[4096]{0:T(1024)}, s32[4096]{0:T(1024)S(1)}) sort(s32[4096]{0:T(1024)S(1)} %reshape.128, s32[4096]{0:T(1024)S(1)} %iota.10), dimensions={0}, to_apply=%region_0.0 | sort | flops 49152 | bytes 65536 | tf_op jit(solution)/shard_map/sort | solution.py:108
  67.5 0.6 add_select_fusion
  68.8 0.9 maximum_bitcast_fusion
  69.7 10.0 %copy.50.v_ref = f32[2048,1,256]{2,1,0:T(1,128)} copy(f32[2048,1,256]{2,0,1:T(8,128)S(1)} %maximum_bitcast_fusion) | data formatting | bytes 4194304 | tf_op jit(solution)/shard_map/reshape | solution.py:120
  79.7 20.9 %shard_map.68 = f32[4096,1,256]{2,1,0:T(1,128)} custom-call(s32[4096]{0:T(1024)} %get-tuple-element.4.key_ref, s32[4096]{0:T(1024)} %get-tuple-element.29.slot_ref, s32[4096]{0:T(1024)} %get-tuple-element.28.side_ref, f32[2048,1,256]{2,1,0:T(1,128)} %copy.50.v_ref), custom_call_target="tpu_custom_call" | custom-call | tf_op jit(solution)/shard_map/pallas_call | solution.py:74
  100.6 2.5 copy.57
  103.1 1.7 add_reduce_fusion
  105.0 1.2 broadcast_divide_fusion
  106.3 1.9 pad_maximum_fusion
  108.2 6.0 %shard_map.69 = f32[2048,1,128]{2,1,0:T(1,128)} custom-call(s32[2048]{0:T(1024)} %a_ref.5, s32[2048]{0:T(1024)} %fusion.20.b_ref, f32[4096,1,128]{2,1,0:T(1,128)} %bitcast.48), custom_call_target="tpu_custom_call" | custom-call | tf_op jit(solution)/shard_map/pallas_call | solution.py:35
  114.2 35.0 %all_to_all.28 = f32[2048,1,128]{2,1,0:T(1,128)S(1)} all-to-all(f32[2048,1,128]{2,1,0:T(1,128)} %shard_map.69), channel_id=1, replica_groups=mesh['dom'=128,'col'=2] {'dom'}, dimensions={0} | all-to-all | bytes 2097152 | tf_op jit(solution)/shard_map/all_to_all | solution.py:94
  149.3 1.2 fusion.15
  150.5 1.3 pad_maximum_fusion.4
  151.8 18.3 %shard_map.70 = f32[4096,1,128]{2,1,0:T(1,128)} custom-call(s32[4096]{0:T(1024)} %get-tuple-element.4.key_ref, s32[4096]{0:T(1024)} %get-tuple-element.29.slot_ref, s32[4096]{0:T(1024)} %get-tuple-element.28.side_ref, f32[2048,1,128]{2,1,0:T(1,128)} %bitcast.52), custom_call_target="tpu_custom_call" | custom-call | tf_op jit(solution)/shard_map/pallas_call | solution.py:74
  170.1 5.3 %divide_add_fusion = f32[4096,64]{1,0:T(8,128)S(1)} fusion(f32[4096]{0:T(1024)S(1)} %get-tuple-element.17, f32[4096]{0:T(1024)S(1)} %get-tuple-element.16, f32[4096,128]{1,0:T(8,128)} %bitcast.35, f32[4096,256]{1,0:T(8,128)} %bitcast.33), kind=kLoop, calls=%fused_computation.17 | loop fusion | flops 2621440 | bytes 5275648 | tf_op jit(solution)/shard_map/add | solution.py:152
  175.5 2.0 pad_maximum_fusion.1
  177.4 5.8 %shard_map.71 = f32[2048,1,128]{2,1,0:T(1,128)} custom-call(s32[2048]{0:T(1024)} %a_ref.5, s32[2048]{0:T(1024)} %fusion.20.b_ref, f32[4096,1,128]{2,1,0:T(1,128)} %bitcast.49), custom_call_target="tpu_custom_call" | custom-call | tf_op jit(solution)/shard_map/pallas_call | solution.py:35
  183.2 33.1 %all_to_all.29 = f32[2048,1,128]{2,1,0:T(1,128)S(1)} all-to-all(f32[2048,1,128]{2,1,0:T(1,128)} %shard_map.71), channel_id=1, replica_groups=mesh['dom'=128,'col'=2] {'dom'}, dimensions={0} | all-to-all | bytes 2097152 | tf_op jit(solution)/shard_map/all_to_all | solution.py:94
  216.3 1.2 fusion.12
  217.5 1.3 pad_maximum_fusion.5
  218.9 18.4 %shard_map.72 = f32[4096,1,128]{2,1,0:T(1,128)} custom-call(s32[4096]{0:T(1024)} %get-tuple-element.4.key_ref, s32[4096]{0:T(1024)} %get-tuple-element.29.slot_ref, s32[4096]{0:T(1024)} %get-tuple-element.28.side_ref, f32[2048,1,128]{2,1,0:T(1,128)} %bitcast.51), custom_call_target="tpu_custom_call" | custom-call | tf_op jit(solution)/shard_map/pallas_call | solution.py:74
  237.3 5.6 %fusion.5 = f32[4096,64]{1,0:T(8,128)S(1)} fusion(f32[4096,128]{1,0:T(8,128)} %bitcast.40, f32[4096]{0:T(1024)S(1)} %get-tuple-element.16, f32[4096]{0:T(1024)S(1)} %get-tuple-element.17, f32[4096,128]{1,0:T(8,128)S(1)} %bitcast.36, f32[4096,256]{1,0:T(8,128)} %bitcast.34), kind=kLoop, calls=%fused_computation.7 | loop fusion | flops 5242880 | bytes 7372800 | tf_op jit(solution)/shard_map/add | solution.py:148
  242.9 1.9 pad_maximum_fusion.2
  244.8 5.8 %shard_map.73 = f32[2048,1,128]{2,1,0:T(1,128)} custom-call(s32[2048]{0:T(1024)} %a_ref.5, s32[2048]{0:T(1024)} %fusion.20.b_ref, f32[4096,1,128]{2,1,0:T(1,128)} %bitcast.50), custom_call_target="tpu_custom_call" | custom-call | tf_op jit(solution)/shard_map/pallas_call | solution.py:35
  250.6 1.7 slice.104
  252.3 1.0 all_to_all.22
  253.4 7.6 %all-to-all-start.3 = ((f32[128,8,128]{2,1,0:T(8,128)}), f32[128,8,128]{2,1,0:T(8,128)}, u32[]{:S(2)}, u32[]{:S(2)}) async-start(f32[128,8,128]{2,1,0:T(8,128)} %all_to_all.22), calls=%async_computation.3 | async-start | bytes 1048576 | tf_op jit(solution)/shard_map/all_to_all | solution.py:94
  261.0 1.6 copy.54
  262.5 13.3 %all-to-all-done.3 = f32[128,8,128]{2,1,0:T(8,128)} async-done(((f32[128,8,128]{2,1,0:T(8,128)}), f32[128,8,128]{2,1,0:T(8,128)}, u32[]{:S(2)}, u32[]{:S(2)}) %all-to-all-start.3) | async-done | bytes 524320 | tf_op jit(solution)/shard_map/all_to_all | solution.py:94
  275.8 1.2 reshape.143
  277.5 9.7 %psum.7 = f32[2048]{0:T(1024)S(1)} all-reduce(f32[2048]{0:T(1024)S(1)} %broadcast_select_fusion), channel_id=1, replica_groups=mesh['dom'=128,'col'=2] {'col'}, use_global_device_ids=true, to_apply=%region_2.3 | all-reduce | flops 2048 | bytes 16384 | tf_op jit(solution)/shard_map/psum | solution.py:158
  287.1 0.6 broadcast_multiply_fusion
  (26 shorter events, 2.0 us)
Async XLA Ops:
  11.0 16.7 %copy-start.8 = (s32[2048]{0:T(1024)S(1)}, s32[2048]{0:T(1024)}, u32[]{:S(2)}) copy-start(s32[2048]{0:T(1024)} %a_ref.5) | copy-start | bytes 24580
  11.0 46.7 %all-to-all-start = ((f32[128,16,66]{2,1,0:T(8,128)}), f32[128,16,66]{2,1,0:T(8,128)S(1)}, u32[]{:S(2)}, u32[]{:S(2)}) async-start(f32[128,16,66]{2,1,0:T(8,128)} %pad_maximum_fusion.3), calls=%async_computation | async-start | bytes 2097152 | tf_op jit(solution)/shard_map/all_to_all | solution.py:94
  61.3 7.6 %copy-start.7 = (f32[2048,64]{1,0:T(8,128)S(1)}, f32[2048,64]{1,0:T(8,128)}, u32[]{:S(2)}) copy-start(f32[2048,64]{1,0:T(8,128)} %slice_negate_fusion) | copy-start | bytes 1572868
  103.1 1.9 copy-start
  114.2 35.1 %copy-start.5 = (f32[2048,1,128]{2,1,0:T(1,128)S(1)}, f32[2048,1,128]{2,1,0:T(1,128)}, u32[]{:S(2)}) copy-start(f32[2048,1,128]{2,1,0:T(1,128)} %shard_map.69) | copy-start | bytes 3145732
  183.2 33.1 %copy-start.4 = (f32[2048,1,128]{2,1,0:T(1,128)S(1)}, f32[2048,1,128]{2,1,0:T(1,128)}, u32[]{:S(2)}) copy-start(f32[2048,1,128]{2,1,0:T(1,128)} %shard_map.71) | copy-start | bytes 3145732
  218.9 18.4 %copy-start.1 = (f32[4096,1,128]{2,1,0:T(1,128)S(1)}, f32[4096,1,128]{2,1,0:T(1,128)}, u32[]{:S(2)}) copy-start(f32[4096,1,128]{2,1,0:T(1,128)} %shard_map.70) | copy-start | bytes 6291460
  242.9 1.9 copy-start.2
  250.6 10.3 %copy-start.3 = (f32[4096,64]{1,0:T(8,128)S(1)}, f32[4096,64]{1,0:T(8,128)}, u32[]{:S(2)}) copy-start(f32[4096,64]{1,0:T(8,128)} %copy-done.2) | copy-start | bytes 3145732
  253.4 22.5 %all-to-all-start.3 = ((f32[128,8,128]{2,1,0:T(8,128)}), f32[128,8,128]{2,1,0:T(8,128)}, u32[]{:S(2)}, u32[]{:S(2)}) async-start(f32[128,8,128]{2,1,0:T(8,128)} %all_to_all.22), calls=%async_computation.3 | async-start | bytes 1048576 | tf_op jit(solution)/shard_map/all_to_all | solution.py:94
  260.9 16.2 %copy-start.6 = (f32[2048,1,128]{2,1,0:T(1,128)S(1)}, f32[2048,1,128]{2,1,0:T(1,128)}, u32[]{:S(2)}) copy-start(f32[2048,1,128]{2,1,0:T(1,128)} %shard_map.73) | copy-start | bytes 3145732

commit v2 on v1

--- a/solution.py
+++ b/solution.py
@@ -11,6 +11,7 @@
 VERT_DEV = 4096
 SWEEPS = 3
 BLOCK = 16
+RUN_BLOCK = 4
 
 
 ground_shift = 1.0
@@ -44,44 +45,59 @@
     )(a, b, x)
 
 
-def _sorted_scatter_kernel(half, key_ref, slot_ref, side_ref, v_ref, o_ref):
-    lanes = o_ref.shape[2]
-    o_ref[...] = jnp.zeros(o_ref.shape, o_ref.dtype)
-    group = (lax.broadcasted_iota(jnp.int32, (1, lanes), 1) // half) % 2
+def _sorted_scatter_kernel(key_ref, slot_ref, v0_ref, v1_ref, s0_ref, s1_ref, t0_ref, t1_ref):
+    lanes = s0_ref.shape[2]
+    rows = s0_ref.shape[0]
+    n = key_ref.shape[0] // 4
+    outs = (s0_ref, t0_ref, s1_ref, t1_ref)
+    vals = (v0_ref, v0_ref, v1_ref, v1_ref)
+    step = 64
+
+    @pl.loop(0, rows // step)
+    def _(i):
+        at = pl.ds(pl.multiple_of(i * step, step), step)
+        for o in outs:
+            o[at] = jnp.zeros((step,) + o.shape[1:], o.dtype)
 
     def body(t, carry):
-        run, prev = carry
-        base = t * BLOCK
-        rows = [v_ref[slot_ref[base + r]] for r in range(BLOCK)]
-        for r in range(BLOCK):
-            i = base + r
-            k = key_ref[i]
-            mine = jnp.where(group == side_ref[i], rows[r], jnp.zeros_like(rows[r]))
-            run = jnp.where(k == prev, run, jnp.zeros_like(run)) + mine
-            o_ref[k] = run
-            prev = k
-        return run, prev
+        runs, prevs = carry
+        runs, prevs = list(runs), list(prevs)
+        base = t * RUN_BLOCK
+        got = [
+            [vals[c][slot_ref[c * n + base + r]] for c in range(4)] for r in range(RUN_BLOCK)
+        ]
+        for r in range(RUN_BLOCK):
+            for c in range(4):
+                k = key_ref[c * n + base + r]
+                runs[c] = jnp.where(k == prevs[c], runs[c], jnp.zeros_like(runs[c])) + got[r][c]
+                outs[c][k] = runs[c]
+                prevs[c] = k
+        return tuple(runs), tuple(prevs)
 
-    lax.fori_loop(
-        0,
-        key_ref.shape[0] // BLOCK,
-        body,
-        (jnp.zeros((1, lanes), jnp.float32), jnp.int32(-1)),
-    )
+    zero = jnp.zeros((1, lanes), jnp.float32)
+    lax.fori_loop(0, n // RUN_BLOCK, body, ((zero,) * 4, (jnp.int32(-1),) * 4))
+
+    @pl.loop(0, rows // step)
+    def _(i):
+        at = pl.ds(pl.multiple_of(i * step, step), step)
+        s0_ref[at] += t0_ref[at]
+        s1_ref[at] += t1_ref[at]
 
 
-def sorted_scatter(half, key, slot, side, vals, rows):
+def sorted_scatter(key, slot, v0, v1, rows):
+    shape = jax.ShapeDtypeStruct((rows,) + v0.shape[1:], v0.dtype)
     return pl.pallas_call(
-        functools.partial(_sorted_scatter_kernel, half),
-        out_shape=jax.ShapeDtypeStruct((rows,) + vals.shape[1:], vals.dtype),
+        _sorted_scatter_kernel,
+        out_shape=(shape, shape),
         in_specs=[
             pl.BlockSpec(memory_space=pltpu.SMEM),
             pl.BlockSpec(memory_space=pltpu.SMEM),
-            pl.BlockSpec(memory_space=pltpu.SMEM),
+            pl.BlockSpec(memory_space=pltpu.VMEM),
             pl.BlockSpec(memory_space=pltpu.VMEM),
         ],
-        out_specs=pl.BlockSpec(memory_space=pltpu.VMEM),
-    )(key, slot, side, vals)
+        out_specs=(pl.BlockSpec(memory_space=pltpu.VMEM), pl.BlockSpec(memory_space=pltpu.VMEM)),
+        scratch_shapes=[pltpu.VMEM((rows,) + v0.shape[1:], v0.dtype)] * 2,
+    )(key, slot, v0, v1)
 
 
 def local(src_local, dst_local, edge_weight, send_counts, sketch):
@@ -96,31 +112,39 @@
     live = (jnp.arange(cap)[None, :] < send_counts.reshape(peers, 1)).astype(jnp.float32)
     w_out = (edge_weight.reshape(peers, cap) * live).reshape(-1)
     root = jnp.sqrt(w_out)[:, None] * sketch.astype(jnp.float32).T
-    payload = jnp.concatenate(
-        [root, w_out[:, None], dst_local.astype(jnp.float32)[:, None]], axis=1
+    lanes = 2 * width
+    side_row = jnp.concatenate(
+        [
+            w_out.reshape(peers, 1, cap),
+            dst_local.astype(jnp.float32).reshape(peers, 1, cap),
+            jnp.zeros((peers, 1, lanes - 2 * cap), jnp.float32),
+        ],
+        axis=2,
     )
+    payload = jnp.concatenate([root.reshape(peers, -1, lanes), side_row], axis=1)
     arrived = a2a(payload)
-    arrived_root = arrived[:, :width]
-    w_in = arrived[:, width]
-    wanted = arrived[:, width + 1].astype(jnp.int32)
+    arrived_root = arrived[:, :-1].reshape(edges, width)
+    w_in = arrived[:, -1, :cap].reshape(-1)
+    wanted = arrived[:, -1, cap:2 * cap].reshape(-1).astype(jnp.int32)
 
-    keys = jnp.stack([src_local, wanted], axis=1).reshape(-1)
+    keys = jnp.concatenate([src_local, wanted + VERT_DEV])
     key_s, entry_s = lax.sort(
         (keys, jnp.arange(2 * edges, dtype=jnp.int32)), num_keys=1
     )
-    slot_s = entry_s // 2
-    side_s = entry_s % 2
+    key_s = key_s % VERT_DEV
+    slot_s = entry_s % edges
 
-    def scatter(vals):
-        return sorted_scatter(width, key_s, slot_s, side_s, vals, VERT_DEV)
+    def scatter(v0, v1):
+        s0, s1 = sorted_scatter(key_s, slot_s, v0, v1, VERT_DEV)
+        return s0.reshape(VERT_DEV, lanes), s1.reshape(VERT_DEV, lanes)
 
     ones = jnp.ones((1, width), jnp.float32)
-    first = jnp.concatenate(
-        [root, -arrived_root, w_out[:, None] * ones, w_in[:, None] * ones], axis=1
-    ).reshape(edges, 1, 4 * width)
-    acc = scatter(first).reshape(VERT_DEV, 4 * width)
-    rhs = acc[:, :width] + acc[:, width:2 * width]
-    degree = acc[:, 2 * width] + acc[:, 3 * width]
+    s0, s1 = scatter(
+        jnp.concatenate([root, w_out[:, None] * ones], axis=1).reshape(edges, 1, lanes),
+        jnp.concatenate([-arrived_root, w_in[:, None] * ones], axis=1).reshape(edges, 1, lanes),
+    )
+    rhs = s0[:, :width] + s1[:, :width]
+    degree = s0[:, width] + s1[:, width]
     diag = ((1.0 + degree_boost) * degree + ground_shift)[:, None]
     extra = (degree_boost * degree + ground_shift)[:, None]
 
@@ -134,9 +158,9 @@
         here = here.reshape(edges, 2 * width)
         flow_out = w_out[:, None] * (here[:, :width] - there[:, width:])
         flow_in = w_in[:, None] * (there[:, :width] - here[:, width:])
-        flows = jnp.concatenate([flow_out, -flow_in], axis=1).reshape(edges, 1, 2 * width)
-        acc = scatter(flows).reshape(VERT_DEV, 2 * width)
-        return (acc[:, :width] + acc[:, width:]) + extra * field
+        flows = jnp.concatenate([flow_out, -flow_in], axis=1).reshape(edges, 1, lanes)
+        s0, s1 = scatter(flows, flows)
+        return (s0[:, :width] + s1[:, width:]) + extra * field
 
     sigma = 1.25
     delta = 0.8

time: 289 us -> 281 us (0.972)
  local copies, waits for them, and re-layouts: 24.2 us -> 9.21 us
  Pallas kernels: 75.3 us -> 84.9 us
    reshape x2, local copies, waits for them, and re-layouts: 10.5 us -> 0.28 us  [the longest x1 0.2 us: local(): root.reshape(peers, -1, lanes)]
    pallas_call x3, Pallas kernels: 57.6 us -> 67.5 us  [sorted_scatter(): pl.pallas_call(_sorted_scatter_kernel, out_shape=(shape, shape), in_specs...]
    unnamed x21 -> x22, local copies, waits for them, and re-layouts: 6.21 us -> 2.82 us
    add x1, other arithmetic: 1.71 us -> 4.62 us  [local(): extra = (degree_boost * degree + ground_shift)[:, None]]
    concatenate x3 -> x6, other arithmetic: 4.22 us -> 6.45 us  [the longest x2 2.62 us: apply(): jnp.concatenate([flow_out, -flow_in], axis=1).reshape(edges, 1, lanes)]
where the time goes in v2:
time: 281 us; the launch traced here: 280 us
  Pallas kernels  84.9 us (30%)
  blocking collectives  77.9 us (28%)
  waiting for transfers between devices  41.9 us (15%)
  other arithmetic  41.8 us (15%)
  starting transfers between devices  23.6 us (8%)
  local copies, waits for them, and re-layouts  9.21 us (3%)
    all_to_all x2, blocking collectives, a2a(): return lax.all_to_all(x, 'dom', split_axis=0, concat_axis=0, tiled=True)  68.3 us
    pallas_call x3, Pallas kernels, sorted_scatter(): pl.pallas_call(_sorted_scatter_kernel, out_shape=(shape, shape), in_specs...  67.5 us
    all_to_all x2, waiting for transfers between devices, a2a(): return lax.all_to_all(x, 'dom', split_axis=0, concat_axis=0, tiled=True)  41.9 us
    all_to_all x2, starting transfers between devices, a2a(): return lax.all_to_all(x, 'dom', split_axis=0, concat_axis=0, tiled=True)  23.6 us
    pallas_call x3, Pallas kernels, pair_gather(): pl.pallas_call(_pair_gather_kernel, out_shape=jax.ShapeDtypeStruct((a.sha...  17.4 us
    psum x1, blocking collectives, local(): resistance = lax.psum(partial_sum, 'col') / SKETCH  9.66 us
    add x1, other arithmetic, local(): solution = solution + direction  6.17 us
    concatenate x3, other arithmetic, ends(): jnp.concatenate([field, field], axis=1).reshape(VERT_DEV, 1, 2 * width)  5.94 us
  transfers between devices with their start and end apart: 2, of which 2 were waited for; matrix products, arithmetic and copies ran while one was open for 1% of the time, Pallas kernels for 0%

profile of v2, /device:TPU:1, one launch (start us, length us, event | category | flops | bytes accessed | tf_op | source)
XLA Modules:
  0.0 280.3 jit_solution(1223556178108434934)
XLA Ops:
  0.6 0.7 convert_element_type.14
  1.3 0.7 iota_compare_fusion
  2.2 0.8 reshape.149
  3.0 0.7 fusion.19
  3.7 0.9 compare_select_fusion
  4.6 1.2 copy.39
  5.8 0.3 multiply_bitcast_fusion
  6.2 0.2 reshape.148
  6.5 1.2 maximum_maximum_fusion
  7.7 16.3 %all-to-all-start = ((f32[128,9,128]{2,1,0:T(8,128)}), f32[128,9,128]{2,1,0:T(8,128)S(1)}, u32[]{:S(2)}, u32[]{:S(2)}) async-start(f32[128,9,128]{2,1,0:T(8,128)} %maximum_maximum_fusion), calls=%async_computation | async-start | bytes 2097152 | tf_op jit(solution)/shard_map/all_to_all | solution.py:110
  24.0 0.3 mul.117
  24.3 1.3 pad_maximum_fusion.3
  25.7 28.6 %all-to-all-done = f32[128,9,128]{2,1,0:T(8,128)S(1)} async-done(((f32[128,9,128]{2,1,0:T(8,128)}), f32[128,9,128]{2,1,0:T(8,128)S(1)}, u32[]{:S(2)}, u32[]{:S(2)}) %all-to-all-start) | async-done | bytes 589856 | tf_op jit(solution)/shard_map/all_to_all | solution.py:110
  54.3 0.2 slice_reduce_fusion
  54.5 0.3 fusion.16
  54.9 0.2 neg.13
  55.2 5.2 %sort.15 = (s32[4096]{0:T(1024)S(1)}, s32[4096]{0:T(1024)S(1)}) sort(s32[4096]{0:T(1024)S(1)} %pad_add_fusion, s32[4096]{0:T(1024)S(1)} %iota.12), dimensions={0}, to_apply=%region_0.0 | sort | flops 49152 | bytes 65536 | tf_op jit(solution)/shard_map/sort | solution.py:131
  60.3 0.6 add_select_fusion
  60.9 0.3 mul.119
  61.3 1.3 pad_maximum_fusion.4
  62.6 22.5 %shard_map.68 = (f32[4096,1,128]{2,1,0:T(1,128)}, f32[4096,1,128]{2,1,0:T(1,128)}) custom-call(s32[4096]{0:T(1024)} %get-tuple-element.35.key_ref, s32[4096]{0:T(1024)} %get-tuple-element.34.slot_ref, f32[2048,1,128]{2,1,0:T(1,128)} %bitcast.60, f32[2048,1,128]{2,1,0:T(1,128)} %bitcast.61), custom_call_target="tpu_custom_call" | custom-call | tf_op jit(solution)/shard_map/pallas_call | solution.py:89
  85.1 4.6 %add_reduce_fusion = (f32[4096]{0:T(1024)S(1)}, f32[4096]{0:T(1024)S(1)}) fusion(f32[4096,128]{1,0:T(8,128)} %bitcast.38, f32[4096,128]{1,0:T(8,128)} %bitcast.34), kind=kLoop, calls=%fused_computation.16 | loop fusion | flops 20480 | bytes 65536 | tf_op jit(solution)/shard_map/add | solution.py:149
  89.7 0.7 broadcast_divide_fusion
  90.5 2.0 pad_maximum_fusion
  92.5 5.8 %shard_map.69 = f32[2048,1,128]{2,1,0:T(1,128)} custom-call(s32[2048]{0:T(1024)} %a_ref.5, s32[2048]{0:T(1024)} %copy-done.8, f32[4096,1,128]{2,1,0:T(1,128)} %bitcast.55), custom_call_target="tpu_custom_call" | custom-call | tf_op jit(solution)/shard_map/pallas_call | solution.py:36
  98.3 35.2 %all_to_all.24 = f32[2048,1,128]{2,1,0:T(1,128)S(1)} all-to-all(f32[2048,1,128]{2,1,0:T(1,128)} %shard_map.69), channel_id=1, replica_groups=mesh['dom'=128,'col'=2] {'dom'}, dimensions={0} | all-to-all | bytes 2097152 | tf_op jit(solution)/shard_map/all_to_all | solution.py:110
  133.5 1.2 fusion.15
  134.8 1.3 pad_maximum_fusion.5
  136.1 22.5 %shard_map.70 = (f32[4096,1,128]{2,1,0:T(1,128)}, f32[4096,1,128]{2,1,0:T(1,128)}) custom-call(s32[4096]{0:T(1024)} %get-tuple-element.35.key_ref, s32[4096]{0:T(1024)} %get-tuple-element.34.slot_ref, f32[2048,1,128]{2,1,0:T(1,128)} %bitcast.51, f32[2048,1,128]{2,1,0:T(1,128)} %bitcast.52), custom_call_target="tpu_custom_call" | custom-call | tf_op jit(solution)/shard_map/pallas_call | solution.py:89
  158.6 5.0 %divide_add_fusion = f32[4096,64]{1,0:T(8,128)S(1)} fusion(f32[4096,64]{1,0:T(8,128)} %copy-done.2, f32[4096]{0:T(1024)S(1)} %get-tuple-element.27, f32[4096]{0:T(1024)S(1)} %get-tuple-element.26, f32[4096,128]{1,0:T(8,128)} %bitcast.58, f32[4096,128]{1,0:T(8,128)} %bitcast.56, f32[4096,128]{1,0:T(8,128)} %bitcast.39, f32[4096,128]{1,0:T(8,128)S(1)} %bitcast.36), kind=kLoop, calls=%fused_computation.15 | loop fusion | flops 2359296 | bytes 6324224 | tf_op jit(solution)/shard_map/add | solution.py:176
  163.6 2.0 pad_maximum_fusion.1
  165.6 5.8 %shard_map.71 = f32[2048,1,128]{2,1,0:T(1,128)} custom-call(s32[2048]{0:T(1024)} %a_ref.5, s32[2048]{0:T(1024)} %copy-done.8, f32[4096,1,128]{2,1,0:T(1,128)} %bitcast.53), custom_call_target="tpu_custom_call" | custom-call | tf_op jit(solution)/shard_map/pallas_call | solution.py:36
  171.4 33.1 %all_to_all.25 = f32[2048,1,128]{2,1,0:T(1,128)S(1)} all-to-all(f32[2048,1,128]{2,1,0:T(1,128)} %shard_map.71), channel_id=1, replica_groups=mesh['dom'=128,'col'=2] {'dom'}, dimensions={0} | all-to-all | bytes 2097152 | tf_op jit(solution)/shard_map/all_to_all | solution.py:110
  204.5 1.2 fusion.12
  205.7 1.3 pad_maximum_fusion.6
  207.1 22.5 %shard_map.72 = (f32[4096,1,128]{2,1,0:T(1,128)}, f32[4096,1,128]{2,1,0:T(1,128)}) custom-call(s32[4096]{0:T(1024)} %get-tuple-element.35.key_ref, s32[4096]{0:T(1024)} %get-tuple-element.34.slot_ref, f32[2048,1,128]{2,1,0:T(1,128)} %bitcast.49, f32[2048,1,128]{2,1,0:T(1,128)} %bitcast.50), custom_call_target="tpu_custom_call" | custom-call | tf_op jit(solution)/shard_map/pallas_call | solution.py:89
  229.5 6.2 %fusion.5 = f32[4096,64]{1,0:T(8,128)S(1)} fusion(f32[4096,128]{1,0:T(8,128)} %bitcast.63, f32[4096,128]{1,0:T(8,128)} %bitcast.62, f32[4096,64]{1,0:T(8,128)} %copy-done.2, f32[4096]{0:T(1024)S(1)} %get-tuple-element.26, f32[4096]{0:T(1024)S(1)} %get-tuple-element.27, f32[4096,128]{1,0:T(8,128)} %bitcast.59, f32[4096,128]{1,0:T(8,128)} %bitcast.57, ...), kind=kLoop, calls=%fused_computation.6 | loop fusion | flops 4980736 | bytes 8421376 | tf_op jit(solution)/shard_map/add | solution.py:172
  235.7 1.9 pad_maximum_fusion.2
  237.6 5.8 %shard_map.73 = f32[2048,1,128]{2,1,0:T(1,128)} custom-call(s32[2048]{0:T(1024)} %a_ref.5, s32[2048]{0:T(1024)} %copy-done.8, f32[4096,1,128]{2,1,0:T(1,128)} %bitcast.54), custom_call_target="tpu_custom_call" | custom-call | tf_op jit(solution)/shard_map/pallas_call | solution.py:36
  243.5 1.7 slice.104
  245.2 1.0 all_to_all.18
  246.2 7.3 %all-to-all-start.3 = ((f32[128,8,128]{2,1,0:T(8,128)}), f32[128,8,128]{2,1,0:T(8,128)}, u32[]{:S(2)}, u32[]{:S(2)}) async-start(f32[128,8,128]{2,1,0:T(8,128)} %all_to_all.18), calls=%async_computation.3 | async-start | bytes 1048576 | tf_op jit(solution)/shard_map/all_to_all | solution.py:110
  253.5 1.6 copy.49
  255.1 13.3 %all-to-all-done.3 = f32[128,8,128]{2,1,0:T(8,128)} async-done(((f32[128,8,128]{2,1,0:T(8,128)}), f32[128,8,128]{2,1,0:T(8,128)}, u32[]{:S(2)}, u32[]{:S(2)}) %all-to-all-start.3) | async-done | bytes 524320 | tf_op jit(solution)/shard_map/all_to_all | solution.py:110
  268.4 1.2 reshape.169
  269.7 0.3 fusion.9
  270.0 9.7 %psum.7 = f32[2048]{0:T(1024)S(1)} all-reduce(f32[2048]{0:T(1024)S(1)} %broadcast_select_fusion), channel_id=1, replica_groups=mesh['dom'=128,'col'=2] {'col'}, use_global_device_ids=true, to_apply=%region_2.3 | all-reduce | flops 2048 | bytes 16384 | tf_op jit(solution)/shard_map/psum | solution.py:182
  279.7 0.6 broadcast_multiply_fusion
  (31 shorter events, 0.5 us)
Async XLA Ops:
  7.7 46.6 %all-to-all-start = ((f32[128,9,128]{2,1,0:T(8,128)}), f32[128,9,128]{2,1,0:T(8,128)S(1)}, u32[]{:S(2)}, u32[]{:S(2)}) async-start(f32[128,9,128]{2,1,0:T(8,128)} %maximum_maximum_fusion), calls=%async_computation | async-start | bytes 2097152 | tf_op jit(solution)/shard_map/all_to_all | solution.py:110
  25.7 29.5 %copy-start.9 = (s32[2048]{0:T(1024)S(1)}, s32[2048]{0:T(1024)}, u32[]{:S(2)}) copy-start(s32[2048]{0:T(1024)} %a_ref.5) | copy-start | bytes 24580
  54.9 7.7 %copy-start.8 = (s32[2048]{0:T(1024)}, s32[2048]{0:T(1024)S(1)}, u32[]{:S(2)}) copy-start(s32[2048]{0:T(1024)S(1)} %convert_element_type.16.b_ref) | copy-start | bytes 24580
  85.1 4.6 %copy-start = (f32[4096,1,128]{2,1,0:T(1,128)S(1)}, f32[4096,1,128]{2,1,0:T(1,128)}, u32[]{:S(2)}) copy-start(f32[4096,1,128]{2,1,0:T(1,128)} %get-tuple-element.12) | copy-start | bytes 6291460
  85.1 4.6 %copy-start.1 = (f32[4096,1,128]{2,1,0:T(1,128)S(1)}, f32[4096,1,128]{2,1,0:T(1,128)}, u32[]{:S(2)}) copy-start(f32[4096,1,128]{2,1,0:T(1,128)} %get-tuple-element.13) | copy-start | bytes 6291460
  90.5 2.0 copy-start.2
  98.3 35.2 %copy-start.6 = (f32[2048,1,128]{2,1,0:T(1,128)S(1)}, f32[2048,1,128]{2,1,0:T(1,128)}, u32[]{:S(2)}) copy-start(f32[2048,1,128]{2,1,0:T(1,128)} %shard_map.69) | copy-start | bytes 3145732
  171.4 33.1 %copy-start.5 = (f32[2048,1,128]{2,1,0:T(1,128)S(1)}, f32[2048,1,128]{2,1,0:T(1,128)}, u32[]{:S(2)}) copy-start(f32[2048,1,128]{2,1,0:T(1,128)} %shard_map.71) | copy-start | bytes 3145732
  235.7 1.9 copy-start.3
  243.5 10.0 %copy-start.4 = (f32[4096,64]{1,0:T(8,128)S(1)}, f32[4096,64]{1,0:T(8,128)}, u32[]{:S(2)}) copy-start(f32[4096,64]{1,0:T(8,128)} %copy-done.3) | copy-start | bytes 3145732
  246.2 22.2 %all-to-all-start.3 = ((f32[128,8,128]{2,1,0:T(8,128)}), f32[128,8,128]{2,1,0:T(8,128)}, u32[]{:S(2)}, u32[]{:S(2)}) async-start(f32[128,8,128]{2,1,0:T(8,128)} %all_to_all.18), calls=%async_computation.3 | async-start | bytes 1048576 | tf_op jit(solution)/shard_map/all_to_all | solution.py:110
  253.5 16.2 %copy-start.7 = (f32[2048,1,128]{2,1,0:T(1,128)S(1)}, f32[2048,1,128]{2,1,0:T(1,128)}, u32[]{:S(2)}) copy-start(f32[2048,1,128]{2,1,0:T(1,128)} %shard_map.73) | copy-start | bytes 3145732

commit v3 on v2

--- a/solution.py
+++ b/solution.py
@@ -11,16 +11,16 @@
 VERT_DEV = 4096
 SWEEPS = 3
 BLOCK = 16
-RUN_BLOCK = 4
+RUN_BLOCK = 8
 
 
 ground_shift = 1.0
 degree_boost = 0.25
 
 
-def _pair_gather_kernel(a_ref, b_ref, x_ref, o_ref):
+def _pair_gather_kernel(half, a_ref, b_ref, x_ref, o_ref):
     lanes = x_ref.shape[2]
-    low = lax.broadcasted_iota(jnp.int32, (1, lanes), 1) < lanes // 2
+    low = (lax.broadcasted_iota(jnp.int32, (1, lanes), 1) // half) % 2 == 0
 
     def body(t, carry):
         base = t * BLOCK
@@ -32,9 +32,9 @@
     lax.fori_loop(0, o_ref.shape[0] // BLOCK, body, 0)
 
 
-def pair_gather(a, b, x):
+def pair_gather(a, b, x, half):
     return pl.pallas_call(
-        _pair_gather_kernel,
+        functools.partial(_pair_gather_kernel, half),
         out_shape=jax.ShapeDtypeStruct((a.shape[0],) + x.shape[1:], x.dtype),
         in_specs=[
             pl.BlockSpec(memory_space=pltpu.SMEM),
@@ -45,59 +45,49 @@
     )(a, b, x)
 
 
-def _sorted_scatter_kernel(key_ref, slot_ref, v0_ref, v1_ref, s0_ref, s1_ref, t0_ref, t1_ref):
-    lanes = s0_ref.shape[2]
-    rows = s0_ref.shape[0]
-    n = key_ref.shape[0] // 4
-    outs = (s0_ref, t0_ref, s1_ref, t1_ref)
-    vals = (v0_ref, v0_ref, v1_ref, v1_ref)
+def _runs_kernel(k0_ref, k1_ref, v_ref, o0_ref, o1_ref):
+    lanes = v_ref.shape[2]
+    rows = o0_ref.shape[0]
     step = 64
 
     @pl.loop(0, rows // step)
     def _(i):
         at = pl.ds(pl.multiple_of(i * step, step), step)
-        for o in outs:
-            o[at] = jnp.zeros((step,) + o.shape[1:], o.dtype)
+        o0_ref[at] = jnp.zeros((step,) + o0_ref.shape[1:], o0_ref.dtype)
+        o1_ref[at] = jnp.zeros((step,) + o1_ref.shape[1:], o1_ref.dtype)
 
     def body(t, carry):
-        runs, prevs = carry
-        runs, prevs = list(runs), list(prevs)
+        r0, r1, p0, p1 = carry
         base = t * RUN_BLOCK
-        got = [
-            [vals[c][slot_ref[c * n + base + r]] for c in range(4)] for r in range(RUN_BLOCK)
-        ]
+        got = [v_ref[base + r] for r in range(RUN_BLOCK)]
         for r in range(RUN_BLOCK):
-            for c in range(4):
-                k = key_ref[c * n + base + r]
-                runs[c] = jnp.where(k == prevs[c], runs[c], jnp.zeros_like(runs[c])) + got[r][c]
-                outs[c][k] = runs[c]
-                prevs[c] = k
-        return tuple(runs), tuple(prevs)
+            k0 = k0_ref[base + r]
+            k1 = k1_ref[base + r]
+            r0 = jnp.where(k0 == p0, r0, jnp.zeros_like(r0)) + got[r]
+            r1 = jnp.where(k1 == p1, r1, jnp.zeros_like(r1)) + got[r]
+            o0_ref[k0] = r0
+            o1_ref[k1] = r1
+            p0, p1 = k0, k1
+        return r0, r1, p0, p1
 
     zero = jnp.zeros((1, lanes), jnp.float32)
-    lax.fori_loop(0, n // RUN_BLOCK, body, ((zero,) * 4, (jnp.int32(-1),) * 4))
-
-    @pl.loop(0, rows // step)
-    def _(i):
-        at = pl.ds(pl.multiple_of(i * step, step), step)
-        s0_ref[at] += t0_ref[at]
-        s1_ref[at] += t1_ref[at]
+    lax.fori_loop(
+        0, v_ref.shape[0] // RUN_BLOCK, body, (zero, zero, jnp.int32(-1), jnp.int32(-1))
+    )
 
 
-def sorted_scatter(key, slot, v0, v1, rows):
-    shape = jax.ShapeDtypeStruct((rows,) + v0.shape[1:], v0.dtype)
+def runs(k0, k1, v, rows):
+    shape = jax.ShapeDtypeStruct((rows,) + v.shape[1:], v.dtype)
     return pl.pallas_call(
-        _sorted_scatter_kernel,
+        _runs_kernel,
         out_shape=(shape, shape),
         in_specs=[
             pl.BlockSpec(memory_space=pltpu.SMEM),
             pl.BlockSpec(memory_space=pltpu.SMEM),
             pl.BlockSpec(memory_space=pltpu.VMEM),
-            pl.BlockSpec(memory_space=pltpu.VMEM),
         ],
         out_specs=(pl.BlockSpec(memory_space=pltpu.VMEM), pl.BlockSpec(memory_space=pltpu.VMEM)),
-        scratch_shapes=[pltpu.VMEM((rows,) + v0.shape[1:], v0.dtype)] * 2,
-    )(key, slot, v0, v1)
+    )(k0, k1, v)
 
 
 def local(src_local, dst_local, edge_weight, send_counts, sketch):
@@ -131,26 +121,29 @@
     key_s, entry_s = lax.sort(
         (keys, jnp.arange(2 * edges, dtype=jnp.int32)), num_keys=1
     )
-    key_s = key_s % VERT_DEV
-    slot_s = entry_s % edges
+    key_0, key_1 = key_s[:edges], key_s[edges:] - VERT_DEV
+    slot_0, slot_1 = entry_s[:edges], entry_s[edges:] - edges
 
-    def scatter(v0, v1):
-        s0, s1 = sorted_scatter(key_s, slot_s, v0, v1, VERT_DEV)
-        return s0.reshape(VERT_DEV, lanes), s1.reshape(VERT_DEV, lanes)
+    def scatter(vals, half):
+        ordered = pair_gather(slot_0, slot_1, vals, half)
+        s0, s1 = runs(key_0, key_1, ordered, VERT_DEV)
+        return s0.reshape(VERT_DEV, -1), s1.reshape(VERT_DEV, -1)
 
     ones = jnp.ones((1, width), jnp.float32)
     s0, s1 = scatter(
-        jnp.concatenate([root, w_out[:, None] * ones], axis=1).reshape(edges, 1, lanes),
-        jnp.concatenate([-arrived_root, w_in[:, None] * ones], axis=1).reshape(edges, 1, lanes),
+        jnp.concatenate(
+            [root, -arrived_root, w_out[:, None] * ones, w_in[:, None] * ones], axis=1
+        ).reshape(edges, 1, 2 * lanes),
+        width,
     )
-    rhs = s0[:, :width] + s1[:, :width]
-    degree = s0[:, width] + s1[:, width]
+    rhs = s0[:, :width] + s1[:, width:lanes]
+    degree = s0[:, lanes] + s1[:, lanes + width]
     diag = ((1.0 + degree_boost) * degree + ground_shift)[:, None]
     extra = (degree_boost * degree + ground_shift)[:, None]
 
     def ends(field):
         doubled = jnp.concatenate([field, field], axis=1).reshape(VERT_DEV, 1, 2 * width)
-        return pair_gather(src_local, wanted, doubled)
+        return pair_gather(src_local, wanted, doubled, width)
 
     def apply(field):
         here = ends(field)
@@ -159,7 +152,7 @@
         flow_out = w_out[:, None] * (here[:, :width] - there[:, width:])
         flow_in = w_in[:, None] * (there[:, :width] - here[:, width:])
         flows = jnp.concatenate([flow_out, -flow_in], axis=1).reshape(edges, 1, lanes)
-        s0, s1 = scatter(flows, flows)
+        s0, s1 = scatter(flows, width)
         return (s0[:, :width] + s1[:, width:]) + extra * field
 
     sigma = 1.25

time: 281 us -> 286 us (1.018)
  blocking collectives: 77.9 us -> 124 us
  waiting for transfers between devices: 41.9 us -> 13.3 us
  starting transfers between devices: 23.6 us -> 7.29 us
  local copies, waits for them, and re-layouts: 9.21 us -> 23.3 us
  Pallas kernels: 84.9 us -> 78.6 us
  other arithmetic: 41.8 us -> 37.1 us
    all_to_all x2 -> x3, blocking collectives: 68.3 us -> 114 us  [a2a(): return lax.all_to_all(x, 'dom', split_axis=0, concat_axis=0, tiled=True)]
    all_to_all x2 -> x1, waiting for transfers between devices: 41.9 us -> 13.3 us  [a2a(): return lax.all_to_all(x, 'dom', split_axis=0, concat_axis=0, tiled=True)]
    all_to_all x2 -> x1, starting transfers between devices: 23.6 us -> 7.29 us  [a2a(): return lax.all_to_all(x, 'dom', split_axis=0, concat_axis=0, tiled=True)]
    reshape x0 -> x1, local copies, waits for them, and re-layouts: none -> 10 us  [local(): s0, s1 = scatter(jnp.concatenate([root, -arrived_root, w_out[:, None] * o...]
    pallas_call x6 -> x9, Pallas kernels: 84.9 us -> 78.6 us  [the longest x3 42.1 us: runs(): pl.pallas_call(_runs_kernel, out_shape=(shape, shape), in_specs=[pl.Block...]
    unnamed x22 -> x24, local copies, waits for them, and re-layouts: 2.82 us -> 6.88 us
    add x1, other arithmetic: 4.62 us -> 1.73 us  [local(): extra = (degree_boost * degree + ground_shift)[:, None]]
  transfers between devices with their start and end apart: 2 -> 1, of which waited for: 2 -> 1; matrix products, arithmetic and copies ran while one was open for 1% -> 1% of each run, Pallas kernels for 0% -> 0%
where the time goes in v3:
time: 286 us; the launch traced here: 285 us
  blocking collectives  124 us (43%)
  Pallas kernels  78.6 us (27%)
  other arithmetic  37.1 us (13%)
  local copies, waits for them, and re-layouts  23.3 us (8%)
  waiting for transfers between devices  13.3 us (5%)
  starting transfers between devices  7.29 us (3%)
    all_to_all x3, blocking collectives, a2a(): return lax.all_to_all(x, 'dom', split_axis=0, concat_axis=0, tiled=True)  114 us
    pallas_call x3, Pallas kernels, runs(): pl.pallas_call(_runs_kernel, out_shape=(shape, shape), in_specs=[pl.Block...  42.1 us
    pallas_call x6, Pallas kernels, pair_gather(): pl.pallas_call(functools.partial(_pair_gather_kernel, half), out_shape=ja...  36.4 us
    all_to_all x1, waiting for transfers between devices, a2a(): return lax.all_to_all(x, 'dom', split_axis=0, concat_axis=0, tiled=True)  13.3 us
    reshape x1, local copies, waits for them, and re-layouts, local(): s0, s1 = scatter(jnp.concatenate([root, -arrived_root, w_out[:, None] * o...  10 us
    psum x1, blocking collectives, local(): resistance = lax.psum(partial_sum, 'col') / SKETCH  9.66 us
    all_to_all x1, starting transfers between devices, a2a(): return lax.all_to_all(x, 'dom', split_axis=0, concat_axis=0, tiled=True)  7.29 us
    unnamed x24, local copies, waits for them, and re-layouts  6.88 us
  transfers between devices with their start and end apart: 1, of which 1 were waited for; matrix products, arithmetic and copies ran while one was open for 1% of the time, Pallas kernels for 0%

profile of v3, /device:TPU:1, one launch (start us, length us, event | category | flops | bytes accessed | tf_op | source)
XLA Modules:
  0.0 284.6 jit_solution(1748284838217456575)
XLA Ops:
  0.6 0.7 convert_element_type.14
  1.3 0.7 iota_compare_fusion
  2.2 0.8 reshape.146
  3.0 0.7 fusion.17
  3.7 0.9 compare_select_fusion
  4.6 1.2 copy.33
  5.8 0.3 multiply_bitcast_fusion
  6.7 46.4 %all_to_all.24 = f32[128,9,128]{2,1,0:T(8,128)S(1)} all-to-all(f32[128,9,128]{2,1,0:T(8,128)S(1)} %maximum_maximum_fusion), channel_id=1, replica_groups=mesh['dom'=128,'col'=2] {'dom'}, dimensions={0} | all-to-all | bytes 1179648 | tf_op jit(solution)/shard_map/all_to_all | solution.py:100
  54.0 0.3 mul.119
  54.3 0.3 mul.117
  54.6 0.9 maximum_bitcast_fusion
  55.5 10.0 %copy.37.x_ref = f32[2048,1,256]{2,1,0:T(1,128)} copy(f32[2048,1,256]{2,0,1:T(8,128)S(1)} %maximum_bitcast_fusion) | data formatting | bytes 4194304 | tf_op jit(solution)/shard_map/reshape | solution.py:136
  65.5 5.2 %sort.15 = (s32[4096]{0:T(1024)S(1)}, s32[4096]{0:T(1024)S(1)}) sort(s32[4096]{0:T(1024)S(1)} %pad_add_fusion, s32[4096]{0:T(1024)S(1)} %iota.12), dimensions={0}, to_apply=%region_0.0 | sort | flops 49152 | bytes 65536 | tf_op jit(solution)/shard_map/sort | solution.py:121
  70.7 0.6 slice_add_fusion.4
  71.3 8.0 %shard_map.68.v_ref = f32[2048,1,256]{2,1,0:T(1,128)} custom-call(s32[2048]{0:T(1024)} %get-tuple-element.35.a_ref, s32[2048]{0:T(1024)} %get-tuple-element.34.b_ref, f32[2048,1,256]{2,1,0:T(1,128)} %copy.37.x_ref), custom_call_target="tpu_custom_call" | custom-call | tf_op jit(solution)/shard_map/pallas_call | solution.py:36
  79.3 15.9 %shard_map.69 = (f32[4096,1,256]{2,1,0:T(1,128)}, f32[4096,1,256]{2,1,0:T(1,128)}) custom-call(s32[2048]{0:T(1024)} %get-tuple-element.38.k0_ref, s32[2048]{0:T(1024)} %get-tuple-element.39.k1_ref, f32[2048,1,256]{2,1,0:T(1,128)} %shard_map.68.v_ref), custom_call_target="tpu_custom_call" | custom-call | tf_op jit(solution)/shard_map/pallas_call | solution.py:81
  95.2 2.6 copy.47
  97.8 0.8 copy-done.7
  98.9 1.7 add_reduce_fusion
  100.7 0.4 copy-done.1
  101.0 1.2 broadcast_divide_fusion
  102.3 2.0 pad_maximum_fusion
  104.3 5.8 %shard_map.70 = f32[2048,1,128]{2,1,0:T(1,128)} custom-call(s32[2048]{0:T(1024)} %a_ref.5, s32[2048]{0:T(1024)} %copy-done.8, f32[4096,1,128]{2,1,0:T(1,128)} %bitcast.51), custom_call_target="tpu_custom_call" | custom-call | tf_op jit(solution)/shard_map/pallas_call | solution.py:36
  110.1 35.0 %all_to_all.25 = f32[2048,1,128]{2,1,0:T(1,128)S(1)} all-to-all(f32[2048,1,128]{2,1,0:T(1,128)} %shard_map.70), channel_id=1, replica_groups=mesh['dom'=128,'col'=2] {'dom'}, dimensions={0} | all-to-all | bytes 2097152 | tf_op jit(solution)/shard_map/all_to_all | solution.py:100
  145.2 1.2 fusion.15
  146.4 1.3 pad_maximum_fusion.3
  147.7 5.5 %shard_map.71.v_ref = f32[2048,1,128]{2,1,0:T(1,128)} custom-call(s32[2048]{0:T(1024)} %get-tuple-element.35.a_ref, s32[2048]{0:T(1024)} %get-tuple-element.34.b_ref, f32[2048,1,128]{2,1,0:T(1,128)} %bitcast.57), custom_call_target="tpu_custom_call" | custom-call | tf_op jit(solution)/shard_map/pallas_call | solution.py:36
  153.2 13.1 %shard_map.72 = (f32[4096,1,128]{2,1,0:T(1,128)}, f32[4096,1,128]{2,1,0:T(1,128)}) custom-call(s32[2048]{0:T(1024)} %get-tuple-element.38.k0_ref, s32[2048]{0:T(1024)} %get-tuple-element.39.k1_ref, f32[2048,1,128]{2,1,0:T(1,128)} %shard_map.71.v_ref), custom_call_target="tpu_custom_call" | custom-call | tf_op jit(solution)/shard_map/pallas_call | solution.py:81
  166.4 5.2 %divide_add_fusion = f32[4096,64]{1,0:T(8,128)S(1)} fusion(f32[4096,64]{1,0:T(8,128)S(1)} %broadcast_divide_fusion, f32[4096]{0:T(1024)S(1)} %get-tuple-element.27, f32[4096]{0:T(1024)S(1)} %get-tuple-element.26, f32[4096,128]{1,0:T(8,128)} %bitcast.54, f32[4096,128]{1,0:T(8,128)} %bitcast.52, f32[4096,256]{1,0:T(8,128)} %bitcast.40, f32[4096,256]{1,0:T(8,128)} %bitcast.36), kind=kLoop, calls=%fused_computation.18 | loop fusion | flops 2359296 | bytes 6324224 | tf_op jit(solution)/shard_map/add | solution.py:169
  171.6 2.0 pad_maximum_fusion.1
  173.5 5.8 %shard_map.73 = f32[2048,1,128]{2,1,0:T(1,128)} custom-call(s32[2048]{0:T(1024)} %a_ref.5, s32[2048]{0:T(1024)} %copy-done.8, f32[4096,1,128]{2,1,0:T(1,128)} %bitcast.49), custom_call_target="tpu_custom_call" | custom-call | tf_op jit(solution)/shard_map/pallas_call | solution.py:36
  179.3 33.1 %all_to_all.26 = f32[2048,1,128]{2,1,0:T(1,128)S(1)} all-to-all(f32[2048,1,128]{2,1,0:T(1,128)} %shard_map.73), channel_id=1, replica_groups=mesh['dom'=128,'col'=2] {'dom'}, dimensions={0} | all-to-all | bytes 2097152 | tf_op jit(solution)/shard_map/all_to_all | solution.py:100
  212.4 1.2 fusion.12
  213.7 1.3 pad_maximum_fusion.4
  215.0 5.5 %shard_map.74.v_ref = f32[2048,1,128]{2,1,0:T(1,128)} custom-call(s32[2048]{0:T(1024)} %get-tuple-element.35.a_ref, s32[2048]{0:T(1024)} %get-tuple-element.34.b_ref, f32[2048,1,128]{2,1,0:T(1,128)} %bitcast.56), custom_call_target="tpu_custom_call" | custom-call | tf_op jit(solution)/shard_map/pallas_call | solution.py:36
  220.4 13.1 %shard_map.75 = (f32[4096,1,128]{2,1,0:T(1,128)}, f32[4096,1,128]{2,1,0:T(1,128)}) custom-call(s32[2048]{0:T(1024)} %get-tuple-element.38.k0_ref, s32[2048]{0:T(1024)} %get-tuple-element.39.k1_ref, f32[2048,1,128]{2,1,0:T(1,128)} %shard_map.74.v_ref), custom_call_target="tpu_custom_call" | custom-call | tf_op jit(solution)/shard_map/pallas_call | solution.py:81
  233.6 6.4 %fusion.5 = f32[4096,64]{1,0:T(8,128)S(1)} fusion(f32[4096,128]{1,0:T(8,128)} %bitcast.59, f32[4096,128]{1,0:T(8,128)} %bitcast.58, f32[4096,64]{1,0:T(8,128)S(1)} %broadcast_divide_fusion, f32[4096]{0:T(1024)S(1)} %get-tuple-element.26, f32[4096]{0:T(1024)S(1)} %get-tuple-element.27, f32[4096,128]{1,0:T(8,128)} %bitcast.55, f32[4096,128]{1,0:T(8,128)} %bitcast.53, ...), kind=kLoop, calls=%fused_computation.8 | loop fusion | flops 4980736 | bytes 8421376 | tf_op jit(solution)/shard_map/add | solution.py:165
  240.0 1.9 pad_maximum_fusion.2
  241.9 5.8 %shard_map.76 = f32[2048,1,128]{2,1,0:T(1,128)} custom-call(s32[2048]{0:T(1024)} %a_ref.5, s32[2048]{0:T(1024)} %copy-done.8, f32[4096,1,128]{2,1,0:T(1,128)} %bitcast.50), custom_call_target="tpu_custom_call" | custom-call | tf_op jit(solution)/shard_map/pallas_call | solution.py:36
  247.8 1.7 slice.120
  249.5 1.0 all_to_all.18
  250.5 7.3 %all-to-all-start.3 = ((f32[128,8,128]{2,1,0:T(8,128)}), f32[128,8,128]{2,1,0:T(8,128)}, u32[]{:S(2)}, u32[]{:S(2)}) async-start(f32[128,8,128]{2,1,0:T(8,128)} %all_to_all.18), calls=%async_computation.3 | async-start | bytes 1048576 | tf_op jit(solution)/shard_map/all_to_all | solution.py:100
  257.8 1.6 copy.41
  259.4 13.3 %all-to-all-done.3 = f32[128,8,128]{2,1,0:T(8,128)} async-done(((f32[128,8,128]{2,1,0:T(8,128)}), f32[128,8,128]{2,1,0:T(8,128)}, u32[]{:S(2)}, u32[]{:S(2)}) %all-to-all-start.3) | async-done | bytes 524320 | tf_op jit(solution)/shard_map/all_to_all | solution.py:100
  272.7 1.2 reshape.165
  274.0 0.3 fusion.9
  274.3 9.7 %psum.7 = f32[2048]{0:T(1024)S(1)} all-reduce(f32[2048]{0:T(1024)S(1)} %broadcast_select_fusion), channel_id=1, replica_groups=mesh['dom'=128,'col'=2] {'col'}, use_global_device_ids=true, to_apply=%region_2.0 | all-reduce | flops 2048 | bytes 16384 | tf_op jit(solution)/shard_map/psum | solution.py:175
  284.0 0.6 broadcast_multiply_fusion
  (35 shorter events, 1.8 us)
Async XLA Ops:
  53.7 0.9 copy-start.8
  55.5 10.0 %copy-start.9 = (s32[2048]{0:T(1024)S(1)}, s32[2048]{0:T(1024)}, u32[]{:S(2)}) copy-start(s32[2048]{0:T(1024)} %a_ref.5) | copy-start | bytes 24580
  95.2 3.4 %copy-start.7 = (f32[4096,1,256]{2,1,0:T(1,128)S(1)}, f32[4096,1,256]{2,1,0:T(1,128)}, u32[]{:S(2)}) copy-start(f32[4096,1,256]{2,1,0:T(1,128)} %get-tuple-element.13) | copy-start | bytes 12582916
  97.8 2.9 %copy-start = (f32[4096,1,256]{2,0,1:T(8,128)}, f32[4096,1,256]{2,0,1:T(8,128)S(1)}, u32[]{:S(2)}) copy-start(f32[4096,1,256]{2,0,1:T(8,128)S(1)} %copy.47) | copy-start | bytes 12582916
  98.9 2.1 copy-start.1
  110.1 35.1 %copy-start.5 = (f32[2048,1,128]{2,1,0:T(1,128)S(1)}, f32[2048,1,128]{2,1,0:T(1,128)}, u32[]{:S(2)}) copy-start(f32[2048,1,128]{2,1,0:T(1,128)} %shard_map.70) | copy-start | bytes 3145732
  179.3 33.1 %copy-start.4 = (f32[2048,1,128]{2,1,0:T(1,128)S(1)}, f32[2048,1,128]{2,1,0:T(1,128)}, u32[]{:S(2)}) copy-start(f32[2048,1,128]{2,1,0:T(1,128)} %shard_map.73) | copy-start | bytes 3145732
  240.0 1.9 copy-start.2
  247.8 10.0 %copy-start.3 = (f32[4096,64]{1,0:T(8,128)S(1)}, f32[4096,64]{1,0:T(8,128)}, u32[]{:S(2)}) copy-start(f32[4096,64]{1,0:T(8,128)} %copy-done.2) | copy-start | bytes 3145732
  250.5 22.2 %all-to-all-start.3 = ((f32[128,8,128]{2,1,0:T(8,128)}), f32[128,8,128]{2,1,0:T(8,128)}, u32[]{:S(2)}, u32[]{:S(2)}) async-start(f32[128,8,128]{2,1,0:T(8,128)} %all_to_all.18), calls=%async_computation.3 | async-start | bytes 1048576 | tf_op jit(solution)/shard_map/all_to_all | solution.py:100
  257.8 16.2 %copy-start.6 = (f32[2048,1,128]{2,1,0:T(1,128)S(1)}, f32[2048,1,128]{2,1,0:T(1,128)}, u32[]{:S(2)}) copy-start(f32[2048,1,128]{2,1,0:T(1,128)} %shard_map.76) | copy-start | bytes 3145732

commit v4 on v1

--- a/solution.py
+++ b/solution.py
@@ -46,7 +46,12 @@
 
 def _sorted_scatter_kernel(half, key_ref, slot_ref, side_ref, v_ref, o_ref):
     lanes = o_ref.shape[2]
-    o_ref[...] = jnp.zeros(o_ref.shape, o_ref.dtype)
+    step = 64
+
+    @pl.loop(0, o_ref.shape[0] // step)
+    def _(i):
+        at = pl.ds(pl.multiple_of(i * step, step), step)
+        o_ref[at] = jnp.zeros((step,) + o_ref.shape[1:], o_ref.dtype)
     group = (lax.broadcasted_iota(jnp.int32, (1, lanes), 1) // half) % 2
 
     def body(t, carry):
@@ -96,13 +101,20 @@
     live = (jnp.arange(cap)[None, :] < send_counts.reshape(peers, 1)).astype(jnp.float32)
     w_out = (edge_weight.reshape(peers, cap) * live).reshape(-1)
     root = jnp.sqrt(w_out)[:, None] * sketch.astype(jnp.float32).T
-    payload = jnp.concatenate(
-        [root, w_out[:, None], dst_local.astype(jnp.float32)[:, None]], axis=1
+    lanes = 2 * width
+    side_row = jnp.concatenate(
+        [
+            w_out.reshape(peers, 1, cap),
+            dst_local.astype(jnp.float32).reshape(peers, 1, cap),
+            jnp.zeros((peers, 1, lanes - 2 * cap), jnp.float32),
+        ],
+        axis=2,
     )
+    payload = jnp.concatenate([root.reshape(peers, -1, lanes), side_row], axis=1)
     arrived = a2a(payload)
-    arrived_root = arrived[:, :width]
-    w_in = arrived[:, width]
-    wanted = arrived[:, width + 1].astype(jnp.int32)
+    arrived_root = arrived[:, :-1].reshape(edges, width)
+    w_in = arrived[:, -1, :cap].reshape(-1)
+    wanted = arrived[:, -1, cap:2 * cap].reshape(-1).astype(jnp.int32)
 
     keys = jnp.stack([src_local, wanted], axis=1).reshape(-1)
     key_s, entry_s = lax.sort(
@@ -112,15 +124,18 @@
     side_s = entry_s % 2
 
     def scatter(vals):
-        return sorted_scatter(width, key_s, slot_s, side_s, vals, VERT_DEV)
+        return sorted_scatter(width, key_s, slot_s, side_s, vals, VERT_DEV).reshape(
+            VERT_DEV, -1
+        )
 
     ones = jnp.ones((1, width), jnp.float32)
-    first = jnp.concatenate(
-        [root, -arrived_root, w_out[:, None] * ones, w_in[:, None] * ones], axis=1
-    ).reshape(edges, 1, 4 * width)
-    acc = scatter(first).reshape(VERT_DEV, 4 * width)
-    rhs = acc[:, :width] + acc[:, width:2 * width]
-    degree = acc[:, 2 * width] + acc[:, 3 * width]
+    acc = scatter(
+        jnp.concatenate(
+            [root, -arrived_root, w_out[:, None] * ones, w_in[:, None] * ones], axis=1
+        ).reshape(edges, 1, 2 * lanes)
+    )
+    rhs = acc[:, :width] + acc[:, width:lanes]
+    degree = acc[:, lanes] + acc[:, lanes + width]
     diag = ((1.0 + degree_boost) * degree + ground_shift)[:, None]
     extra = (degree_boost * degree + ground_shift)[:, None]
 
@@ -134,8 +149,8 @@
         here = here.reshape(edges, 2 * width)
         flow_out = w_out[:, None] * (here[:, :width] - there[:, width:])
         flow_in = w_in[:, None] * (there[:, :width] - here[:, width:])
-        flows = jnp.concatenate([flow_out, -flow_in], axis=1).reshape(edges, 1, 2 * width)
-        acc = scatter(flows).reshape(VERT_DEV, 2 * width)
+        flows = jnp.concatenate([flow_out, -flow_in], axis=1).reshape(edges, 1, lanes)
+        acc = scatter(flows)
         return (acc[:, :width] + acc[:, width:]) + extra * field
 
     sigma = 1.25

time: 289 us -> 284 us (0.983)
  blocking collectives: 77.8 us -> 124 us
  waiting for transfers between devices: 43 us -> 13.3 us
  starting transfers between devices: 24.2 us -> 7.29 us
  other arithmetic: 42.4 us -> 38 us
    all_to_all x2 -> x3, blocking collectives: 68.1 us -> 114 us  [a2a(): return lax.all_to_all(x, 'dom', split_axis=0, concat_axis=0, tiled=True)]
    all_to_all x2 -> x1, waiting for transfers between devices: 43 us -> 13.3 us  [a2a(): return lax.all_to_all(x, 'dom', split_axis=0, concat_axis=0, tiled=True)]
    all_to_all x2 -> x1, starting transfers between devices: 24.2 us -> 7.29 us  [a2a(): return lax.all_to_all(x, 'dom', split_axis=0, concat_axis=0, tiled=True)]
    unnamed x21 -> x19, local copies, waits for them, and re-layouts: 6.21 us -> 5.47 us
    reshape x1 -> x3, local copies, waits for them, and re-layouts: 10 us -> 10.3 us  [the longest x1 10 us: local(): acc = scatter(jnp.concatenate([root, -arrived_root, w_out[:, None] * ones...]
  transfers between devices with their start and end apart: 2 -> 1, of which waited for: 2 -> 1; matrix products, arithmetic and copies ran while one was open for 1% -> 1% of each run, Pallas kernels for 0% -> 0%
where the time goes in v4:
time: 284 us; the launch traced here: 283 us
  blocking collectives  124 us (44%)
  Pallas kernels  75.4 us (27%)
  other arithmetic  38 us (13%)
  local copies, waits for them, and re-layouts  24.3 us (9%)
  waiting for transfers between devices  13.3 us (5%)
  starting transfers between devices  7.29 us (3%)
    all_to_all x3, blocking collectives, a2a(): return lax.all_to_all(x, 'dom', split_axis=0, concat_axis=0, tiled=True)  114 us
    pallas_call x3, Pallas kernels, sorted_scatter(): pl.pallas_call(functools.partial(_sorted_scatter_kernel, half), out_shape...  58 us
    pallas_call x3, Pallas kernels, pair_gather(): pl.pallas_call(_pair_gather_kernel, out_shape=jax.ShapeDtypeStruct((a.sha...  17.4 us
    all_to_all x1, waiting for transfers between devices, a2a(): return lax.all_to_all(x, 'dom', split_axis=0, concat_axis=0, tiled=True)  13.3 us
    reshape x1, local copies, waits for them, and re-layouts, local(): acc = scatter(jnp.concatenate([root, -arrived_root, w_out[:, None] * ones...  10 us
    psum x1, blocking collectives, local(): resistance = lax.psum(partial_sum, 'col') / SKETCH  9.66 us
    all_to_all x1, starting transfers between devices, a2a(): return lax.all_to_all(x, 'dom', split_axis=0, concat_axis=0, tiled=True)  7.29 us
    concatenate x3, other arithmetic, ends(): jnp.concatenate([field, field], axis=1).reshape(VERT_DEV, 1, 2 * width)  5.81 us
  transfers between devices with their start and end apart: 1, of which 1 were waited for; matrix products, arithmetic and copies ran while one was open for 1% of the time, Pallas kernels for 0%

profile of v4, /device:TPU:1, one launch (start us, length us, event | category | flops | bytes accessed | tf_op | source)
XLA Modules:
  0.0 283.3 jit_solution(12404491029234695919)
XLA Ops:
  0.6 0.7 convert_element_type.16
  1.3 0.7 iota_compare_fusion
  2.2 0.8 reshape.151
  3.0 0.7 fusion.19
  3.7 0.9 compare_select_fusion
  4.6 1.2 copy.35
  5.8 0.3 multiply_bitcast_fusion
  6.7 46.4 %all_to_all.24 = f32[128,9,128]{2,1,0:T(8,128)S(1)} all-to-all(f32[128,9,128]{2,1,0:T(8,128)S(1)} %maximum_maximum_fusion), channel_id=1, replica_groups=mesh['dom'=128,'col'=2] {'dom'}, dimensions={0} | all-to-all | bytes 1179648 | tf_op jit(solution)/shard_map/all_to_all | solution.py:99
  53.8 0.7 convert_element_type.19.b_ref
  54.5 0.8 slice_negate_fusion
  55.4 1.2 neg.13
  56.6 0.4 copy.39
  57.0 0.5 reshape.153
  57.5 5.8 %sort.15 = (s32[4096]{0:T(1024)}, s32[4096]{0:T(1024)S(1)}) sort(s32[4096]{0:T(1024)S(1)} %reshape.153, s32[4096]{0:T(1024)S(1)} %iota.12), dimensions={0}, to_apply=%region_0.0 | sort | flops 49152 | bytes 65536 | tf_op jit(solution)/shard_map/sort | solution.py:120
  63.3 0.6 add_select_fusion
  63.9 0.3 mul.119
  64.2 0.3 mul.117
  64.6 0.9 maximum_bitcast_fusion
  65.4 10.0 %copy.40.v_ref = f32[2048,1,256]{2,1,0:T(1,128)} copy(f32[2048,1,256]{2,0,1:T(8,128)S(1)} %maximum_bitcast_fusion) | data formatting | bytes 4194304 | tf_op jit(solution)/shard_map/reshape | solution.py:135
  75.4 21.0 %shard_map.68 = f32[4096,1,256]{2,1,0:T(1,128)} custom-call(s32[4096]{0:T(1024)} %get-tuple-element.4.key_ref, s32[4096]{0:T(1024)} %get-tuple-element.25.slot_ref, s32[4096]{0:T(1024)} %get-tuple-element.24.side_ref, f32[2048,1,256]{2,1,0:T(1,128)} %copy.40.v_ref), custom_call_target="tpu_custom_call" | custom-call | tf_op jit(solution)/shard_map/pallas_call | solution.py:79
  96.5 2.5 copy.47
  99.0 1.7 add_reduce_fusion
  100.9 1.2 broadcast_divide_fusion
  102.1 1.9 pad_maximum_fusion
  104.1 5.8 %shard_map.69 = f32[2048,1,128]{2,1,0:T(1,128)} custom-call(s32[2048]{0:T(1024)} %a_ref.5, s32[2048]{0:T(1024)} %convert_element_type.19.b_ref, f32[4096,1,128]{2,1,0:T(1,128)} %bitcast.45), custom_call_target="tpu_custom_call" | custom-call | tf_op jit(solution)/shard_map/pallas_call | solution.py:35
  109.9 35.0 %all_to_all.25 = f32[2048,1,128]{2,1,0:T(1,128)S(1)} all-to-all(f32[2048,1,128]{2,1,0:T(1,128)} %shard_map.69), channel_id=1, replica_groups=mesh['dom'=128,'col'=2] {'dom'}, dimensions={0} | all-to-all | bytes 2097152 | tf_op jit(solution)/shard_map/all_to_all | solution.py:99
  144.9 1.2 fusion.15
  146.2 1.3 pad_maximum_fusion.3
  147.5 18.4 %shard_map.70 = f32[4096,1,128]{2,1,0:T(1,128)} custom-call(s32[4096]{0:T(1024)} %get-tuple-element.4.key_ref, s32[4096]{0:T(1024)} %get-tuple-element.25.slot_ref, s32[4096]{0:T(1024)} %get-tuple-element.24.side_ref, f32[2048,1,128]{2,1,0:T(1,128)} %bitcast.49), custom_call_target="tpu_custom_call" | custom-call | tf_op jit(solution)/shard_map/pallas_call | solution.py:79
  165.9 5.3 %divide_add_fusion = f32[4096,64]{1,0:T(8,128)S(1)} fusion(f32[4096]{0:T(1024)S(1)} %get-tuple-element.15, f32[4096]{0:T(1024)S(1)} %get-tuple-element.14, f32[4096,128]{1,0:T(8,128)} %bitcast.35, f32[4096,256]{1,0:T(8,128)} %bitcast.33), kind=kLoop, calls=%fused_computation.17 | loop fusion | flops 2621440 | bytes 5275648 | tf_op jit(solution)/shard_map/add | solution.py:167
  171.2 2.0 pad_maximum_fusion.1
  173.2 5.8 %shard_map.71 = f32[2048,1,128]{2,1,0:T(1,128)} custom-call(s32[2048]{0:T(1024)} %a_ref.5, s32[2048]{0:T(1024)} %convert_element_type.19.b_ref, f32[4096,1,128]{2,1,0:T(1,128)} %bitcast.46), custom_call_target="tpu_custom_call" | custom-call | tf_op jit(solution)/shard_map/pallas_call | solution.py:35
  179.0 33.1 %all_to_all.26 = f32[2048,1,128]{2,1,0:T(1,128)S(1)} all-to-all(f32[2048,1,128]{2,1,0:T(1,128)} %shard_map.71), channel_id=1, replica_groups=mesh['dom'=128,'col'=2] {'dom'}, dimensions={0} | all-to-all | bytes 2097152 | tf_op jit(solution)/shard_map/all_to_all | solution.py:99
  212.0 1.2 fusion.12
  213.3 1.3 pad_maximum_fusion.4
  214.6 18.5 %shard_map.72 = f32[4096,1,128]{2,1,0:T(1,128)} custom-call(s32[4096]{0:T(1024)} %get-tuple-element.4.key_ref, s32[4096]{0:T(1024)} %get-tuple-element.25.slot_ref, s32[4096]{0:T(1024)} %get-tuple-element.24.side_ref, f32[2048,1,128]{2,1,0:T(1,128)} %bitcast.48), custom_call_target="tpu_custom_call" | custom-call | tf_op jit(solution)/shard_map/pallas_call | solution.py:79
  233.1 5.6 %fusion.5 = f32[4096,64]{1,0:T(8,128)S(1)} fusion(f32[4096,128]{1,0:T(8,128)} %bitcast.37, f32[4096]{0:T(1024)S(1)} %get-tuple-element.14, f32[4096]{0:T(1024)S(1)} %get-tuple-element.15, f32[4096,128]{1,0:T(8,128)S(1)} %bitcast.36, f32[4096,256]{1,0:T(8,128)} %bitcast.34), kind=kLoop, calls=%fused_computation.7 | loop fusion | flops 5242880 | bytes 7372800 | tf_op jit(solution)/shard_map/add | solution.py:163
  238.7 1.9 pad_maximum_fusion.2
  240.7 5.8 %shard_map.73 = f32[2048,1,128]{2,1,0:T(1,128)} custom-call(s32[2048]{0:T(1024)} %a_ref.5, s32[2048]{0:T(1024)} %convert_element_type.19.b_ref, f32[4096,1,128]{2,1,0:T(1,128)} %bitcast.47), custom_call_target="tpu_custom_call" | custom-call | tf_op jit(solution)/shard_map/pallas_call | solution.py:35
  246.5 1.7 slice.104
  248.2 1.0 all_to_all.18
  249.2 7.3 %all-to-all-start.3 = ((f32[128,8,128]{2,1,0:T(8,128)}), f32[128,8,128]{2,1,0:T(8,128)}, u32[]{:S(2)}, u32[]{:S(2)}) async-start(f32[128,8,128]{2,1,0:T(8,128)} %all_to_all.18), calls=%async_computation.3 | async-start | bytes 1048576 | tf_op jit(solution)/shard_map/all_to_all | solution.py:99
  256.5 1.6 copy.44
  258.1 13.3 %all-to-all-done.3 = f32[128,8,128]{2,1,0:T(8,128)} async-done(((f32[128,8,128]{2,1,0:T(8,128)}), f32[128,8,128]{2,1,0:T(8,128)}, u32[]{:S(2)}, u32[]{:S(2)}) %all-to-all-start.3) | async-done | bytes 524320 | tf_op jit(solution)/shard_map/all_to_all | solution.py:99
  271.4 1.2 reshape.168
  272.7 0.3 fusion.9
  273.1 9.7 %psum.7 = f32[2048]{0:T(1024)S(1)} all-reduce(f32[2048]{0:T(1024)S(1)} %broadcast_select_fusion), channel_id=1, replica_groups=mesh['dom'=128,'col'=2] {'col'}, use_global_device_ids=true, to_apply=%region_2.3 | all-reduce | flops 2048 | bytes 16384 | tf_op jit(solution)/shard_map/psum | solution.py:173
  282.7 0.6 broadcast_multiply_fusion
  (29 shorter events, 1.7 us)
Async XLA Ops:
  53.1 3.5 %copy-start.7 = (s32[2048]{0:T(1024)S(1)}, s32[2048]{0:T(1024)}, u32[]{:S(2)}) copy-start(s32[2048]{0:T(1024)} %a_ref.5) | copy-start | bytes 24580
  98.9 1.9 copy-start
  109.9 35.1 %copy-start.5 = (f32[2048,1,128]{2,1,0:T(1,128)S(1)}, f32[2048,1,128]{2,1,0:T(1,128)}, u32[]{:S(2)}) copy-start(f32[2048,1,128]{2,1,0:T(1,128)} %shard_map.69) | copy-start | bytes 3145732
  179.0 33.1 %copy-start.4 = (f32[2048,1,128]{2,1,0:T(1,128)S(1)}, f32[2048,1,128]{2,1,0:T(1,128)}, u32[]{:S(2)}) copy-start(f32[2048,1,128]{2,1,0:T(1,128)} %shard_map.71) | copy-start | bytes 3145732
  214.6 18.5 %copy-start.1 = (f32[4096,1,128]{2,1,0:T(1,128)S(1)}, f32[4096,1,128]{2,1,0:T(1,128)}, u32[]{:S(2)}) copy-start(f32[4096,1,128]{2,1,0:T(1,128)} %shard_map.70) | copy-start | bytes 6291460
  238.7 1.9 copy-start.2
  246.5 10.0 %copy-start.3 = (f32[4096,64]{1,0:T(8,128)S(1)}, f32[4096,64]{1,0:T(8,128)}, u32[]{:S(2)}) copy-start(f32[4096,64]{1,0:T(8,128)} %copy-done.2) | copy-start | bytes 3145732
  249.2 22.2 %all-to-all-start.3 = ((f32[128,8,128]{2,1,0:T(8,128)}), f32[128,8,128]{2,1,0:T(8,128)}, u32[]{:S(2)}, u32[]{:S(2)}) async-start(f32[128,8,128]{2,1,0:T(8,128)} %all_to_all.18), calls=%async_computation.3 | async-start | bytes 1048576 | tf_op jit(solution)/shard_map/all_to_all | solution.py:99
  256.5 16.2 %copy-start.6 = (f32[2048,1,128]{2,1,0:T(1,128)S(1)}, f32[2048,1,128]{2,1,0:T(1,128)}, u32[]{:S(2)}) copy-start(f32[2048,1,128]{2,1,0:T(1,128)} %shard_map.73) | copy-start | bytes 3145732

commit v5 on v4

--- a/solution.py
+++ b/solution.py
@@ -11,6 +11,7 @@
 VERT_DEV = 4096
 SWEEPS = 3
 BLOCK = 16
+CHUNKS = 2
 
 
 ground_shift = 1.0
@@ -143,15 +144,39 @@
         doubled = jnp.concatenate([field, field], axis=1).reshape(VERT_DEV, 1, 2 * width)
         return pair_gather(src_local, wanted, doubled)
 
+    part = cap // CHUNKS
+
+    def chunk(x, c):
+        return x.reshape(peers, cap, -1)[:, c * part:(c + 1) * part].reshape(
+            (peers * part,) + x.shape[1:]
+        )
+
+    parts = []
+    for c in range(CHUNKS):
+        src_c, wanted_c = chunk(src_local, c), chunk(wanted, c)
+        keys_c = jnp.stack([src_c, wanted_c], axis=1).reshape(-1)
+        key_c, entry_c = lax.sort(
+            (keys_c, jnp.arange(2 * peers * part, dtype=jnp.int32)), num_keys=1
+        )
+        parts.append(
+            (src_c, wanted_c, chunk(w_out, c), chunk(w_in, c), key_c, entry_c // 2, entry_c % 2)
+        )
+
     def apply(field):
-        here = ends(field)
-        there = a2a(here).reshape(edges, 2 * width)
-        here = here.reshape(edges, 2 * width)
-        flow_out = w_out[:, None] * (here[:, :width] - there[:, width:])
-        flow_in = w_in[:, None] * (there[:, :width] - here[:, width:])
-        flows = jnp.concatenate([flow_out, -flow_in], axis=1).reshape(edges, 1, lanes)
-        acc = scatter(flows)
-        return (acc[:, :width] + acc[:, width:]) + extra * field
+        doubled = jnp.concatenate([field, field], axis=1).reshape(VERT_DEV, 1, 2 * width)
+        total = None
+        for src_c, wanted_c, w_out_c, w_in_c, key_c, slot_c, side_c in parts:
+            here = pair_gather(src_c, wanted_c, doubled)
+            there = a2a(here).reshape(-1, 2 * width)
+            here = here.reshape(-1, 2 * width)
+            flow_out = w_out_c[:, None] * (here[:, :width] - there[:, width:])
+            flow_in = w_in_c[:, None] * (there[:, :width] - here[:, width:])
+            flows = jnp.concatenate([flow_out, -flow_in], axis=1).reshape(-1, 1, lanes)
+            acc = sorted_scatter(width, key_c, slot_c, side_c, flows, VERT_DEV).reshape(
+                VERT_DEV, lanes
+            )
+            total = acc if total is None else total + acc
+        return (total[:, :width] + total[:, width:]) + extra * field
 
     sigma = 1.25
     delta = 0.8

time: 284 us -> 308 us (1.085)
  blocking collectives: 124 us -> 9.68 us
  waiting for transfers between devices: 13.3 us -> 68.6 us
  starting transfers between devices: 7.29 us -> 59.3 us
  other arithmetic: 38 us -> 54.2 us
  Pallas kernels: 75.4 us -> 86.2 us
    all_to_all x3 -> x0, blocking collectives: 114 us -> none  [a2a(): return lax.all_to_all(x, 'dom', split_axis=0, concat_axis=0, tiled=True)]
    all_to_all x1 -> x6, waiting for transfers between devices: 13.3 us -> 68.6 us  [a2a(): return lax.all_to_all(x, 'dom', split_axis=0, concat_axis=0, tiled=True)]
    all_to_all x1 -> x6, starting transfers between devices: 7.29 us -> 59.3 us  [a2a(): return lax.all_to_all(x, 'dom', split_axis=0, concat_axis=0, tiled=True)]
    sort x0 -> x2, other arithmetic: none -> 10.1 us  [local(): lax.sort((keys_c, jnp.arange(2 * peers * part, dtype=jnp.int32)), num_key...]
    reshape x1, local copies, waits for them, and re-layouts: 10 us -> 2.71 us  [local(): acc = scatter(jnp.concatenate([root, -arrived_root, w_out[:, None] * ones...]
    pallas_call x3 -> x5, Pallas kernels: 58 us -> 64.2 us  [sorted_scatter(): pl.pallas_call(functools.partial(_sorted_scatter_kernel, half), out_shape...]
    concatenate x2 -> x7, other arithmetic: 2.62 us -> 8.78 us  [the longest x4 4.05 us: apply(): flows = jnp.concatenate([flow_out, -flow_in], axis=1).reshape(-1, 1, lanes)]
    add x0 -> x2, other arithmetic: none -> 5.17 us  [apply(): total = acc if total is None else total + acc]
  transfers between devices with their start and end apart: 1 -> 6, of which waited for: 1 -> 6; matrix products, arithmetic and copies ran while one was open for 1% -> 7% of each run, Pallas kernels for 0% -> 6%
where the time goes in v5:
time: 308 us; the launch traced here: 306 us
  Pallas kernels  86.2 us (28%)
  waiting for transfers between devices  68.6 us (22%)
  starting transfers between devices  59.3 us (19%)
  other arithmetic  54.2 us (18%)
  local copies, waits for them, and re-layouts  27.2 us (9%)
  blocking collectives  9.68 us (3%)
    all_to_all x6, waiting for transfers between devices, a2a(): return lax.all_to_all(x, 'dom', split_axis=0, concat_axis=0, tiled=True)  68.6 us
    pallas_call x5, Pallas kernels, sorted_scatter(): pl.pallas_call(functools.partial(_sorted_scatter_kernel, half), out_shape...  64.2 us
    all_to_all x6, starting transfers between devices, a2a(): return lax.all_to_all(x, 'dom', split_axis=0, concat_axis=0, tiled=True)  59.3 us
    pallas_call x5, Pallas kernels, pair_gather(): pl.pallas_call(_pair_gather_kernel, out_shape=jax.ShapeDtypeStruct((a.sha...  22 us
    sort x2, other arithmetic, local(): lax.sort((keys_c, jnp.arange(2 * peers * part, dtype=jnp.int32)), num_key...  10.1 us
    psum x1, blocking collectives, local(): resistance = lax.psum(partial_sum, 'col') / SKETCH  9.68 us
    unnamed x47, local copies, waits for them, and re-layouts  8.04 us
  transfers between devices with their start and end apart: 6, of which 6 were waited for; matrix products, arithmetic and copies ran while one was open for 7% of the time, Pallas kernels for 6%

profile of v5, /device:TPU:1, one launch (start us, length us, event | category | flops | bytes accessed | tf_op | source)
XLA Modules:
  0.0 306.3 jit_solution(9670449174748114811)
XLA Ops:
  3.0 1.3 fusion.30
  5.2 1.2 copy.61
  7.1 1.2 maximum_maximum_fusion
  8.3 16.3 %all-to-all-start = ((f32[128,9,128]{2,1,0:T(8,128)}), f32[128,9,128]{2,1,0:T(8,128)S(1)}, u32[]{:S(2)}, u32[]{:S(2)}) async-start(f32[128,9,128]{2,1,0:T(8,128)} %maximum_maximum_fusion), calls=%async_computation | async-start | bytes 2097152 | tf_op jit(solution)/shard_map/all_to_all | solution.py:100
  25.5 29.4 %all-to-all-done = f32[128,9,128]{2,1,0:T(8,128)S(1)} async-done(((f32[128,9,128]{2,1,0:T(8,128)}), f32[128,9,128]{2,1,0:T(8,128)S(1)}, u32[]{:S(2)}, u32[]{:S(2)}) %all-to-all-start) | async-done | bytes 589856 | tf_op jit(solution)/shard_map/all_to_all | solution.py:100
  57.8 1.2 neg.19
  59.7 1.1 copy.65
  61.3 5.8 %sort.45 = (s32[4096]{0:T(1024)}, s32[4096]{0:T(1024)S(1)}) sort(s32[4096]{0:T(1024)S(1)} %reshape.255, s32[4096]{0:T(1024)S(1)} %iota.21), dimensions={0}, to_apply=%region_0.0 | sort | flops 49152 | bytes 65536 | tf_op jit(solution)/shard_map/sort | solution.py:121
  70.6 2.7 reshape.256.v_ref
  73.4 21.1 %shard_map.68 = f32[4096,1,256]{2,1,0:T(1,128)} custom-call(s32[4096]{0:T(1024)} %get-tuple-element.8.key_ref, s32[4096]{0:T(1024)} %get-tuple-element.46.slot_ref, s32[4096]{0:T(1024)} %get-tuple-element.45.side_ref, f32[2048,1,256]{2,1,0:T(1,128)} %reshape.256.v_ref), custom_call_target="tpu_custom_call" | custom-call | tf_op jit(solution)/shard_map/pallas_call | solution.py:80
  94.4 2.5 copy.81
  96.9 1.7 add_reduce_fusion
  98.8 1.2 broadcast_divide_fusion
  100.1 1.9 pad_maximum_fusion.1
  102.0 4.0 %shard_map.69 = f32[1024,1,128]{2,1,0:T(1,128)} custom-call(s32[1024]{0:T(1024)} %reshape.261.a_ref, s32[1024]{0:T(1024)} %reshape.262.b_ref, f32[4096,1,128]{2,1,0:T(1,128)} %bitcast.73), custom_call_target="tpu_custom_call" | custom-call | tf_op jit(solution)/shard_map/pallas_call | solution.py:36
  106.0 6.4 %all-to-all-start.1 = ((f32[1024,1,128]{2,1,0:T(1,128)}), f32[1024,1,128]{2,1,0:T(1,128)S(1)}, u32[]{:S(2)}, u32[]{:S(2)}) async-start(f32[1024,1,128]{2,1,0:T(1,128)} %shard_map.69), calls=%async_computation.1 | async-start | bytes 1048576 | tf_op jit(solution)/shard_map/all_to_all | solution.py:100
  114.9 4.0 %shard_map.71 = f32[1024,1,128]{2,1,0:T(1,128)} custom-call(s32[1024]{0:T(1024)} %reshape.268.a_ref, s32[1024]{0:T(1024)} %reshape.269.b_ref, f32[4096,1,128]{2,1,0:T(1,128)} %bitcast.74), custom_call_target="tpu_custom_call" | custom-call | tf_op jit(solution)/shard_map/pallas_call | solution.py:36
  119.0 10.7 %all-to-all-done.1 = f32[1024,1,128]{2,1,0:T(1,128)S(1)} async-done(((f32[1024,1,128]{2,1,0:T(1,128)}), f32[1024,1,128]{2,1,0:T(1,128)S(1)}, u32[]{:S(2)}, u32[]{:S(2)}) %all-to-all-start.1) | async-done | bytes 524320 | tf_op jit(solution)/shard_map/all_to_all | solution.py:100
  129.6 6.7 %all-to-all-start.2 = ((f32[1024,1,128]{2,1,0:T(1,128)}), f32[1024,1,128]{2,1,0:T(1,128)S(1)}, u32[]{:S(2)}, u32[]{:S(2)}) async-start(f32[1024,1,128]{2,1,0:T(1,128)} %shard_map.71), calls=%async_computation.2 | async-start | bytes 1048576 | tf_op jit(solution)/shard_map/all_to_all | solution.py:100
  137.4 5.0 %sort.46 = (s32[2048]{0:T(1024)}, s32[2048]{0:T(1024)S(1)}) sort(s32[2048]{0:T(1024)S(1)} %reshape.259, s32[2048]{0:T(1024)S(1)} %iota.22), dimensions={0}, to_apply=%region_1.2 | sort | flops 22528 | bytes 32768 | tf_op jit(solution)/shard_map/sort | solution.py:158
  142.4 5.0 %sort.47 = (s32[2048]{0:T(1024)}, s32[2048]{0:T(1024)S(1)}) sort(s32[2048]{0:T(1024)S(1)} %reshape.267, s32[2048]{0:T(1024)S(1)} %iota.23), dimensions={0}, to_apply=%region_2.3 | sort | flops 22528 | bytes 32768 | tf_op jit(solution)/shard_map/sort | solution.py:158
  150.3 2.4 all-to-all-done.2
  153.3 1.0 pad_maximum_fusion.5
  154.3 10.8 %shard_map.72 = f32[4096,1,128]{2,1,0:T(1,128)} custom-call(s32[2048]{0:T(1024)} %get-tuple-element.12.key_ref, s32[2048]{0:T(1024)} %get-tuple-element.48.slot_ref, s32[2048]{0:T(1024)} %get-tuple-element.47.side_ref, f32[1024,1,128]{2,1,0:T(1,128)} %bitcast.96), custom_call_target="tpu_custom_call" | custom-call | tf_op jit(solution)/shard_map/pallas_call | solution.py:80
  165.1 10.8 %shard_map.70 = f32[4096,1,128]{2,1,0:T(1,128)} custom-call(s32[2048]{0:T(1024)} %get-tuple-element.10.key_ref, s32[2048]{0:T(1024)} %get-tuple-element.50.slot_ref, s32[2048]{0:T(1024)} %get-tuple-element.49.side_ref, f32[1024,1,128]{2,1,0:T(1,128)} %bitcast.93), custom_call_target="tpu_custom_call" | custom-call | tf_op jit(solution)/shard_map/pallas_call | solution.py:80
  175.9 2.6 add_bitcast_fusion.1
  179.3 2.5 divide_add_fusion
  181.8 1.9 pad_maximum_fusion.2
  183.7 4.0 %shard_map.75 = f32[1024,1,128]{2,1,0:T(1,128)} custom-call(s32[1024]{0:T(1024)} %reshape.268.a_ref, s32[1024]{0:T(1024)} %reshape.269.b_ref, f32[4096,1,128]{2,1,0:T(1,128)} %bitcast.76), custom_call_target="tpu_custom_call" | custom-call | tf_op jit(solution)/shard_map/pallas_call | solution.py:36
  187.8 10.9 %all-to-all-start.4 = ((f32[1024,1,128]{2,1,0:T(1,128)}), f32[1024,1,128]{2,1,0:T(1,128)S(1)}, u32[]{:S(2)}, u32[]{:S(2)}) async-start(f32[1024,1,128]{2,1,0:T(1,128)} %shard_map.75), calls=%async_computation.4 | async-start | bytes 1048576 | tf_op jit(solution)/shard_map/all_to_all | solution.py:100
  198.7 4.1 %shard_map.73 = f32[1024,1,128]{2,1,0:T(1,128)} custom-call(s32[1024]{0:T(1024)} %reshape.261.a_ref, s32[1024]{0:T(1024)} %reshape.262.b_ref, f32[4096,1,128]{2,1,0:T(1,128)} %bitcast.77), custom_call_target="tpu_custom_call" | custom-call | tf_op jit(solution)/shard_map/pallas_call | solution.py:36
  202.8 11.6 %all-to-all-done.4 = f32[1024,1,128]{2,1,0:T(1,128)S(1)} async-done(((f32[1024,1,128]{2,1,0:T(1,128)}), f32[1024,1,128]{2,1,0:T(1,128)S(1)}, u32[]{:S(2)}, u32[]{:S(2)}) %all-to-all-start.4) | async-done | bytes 524320 | tf_op jit(solution)/shard_map/all_to_all | solution.py:100
  215.1 6.5 %all-to-all-start.3 = ((f32[1024,1,128]{2,1,0:T(1,128)}), f32[1024,1,128]{2,1,0:T(1,128)S(1)}, u32[]{:S(2)}, u32[]{:S(2)}) async-start(f32[1024,1,128]{2,1,0:T(1,128)} %shard_map.73), calls=%async_computation.3 | async-start | bytes 1048576 | tf_op jit(solution)/shard_map/all_to_all | solution.py:100
  222.4 1.8 fusion.12
  224.2 1.0 pad_maximum_fusion.7
  225.2 10.8 %shard_map.76 = f32[4096,1,128]{2,1,0:T(1,128)} custom-call(s32[2048]{0:T(1024)} %get-tuple-element.12.key_ref, s32[2048]{0:T(1024)} %get-tuple-element.48.slot_ref, s32[2048]{0:T(1024)} %get-tuple-element.47.side_ref, f32[1024,1,128]{2,1,0:T(1,128)} %bitcast.94), custom_call_target="tpu_custom_call" | custom-call | tf_op jit(solution)/shard_map/pallas_call | solution.py:80
  236.0 1.3 all-to-all-done.3
  238.9 10.8 %shard_map.74 = f32[4096,1,128]{2,1,0:T(1,128)} custom-call(s32[2048]{0:T(1024)} %get-tuple-element.10.key_ref, s32[2048]{0:T(1024)} %get-tuple-element.50.slot_ref, s32[2048]{0:T(1024)} %get-tuple-element.49.side_ref, f32[1024,1,128]{2,1,0:T(1,128)} %bitcast.95), custom_call_target="tpu_custom_call" | custom-call | tf_op jit(solution)/shard_map/pallas_call | solution.py:80
  249.7 2.6 add_bitcast_fusion
  253.2 3.3 %fusion.5 = f32[4096,64]{1,0:T(8,128)S(1)} fusion(f32[4096,128]{1,0:T(8,128)S(1)} %add_bitcast_fusion, f32[4096]{0:T(1024)S(1)} %copy-done.12, f32[4096]{0:T(1024)S(1)} %get-tuple-element.23, f32[4096,128]{1,0:T(8,128)S(1)} %add_bitcast_fusion.1, f32[4096,256]{1,0:T(8,128)S(1)} %bitcast.72), kind=kLoop, calls=%fused_computation.7 | loop fusion | flops 5242880 | bytes 7372800 | tf_op jit(solution)/shard_map/add | solution.py:188
  256.5 1.9 pad_maximum_fusion.3
  258.5 5.8 %shard_map.77 = f32[2048,1,128]{2,1,0:T(1,128)} custom-call(s32[2048]{0:T(1024)} %a_ref.1, s32[2048]{0:T(1024)} %convert_element_type.22.b_ref, f32[4096,1,128]{2,1,0:T(1,128)} %bitcast.88), custom_call_target="tpu_custom_call" | custom-call | tf_op jit(solution)/shard_map/pallas_call | solution.py:36
  264.3 1.7 slice.184
  267.0 12.5 %all-to-all-start.5 = ((f32[128,8,128]{2,1,0:T(8,128)}), f32[128,8,128]{2,1,0:T(8,128)}, u32[]{:S(2)}, u32[]{:S(2)}) async-start(f32[128,8,128]{2,1,0:T(8,128)} %all_to_all.26), calls=%async_computation.5 | async-start | bytes 1048576 | tf_op jit(solution)/shard_map/all_to_all | solution.py:100
  279.5 1.6 copy.78
  281.1 13.3 %all-to-all-done.5 = f32[128,8,128]{2,1,0:T(8,128)} async-done(((f32[128,8,128]{2,1,0:T(8,128)}), f32[128,8,128]{2,1,0:T(8,128)}, u32[]{:S(2)}, u32[]{:S(2)}) %all-to-all-start.5) | async-done | bytes 524320 | tf_op jit(solution)/shard_map/all_to_all | solution.py:100
  294.4 1.2 reshape.282
  296.0 9.7 %psum.7 = f32[2048]{0:T(1024)S(1)} all-reduce(f32[2048]{0:T(1024)S(1)} %broadcast_select_fusion), channel_id=1, replica_groups=mesh['dom'=128,'col'=2] {'col'}, use_global_device_ids=true, to_apply=%region_4.5 | all-reduce | flops 2048 | bytes 16384 | tf_op jit(solution)/shard_map/psum | solution.py:198
  (105 shorter events, 26.3 us)
Async XLA Ops:
  2.2 2.2 copy-start.19
  7.0 17.6 %copy-start.13 = (s32[2048]{0:T(1024)S(1)}, s32[2048]{0:T(1024)}, u32[]{:S(2)}) copy-start(s32[2048]{0:T(1024)} %a_ref.1) | copy-start | bytes 24580
  8.3 46.6 %all-to-all-start = ((f32[128,9,128]{2,1,0:T(8,128)}), f32[128,9,128]{2,1,0:T(8,128)S(1)}, u32[]{:S(2)}, u32[]{:S(2)}) async-start(f32[128,9,128]{2,1,0:T(8,128)} %maximum_maximum_fusion), calls=%async_computation | async-start | bytes 2097152 | tf_op jit(solution)/shard_map/all_to_all | solution.py:100
  96.9 1.9 copy-start
  98.6 79.8 %copy-start.11 = (f32[4096]{0:T(1024)}, f32[4096]{0:T(1024)S(1)}, u32[]{:S(2)}) copy-start(f32[4096]{0:T(1024)S(1)} %get-tuple-element.22) | copy-start | bytes 49156
  102.0 10.4 %copy-start.14 = (f32[2048]{0:T(1024)S(1)}, f32[2048]{0:T(1024)}, u32[]{:S(2)}) copy-start(f32[2048]{0:T(1024)} %param.7) | copy-start | bytes 24580
  102.0 11.4 %copy-start.21 = (s32[1,128]{1,0:T(1,128)S(1)}, s32[1,128]{1,0:T(1,128)}, u32[]{:S(2)}) copy-start(s32[1,128]{1,0:T(1,128)} %param.8) | copy-start | bytes 1540
  106.0 23.6 %all-to-all-start.1 = ((f32[1024,1,128]{2,1,0:T(1,128)}), f32[1024,1,128]{2,1,0:T(1,128)S(1)}, u32[]{:S(2)}, u32[]{:S(2)}) async-start(f32[1024,1,128]{2,1,0:T(1,128)} %shard_map.69), calls=%async_computation.1 | async-start | bytes 1048576 | tf_op jit(solution)/shard_map/all_to_all | solution.py:100
  113.7 39.0 %copy-start.17 = (f32[1024]{0:T(1024)}, f32[1024]{0:T(1024)S(1)}, u32[]{:S(2)}) copy-start(f32[1024]{0:T(1024)S(1)} %mul.173) | copy-start | bytes 12292
  113.8 34.9 %copy-start.15 = (f32[1024]{0:T(1024)}, f32[1024]{0:T(1024)S(1)}, u32[]{:S(2)}) copy-start(f32[1024]{0:T(1024)S(1)} %mul.167) | copy-start | bytes 12292
  119.0 29.7 %copy-start.6 = (f32[1024,1,128]{2,1,0:T(1,128)S(1)}, f32[1024,1,128]{2,1,0:T(1,128)}, u32[]{:S(2)}) copy-start(f32[1024,1,128]{2,1,0:T(1,128)} %shard_map.69) | copy-start | bytes 1572868
  129.6 23.0 %all-to-all-start.2 = ((f32[1024,1,128]{2,1,0:T(1,128)}), f32[1024,1,128]{2,1,0:T(1,128)S(1)}, u32[]{:S(2)}, u32[]{:S(2)}) async-start(f32[1024,1,128]{2,1,0:T(1,128)} %shard_map.71), calls=%async_computation.2 | async-start | bytes 1048576 | tf_op jit(solution)/shard_map/all_to_all | solution.py:100
  148.7 4.0 %copy-start.7 = (f32[1024,1,128]{2,1,0:T(1,128)S(1)}, f32[1024,1,128]{2,1,0:T(1,128)}, u32[]{:S(2)}) copy-start(f32[1024,1,128]{2,1,0:T(1,128)} %shard_map.71) | copy-start | bytes 1572868
  175.9 3.4 %copy-start.1 = (f32[4096,1,256]{2,0,1:T(8,128)S(1)}, f32[4096,1,256]{2,0,1:T(8,128)}, u32[]{:S(2)}) copy-start(f32[4096,1,256]{2,0,1:T(8,128)} %copy-done) | copy-start | bytes 12582916
  187.8 26.6 %all-to-all-start.4 = ((f32[1024,1,128]{2,1,0:T(1,128)}), f32[1024,1,128]{2,1,0:T(1,128)S(1)}, u32[]{:S(2)}, u32[]{:S(2)}) async-start(f32[1024,1,128]{2,1,0:T(1,128)} %shard_map.75), calls=%async_computation.4 | async-start | bytes 1048576 | tf_op jit(solution)/shard_map/all_to_all | solution.py:100
  198.7 23.7 %copy-start.9 = (f32[1024,1,128]{2,1,0:T(1,128)S(1)}, f32[1024,1,128]{2,1,0:T(1,128)}, u32[]{:S(2)}) copy-start(f32[1024,1,128]{2,1,0:T(1,128)} %shard_map.75) | copy-start | bytes 1572868
  198.7 23.7 %copy-start.18 = (f32[1024]{0:T(1024)S(1)}, f32[1024]{0:T(1024)}, u32[]{:S(2)}) copy-start(f32[1024]{0:T(1024)} %copy-done.17) | copy-start | bytes 12292
  214.3 0.8 copy-start.10
  215.1 22.2 %all-to-all-start.3 = ((f32[1024,1,128]{2,1,0:T(1,128)}), f32[1024,1,128]{2,1,0:T(1,128)S(1)}, u32[]{:S(2)}, u32[]{:S(2)}) async-start(f32[1024,1,128]{2,1,0:T(1,128)} %shard_map.73), calls=%async_computation.3 | async-start | bytes 1048576 | tf_op jit(solution)/shard_map/all_to_all | solution.py:100
  224.2 13.1 %copy-start.8 = (f32[1024,1,128]{2,1,0:T(1,128)S(1)}, f32[1024,1,128]{2,1,0:T(1,128)}, u32[]{:S(2)}) copy-start(f32[1024,1,128]{2,1,0:T(1,128)} %shard_map.73) | copy-start | bytes 1572868
  224.2 13.1 %copy-start.16 = (f32[1024]{0:T(1024)S(1)}, f32[1024]{0:T(1024)}, u32[]{:S(2)}) copy-start(f32[1024]{0:T(1024)} %copy-done.15) | copy-start | bytes 12292
  249.7 3.4 %copy-start.2 = (f32[4096,1,256]{2,0,1:T(8,128)S(1)}, f32[4096,1,256]{2,0,1:T(8,128)}, u32[]{:S(2)}) copy-start(f32[4096,1,256]{2,0,1:T(8,128)} %copy-done) | copy-start | bytes 12582916
  249.7 3.4 %copy-start.12 = (f32[4096]{0:T(1024)S(1)}, f32[4096]{0:T(1024)}, u32[]{:S(2)}) copy-start(f32[4096]{0:T(1024)} %copy-done.11) | copy-start | bytes 49156
  256.5 1.9 copy-start.3
  264.3 15.2 %copy-start.4 = (f32[4096,64]{1,0:T(8,128)S(1)}, f32[4096,64]{1,0:T(8,128)}, u32[]{:S(2)}) copy-start(f32[4096,64]{1,0:T(8,128)} %copy-done.3) | copy-start | bytes 3145732
  267.0 27.4 %all-to-all-start.5 = ((f32[128,8,128]{2,1,0:T(8,128)}), f32[128,8,128]{2,1,0:T(8,128)}, u32[]{:S(2)}, u32[]{:S(2)}) async-start(f32[128,8,128]{2,1,0:T(8,128)} %all_to_all.26), calls=%async_computation.5 | async-start | bytes 1048576 | tf_op jit(solution)/shard_map/all_to_all | solution.py:100
  279.5 16.2 %copy-start.5 = (f32[2048,1,128]{2,1,0:T(1,128)S(1)}, f32[2048,1,128]{2,1,0:T(1,128)}, u32[]{:S(2)}) copy-start(f32[2048,1,128]{2,1,0:T(1,128)} %shard_map.77) | copy-start | bytes 3145732
  281.1 15.0 %copy-start.20 = (pred[2048]{0:T(1024)(128)(4,1)S(1)}, pred[2048]{0:T(1024)(128)(4,1)}, u32[]{:S(2)}) copy-start(pred[2048]{0:T(1024)(128)(4,1)} %copy-done.19) | copy-start | bytes 6148

commit v6 on v4

--- a/solution.py
+++ b/solution.py
@@ -44,7 +44,7 @@
     )(a, b, x)
 
 
-def _sorted_scatter_kernel(half, key_ref, slot_ref, side_ref, v_ref, o_ref):
+def _runs_kernel(key_ref, slot_ref, v_ref, o_ref):
     lanes = o_ref.shape[2]
     step = 64
 
@@ -52,17 +52,14 @@
     def _(i):
         at = pl.ds(pl.multiple_of(i * step, step), step)
         o_ref[at] = jnp.zeros((step,) + o_ref.shape[1:], o_ref.dtype)
-    group = (lax.broadcasted_iota(jnp.int32, (1, lanes), 1) // half) % 2
 
     def body(t, carry):
         run, prev = carry
         base = t * BLOCK
         rows = [v_ref[slot_ref[base + r]] for r in range(BLOCK)]
         for r in range(BLOCK):
-            i = base + r
-            k = key_ref[i]
-            mine = jnp.where(group == side_ref[i], rows[r], jnp.zeros_like(rows[r]))
-            run = jnp.where(k == prev, run, jnp.zeros_like(run)) + mine
+            k = key_ref[base + r]
+            run = jnp.where(k == prev, run, jnp.zeros_like(run)) + rows[r]
             o_ref[k] = run
             prev = k
         return run, prev
@@ -75,18 +72,17 @@
     )
 
 
-def sorted_scatter(half, key, slot, side, vals, rows):
+def sorted_sum(key, slot, vals, rows):
     return pl.pallas_call(
-        functools.partial(_sorted_scatter_kernel, half),
+        _runs_kernel,
         out_shape=jax.ShapeDtypeStruct((rows,) + vals.shape[1:], vals.dtype),
         in_specs=[
-            pl.BlockSpec(memory_space=pltpu.SMEM),
             pl.BlockSpec(memory_space=pltpu.SMEM),
             pl.BlockSpec(memory_space=pltpu.SMEM),
             pl.BlockSpec(memory_space=pltpu.VMEM),
         ],
         out_specs=pl.BlockSpec(memory_space=pltpu.VMEM),
-    )(key, slot, side, vals)
+    )(key, slot, vals).reshape(rows, -1)
 
 
 def local(src_local, dst_local, edge_weight, send_counts, sketch):
@@ -102,6 +98,17 @@
     w_out = (edge_weight.reshape(peers, cap) * live).reshape(-1)
     root = jnp.sqrt(w_out)[:, None] * sketch.astype(jnp.float32).T
     lanes = 2 * width
+    ones = jnp.ones((1, width), jnp.float32)
+    slots = jnp.arange(edges, dtype=jnp.int32)
+
+    key_0, slot_0 = lax.sort((src_local, slots), num_keys=1)
+    own = sorted_sum(
+        key_0,
+        slot_0,
+        jnp.concatenate([root, w_out[:, None] * ones], axis=1).reshape(edges, 1, lanes),
+        VERT_DEV,
+    )
+
     side_row = jnp.concatenate(
         [
             w_out.reshape(peers, 1, cap),
@@ -116,26 +123,17 @@
     w_in = arrived[:, -1, :cap].reshape(-1)
     wanted = arrived[:, -1, cap:2 * cap].reshape(-1).astype(jnp.int32)
 
-    keys = jnp.stack([src_local, wanted], axis=1).reshape(-1)
-    key_s, entry_s = lax.sort(
-        (keys, jnp.arange(2 * edges, dtype=jnp.int32)), num_keys=1
+    key_1, slot_1 = lax.sort((wanted, slots), num_keys=1)
+    far = sorted_sum(
+        key_1,
+        slot_1,
+        jnp.concatenate([-arrived_root, w_in[:, None] * ones], axis=1).reshape(
+            edges, 1, lanes
+        ),
+        VERT_DEV,
     )
-    slot_s = entry_s // 2
-    side_s = entry_s % 2
-
-    def scatter(vals):
-        return sorted_scatter(width, key_s, slot_s, side_s, vals, VERT_DEV).reshape(
-            VERT_DEV, -1
-        )
-
-    ones = jnp.ones((1, width), jnp.float32)
-    acc = scatter(
-        jnp.concatenate(
-            [root, -arrived_root, w_out[:, None] * ones, w_in[:, None] * ones], axis=1
-        ).reshape(edges, 1, 2 * lanes)
-    )
-    rhs = acc[:, :width] + acc[:, width:lanes]
-    degree = acc[:, lanes] + acc[:, lanes + width]
+    rhs = own[:, :width] + far[:, :width]
+    degree = own[:, width] + far[:, width]
     diag = ((1.0 + degree_boost) * degree + ground_shift)[:, None]
     extra = (degree_boost * degree + ground_shift)[:, None]
 
@@ -150,8 +148,9 @@
         flow_out = w_out[:, None] * (here[:, :width] - there[:, width:])
         flow_in = w_in[:, None] * (there[:, :width] - here[:, width:])
         flows = jnp.concatenate([flow_out, -flow_in], axis=1).reshape(edges, 1, lanes)
-        acc = scatter(flows)
-        return (acc[:, :width] + acc[:, width:]) + extra * field
+        at_first = sorted_sum(key_0, slot_0, flows, VERT_DEV)
+        at_second = sorted_sum(key_1, slot_1, flows, VERT_DEV)
+        return (at_first[:, :width] + at_second[:, width:]) + extra * field
 
     sigma = 1.25
     delta = 0.8

time: 284 us -> 258 us (0.908)
  blocking collectives: 124 us -> 77.8 us
  starting transfers between devices: 7.29 us -> 23.6 us
  local copies, waits for them, and re-layouts: 24.3 us -> 9.21 us
  waiting for transfers between devices: 13.3 us -> 27.9 us
  other arithmetic: 38 us -> 45.5 us
  Pallas kernels: 75.4 us -> 71.6 us
    all_to_all x3 -> x2, blocking collectives: 114 us -> 68.1 us  [a2a(): return lax.all_to_all(x, 'dom', split_axis=0, concat_axis=0, tiled=True)]
    all_to_all x1 -> x2, starting transfers between devices: 7.29 us -> 23.6 us  [a2a(): return lax.all_to_all(x, 'dom', split_axis=0, concat_axis=0, tiled=True)]
    all_to_all x1 -> x2, waiting for transfers between devices: 13.3 us -> 27.9 us  [a2a(): return lax.all_to_all(x, 'dom', split_axis=0, concat_axis=0, tiled=True)]
    reshape x2 -> x0, local copies, waits for them, and re-layouts: 10.5 us -> none  [the longest x1 10 us: local(): acc = scatter(jnp.concatenate([root, -arrived_root, w_out[:, None] * ones...]
    sort x1 -> x2, other arithmetic: 5.77 us -> 10.1 us  [the longest x1 5.05 us: local(): key_0, slot_0 = lax.sort((src_local, slots), num_keys=1)]
    pallas_call x3 -> x6, Pallas kernels: 58 us -> 54.2 us  [sorted_sum(): pl.pallas_call(_runs_kernel, out_shape=jax.ShapeDtypeStruct((rows,) + val...]
  transfers between devices with their start and end apart: 1 -> 2, of which waited for: 1 -> 2; matrix products, arithmetic and copies ran while one was open for 1% -> 3% of each run, Pallas kernels for 0% -> 3%
where the time goes in v6:
time: 258 us; the launch traced here: 256 us
  blocking collectives  77.8 us (30%)
  Pallas kernels  71.6 us (28%)
  other arithmetic  45.5 us (18%)
  waiting for transfers between devices  27.9 us (11%)
  starting transfers between devices  23.6 us (9%)
  local copies, waits for them, and re-layouts  9.21 us (4%)
    all_to_all x2, blocking collectives, a2a(): return lax.all_to_all(x, 'dom', split_axis=0, concat_axis=0, tiled=True)  68.1 us
    pallas_call x6, Pallas kernels, sorted_sum(): pl.pallas_call(_runs_kernel, out_shape=jax.ShapeDtypeStruct((rows,) + val...  54.2 us
    all_to_all x2, waiting for transfers between devices, a2a(): return lax.all_to_all(x, 'dom', split_axis=0, concat_axis=0, tiled=True)  27.9 us
    all_to_all x2, starting transfers between devices, a2a(): return lax.all_to_all(x, 'dom', split_axis=0, concat_axis=0, tiled=True)  23.6 us
    pallas_call x3, Pallas kernels, pair_gather(): pl.pallas_call(_pair_gather_kernel, out_shape=jax.ShapeDtypeStruct((a.sha...  17.4 us
    psum x1, blocking collectives, local(): resistance = lax.psum(partial_sum, 'col') / SKETCH  9.66 us
    add x1, other arithmetic, local(): solution = solution + direction  6.17 us
    concatenate x3, other arithmetic, ends(): jnp.concatenate([field, field], axis=1).reshape(VERT_DEV, 1, 2 * width)  5.94 us
  transfers between devices with their start and end apart: 2, of which 2 were waited for; matrix products, arithmetic and copies ran while one was open for 3% of the time, Pallas kernels for 3%

profile of v6, /device:TPU:1, one launch (start us, length us, event | category | flops | bytes accessed | tf_op | source)
XLA Modules:
  0.0 256.5 jit_solution(12020113525687970293)
XLA Ops:
  0.6 0.7 convert_element_type.14
  1.3 0.7 iota_compare_fusion
  2.2 0.8 reshape.151
  3.0 0.7 fusion.17
  3.7 0.9 compare_select_fusion
  4.6 1.2 copy.39
  5.8 0.3 multiply_bitcast_fusion
  6.5 1.2 maximum_maximum_fusion
  7.7 16.3 %all-to-all-start = ((f32[128,9,128]{2,1,0:T(8,128)}), f32[128,9,128]{2,1,0:T(8,128)S(1)}, u32[]{:S(2)}, u32[]{:S(2)}) async-start(f32[128,9,128]{2,1,0:T(8,128)} %maximum_maximum_fusion), calls=%async_computation | async-start | bytes 2097152 | tf_op jit(solution)/shard_map/all_to_all | solution.py:95
  24.0 5.1 %sort.30 = (s32[2048]{0:T(1024)}, s32[2048]{0:T(1024)}) sort(s32[2048]{0:T(1024)S(1)} %copy-done.9, s32[2048]{0:T(1024)S(1)} %iota.14), dimensions={0}, to_apply=%region_0.0 | sort | flops 22528 | bytes 32768 | tf_op jit(solution)/shard_map/sort | solution.py:104
  29.1 0.3 mul.116
  29.4 1.3 pad_maximum_fusion.3
  30.8 9.0 %shard_map.68 = f32[4096,1,128]{2,1,0:T(1,128)} custom-call(s32[2048]{0:T(1024)} %get-tuple-element.6.key_ref, s32[2048]{0:T(1024)} %get-tuple-element.7.slot_ref, f32[2048,1,128]{2,1,0:T(1,128)} %bitcast.62), custom_call_target="tpu_custom_call" | custom-call | tf_op jit(solution)/shard_map/pallas_call | solution.py:76
  39.7 14.5 %all-to-all-done = f32[128,9,128]{2,1,0:T(8,128)S(1)} async-done(((f32[128,9,128]{2,1,0:T(8,128)}), f32[128,9,128]{2,1,0:T(8,128)S(1)}, u32[]{:S(2)}, u32[]{:S(2)}) %all-to-all-start) | async-done | bytes 589856 | tf_op jit(solution)/shard_map/all_to_all | solution.py:95
  54.5 0.3 fusion.16
  55.1 5.0 %sort.31 = (s32[2048]{0:T(1024)}, s32[2048]{0:T(1024)}) sort(s32[2048]{0:T(1024)S(1)} %convert_element_type.16.b_ref, s32[2048]{0:T(1024)S(1)} %iota.15), dimensions={0}, to_apply=%region_1.0 | sort | flops 22528 | bytes 32768 | tf_op jit(solution)/shard_map/sort | solution.py:126
  60.2 0.3 mul.119
  60.5 1.3 pad_maximum_fusion.4
  61.8 9.2 %shard_map.69 = f32[4096,1,128]{2,1,0:T(1,128)} custom-call(s32[2048]{0:T(1024)} %get-tuple-element.8.key_ref, s32[2048]{0:T(1024)} %get-tuple-element.9.slot_ref, f32[2048,1,128]{2,1,0:T(1,128)} %bitcast.63), custom_call_target="tpu_custom_call" | custom-call | tf_op jit(solution)/shard_map/pallas_call | solution.py:76
  71.0 4.0 %add_reduce_fusion = (f32[4096]{0:T(1024)S(1)}, f32[4096]{0:T(1024)S(1)}) fusion(f32[4096,128]{1,0:T(8,128)} %bitcast.38, f32[4096,128]{1,0:T(8,128)S(1)} %bitcast.34), kind=kLoop, calls=%fused_computation.16 | loop fusion | flops 20480 | bytes 65536 | tf_op jit(solution)/shard_map/add | solution.py:138
  75.0 0.7 broadcast_divide_fusion
  75.8 2.0 pad_maximum_fusion
  77.8 5.8 %shard_map.70 = f32[2048,1,128]{2,1,0:T(1,128)} custom-call(s32[2048]{0:T(1024)} %a_ref.5, s32[2048]{0:T(1024)} %copy-done.8, f32[4096,1,128]{2,1,0:T(1,128)} %bitcast.59), custom_call_target="tpu_custom_call" | custom-call | tf_op jit(solution)/shard_map/pallas_call | solution.py:35
  83.6 35.0 %all_to_all.24 = f32[2048,1,128]{2,1,0:T(1,128)S(1)} all-to-all(f32[2048,1,128]{2,1,0:T(1,128)} %shard_map.70), channel_id=1, replica_groups=mesh['dom'=128,'col'=2] {'dom'}, dimensions={0} | all-to-all | bytes 2097152 | tf_op jit(solution)/shard_map/all_to_all | solution.py:95
  118.6 1.2 fusion.15
  119.9 1.3 pad_maximum_fusion.5
  121.2 9.0 %shard_map.72 = f32[4096,1,128]{2,1,0:T(1,128)} custom-call(s32[2048]{0:T(1024)} %get-tuple-element.8.key_ref, s32[2048]{0:T(1024)} %get-tuple-element.9.slot_ref, f32[2048,1,128]{2,1,0:T(1,128)} %bitcast.51), custom_call_target="tpu_custom_call" | custom-call | tf_op jit(solution)/shard_map/pallas_call | solution.py:76
  130.2 9.0 %shard_map.71 = f32[4096,1,128]{2,1,0:T(1,128)} custom-call(s32[2048]{0:T(1024)} %get-tuple-element.6.key_ref, s32[2048]{0:T(1024)} %get-tuple-element.7.slot_ref, f32[2048,1,128]{2,1,0:T(1,128)} %bitcast.52), custom_call_target="tpu_custom_call" | custom-call | tf_op jit(solution)/shard_map/pallas_call | solution.py:76
  139.2 5.0 %divide_add_fusion = f32[4096,64]{1,0:T(8,128)S(1)} fusion(f32[4096,64]{1,0:T(8,128)} %copy-done.2, f32[4096]{0:T(1024)S(1)} %get-tuple-element.19, f32[4096]{0:T(1024)S(1)} %get-tuple-element.18, f32[4096,128]{1,0:T(8,128)} %bitcast.43, f32[4096,128]{1,0:T(8,128)} %bitcast.45, f32[4096,128]{1,0:T(8,128)} %bitcast.39, f32[4096,128]{1,0:T(8,128)S(1)} %bitcast.36), kind=kLoop, calls=%fused_computation.15 | loop fusion | flops 2359296 | bytes 6324224 | tf_op jit(solution)/shard_map/add | solution.py:166
  144.2 2.0 pad_maximum_fusion.1
  146.2 5.8 %shard_map.73 = f32[2048,1,128]{2,1,0:T(1,128)} custom-call(s32[2048]{0:T(1024)} %a_ref.5, s32[2048]{0:T(1024)} %copy-done.8, f32[4096,1,128]{2,1,0:T(1,128)} %bitcast.57), custom_call_target="tpu_custom_call" | custom-call | tf_op jit(solution)/shard_map/pallas_call | solution.py:35
  152.1 33.1 %all_to_all.25 = f32[2048,1,128]{2,1,0:T(1,128)S(1)} all-to-all(f32[2048,1,128]{2,1,0:T(1,128)} %shard_map.73), channel_id=1, replica_groups=mesh['dom'=128,'col'=2] {'dom'}, dimensions={0} | all-to-all | bytes 2097152 | tf_op jit(solution)/shard_map/all_to_all | solution.py:95
  185.1 1.2 fusion.12
  186.4 1.3 pad_maximum_fusion.6
  187.7 9.1 %shard_map.75 = f32[4096,1,128]{2,1,0:T(1,128)} custom-call(s32[2048]{0:T(1024)} %get-tuple-element.8.key_ref, s32[2048]{0:T(1024)} %get-tuple-element.9.slot_ref, f32[2048,1,128]{2,1,0:T(1,128)} %bitcast.49), custom_call_target="tpu_custom_call" | custom-call | tf_op jit(solution)/shard_map/pallas_call | solution.py:76
  196.7 9.0 %shard_map.74 = f32[4096,1,128]{2,1,0:T(1,128)} custom-call(s32[2048]{0:T(1024)} %get-tuple-element.6.key_ref, s32[2048]{0:T(1024)} %get-tuple-element.7.slot_ref, f32[2048,1,128]{2,1,0:T(1,128)} %bitcast.50), custom_call_target="tpu_custom_call" | custom-call | tf_op jit(solution)/shard_map/pallas_call | solution.py:76
  205.7 6.2 %fusion.5 = f32[4096,64]{1,0:T(8,128)S(1)} fusion(f32[4096,128]{1,0:T(8,128)} %bitcast.60, f32[4096,128]{1,0:T(8,128)} %bitcast.61, f32[4096,64]{1,0:T(8,128)} %copy-done.2, f32[4096]{0:T(1024)S(1)} %get-tuple-element.18, f32[4096]{0:T(1024)S(1)} %get-tuple-element.19, f32[4096,128]{1,0:T(8,128)} %bitcast.44, f32[4096,128]{1,0:T(8,128)} %bitcast.46, ...), kind=kLoop, calls=%fused_computation.6 | loop fusion | flops 4980736 | bytes 8421376 | tf_op jit(solution)/shard_map/add | solution.py:162
  211.9 1.9 pad_maximum_fusion.2
  213.8 5.8 %shard_map.76 = f32[2048,1,128]{2,1,0:T(1,128)} custom-call(s32[2048]{0:T(1024)} %a_ref.5, s32[2048]{0:T(1024)} %copy-done.8, f32[4096,1,128]{2,1,0:T(1,128)} %bitcast.58), custom_call_target="tpu_custom_call" | custom-call | tf_op jit(solution)/shard_map/pallas_call | solution.py:35
  219.6 1.7 slice.104
  221.3 1.0 all_to_all.18
  222.3 7.3 %all-to-all-start.3 = ((f32[128,8,128]{2,1,0:T(8,128)}), f32[128,8,128]{2,1,0:T(8,128)}, u32[]{:S(2)}, u32[]{:S(2)}) async-start(f32[128,8,128]{2,1,0:T(8,128)} %all_to_all.18), calls=%async_computation.3 | async-start | bytes 1048576 | tf_op jit(solution)/shard_map/all_to_all | solution.py:95
  229.7 1.6 copy.49
  231.2 13.3 %all-to-all-done.3 = f32[128,8,128]{2,1,0:T(8,128)} async-done(((f32[128,8,128]{2,1,0:T(8,128)}), f32[128,8,128]{2,1,0:T(8,128)}, u32[]{:S(2)}, u32[]{:S(2)}) %all-to-all-start.3) | async-done | bytes 524320 | tf_op jit(solution)/shard_map/all_to_all | solution.py:95
  244.6 1.2 reshape.169
  245.8 0.3 fusion.9
  246.2 9.7 %psum.7 = f32[2048]{0:T(1024)S(1)} all-reduce(f32[2048]{0:T(1024)S(1)} %broadcast_select_fusion), channel_id=1, replica_groups=mesh['dom'=128,'col'=2] {'col'}, use_global_device_ids=true, to_apply=%region_3.0 | all-reduce | flops 2048 | bytes 16384 | tf_op jit(solution)/shard_map/psum | solution.py:172
  255.9 0.6 broadcast_multiply_fusion
  (33 shorter events, 1.1 us)
Async XLA Ops:
  6.4 17.6 %copy-start.9 = (s32[2048]{0:T(1024)S(1)}, s32[2048]{0:T(1024)}, u32[]{:S(2)}) copy-start(s32[2048]{0:T(1024)} %a_ref.5) | copy-start | bytes 24580
  7.7 46.6 %all-to-all-start = ((f32[128,9,128]{2,1,0:T(8,128)}), f32[128,9,128]{2,1,0:T(8,128)S(1)}, u32[]{:S(2)}, u32[]{:S(2)}) async-start(f32[128,9,128]{2,1,0:T(8,128)} %maximum_maximum_fusion), calls=%async_computation | async-start | bytes 2097152 | tf_op jit(solution)/shard_map/all_to_all | solution.py:95
  54.9 7.0 %copy-start.8 = (s32[2048]{0:T(1024)}, s32[2048]{0:T(1024)S(1)}, u32[]{:S(2)}) copy-start(s32[2048]{0:T(1024)S(1)} %convert_element_type.16.b_ref) | copy-start | bytes 24580
  61.8 9.2 %copy-start = (f32[4096,1,128]{2,1,0:T(1,128)S(1)}, f32[4096,1,128]{2,1,0:T(1,128)}, u32[]{:S(2)}) copy-start(f32[4096,1,128]{2,1,0:T(1,128)} %shard_map.68) | copy-start | bytes 6291460
  71.0 4.0 %copy-start.1 = (f32[4096,1,128]{2,1,0:T(1,128)S(1)}, f32[4096,1,128]{2,1,0:T(1,128)}, u32[]{:S(2)}) copy-start(f32[4096,1,128]{2,1,0:T(1,128)} %shard_map.69) | copy-start | bytes 6291460
  75.7 2.0 copy-start.2
  83.6 35.1 %copy-start.6 = (f32[2048,1,128]{2,1,0:T(1,128)S(1)}, f32[2048,1,128]{2,1,0:T(1,128)}, u32[]{:S(2)}) copy-start(f32[2048,1,128]{2,1,0:T(1,128)} %shard_map.70) | copy-start | bytes 3145732
  152.1 33.1 %copy-start.5 = (f32[2048,1,128]{2,1,0:T(1,128)S(1)}, f32[2048,1,128]{2,1,0:T(1,128)}, u32[]{:S(2)}) copy-start(f32[2048,1,128]{2,1,0:T(1,128)} %shard_map.73) | copy-start | bytes 3145732
  211.9 1.9 copy-start.3
  219.6 10.0 %copy-start.4 = (f32[4096,64]{1,0:T(8,128)S(1)}, f32[4096,64]{1,0:T(8,128)}, u32[]{:S(2)}) copy-start(f32[4096,64]{1,0:T(8,128)} %copy-done.3) | copy-start | bytes 3145732
  222.3 22.2 %all-to-all-start.3 = ((f32[128,8,128]{2,1,0:T(8,128)}), f32[128,8,128]{2,1,0:T(8,128)}, u32[]{:S(2)}, u32[]{:S(2)}) async-start(f32[128,8,128]{2,1,0:T(8,128)} %all_to_all.18), calls=%async_computation.3 | async-start | bytes 1048576 | tf_op jit(solution)/shard_map/all_to_all | solution.py:95
  229.7 16.2 %copy-start.7 = (f32[2048,1,128]{2,1,0:T(1,128)S(1)}, f32[2048,1,128]{2,1,0:T(1,128)}, u32[]{:S(2)}) copy-start(f32[2048,1,128]{2,1,0:T(1,128)} %shard_map.76) | copy-start | bytes 3145732

commit v7 on v6

--- a/solution.py
+++ b/solution.py
@@ -165,9 +165,10 @@
             newer = 1.0 / (2.0 * sigma - coeff)
             direction = newer * coeff * direction + 2.0 * newer / delta * resid / diag
             coeff = newer
-    here = ends(solution).reshape(edges, 2 * width)
-    far = a2a(here[:, width:].reshape(edges // 2, 2 * width)).reshape(edges, width)
-    diff = here[:, :width] - far
+    doubled = jnp.concatenate([solution, solution], axis=1).reshape(VERT_DEV, 1, lanes)
+    far = a2a(pair_gather(wanted[0::2], wanted[1::2], doubled)).reshape(edges, width)
+    near = pair_gather(src_local[0::2], src_local[1::2], doubled).reshape(edges, width)
+    diff = near - far
     partial_sum = jnp.sum(diff * diff, axis=1) * live.reshape(-1)
     resistance = lax.psum(partial_sum, "col") / SKETCH
     return (solution.T, resistance)

time: 258 us -> 255 us (0.988)
  blocking collectives: 77.8 us -> 44.6 us
  waiting for transfers between devices: 27.9 us -> 47 us
  starting transfers between devices: 23.6 us -> 30.3 us
  other arithmetic: 45.5 us -> 48.3 us
    all_to_all x2 -> x1, blocking collectives: 68.1 us -> 35 us  [a2a(): return lax.all_to_all(x, 'dom', split_axis=0, concat_axis=0, tiled=True)]
    all_to_all x2 -> x3, waiting for transfers between devices: 27.9 us -> 47 us  [a2a(): return lax.all_to_all(x, 'dom', split_axis=0, concat_axis=0, tiled=True)]
    all_to_all x2 -> x3, starting transfers between devices: 23.6 us -> 30.3 us  [a2a(): return lax.all_to_all(x, 'dom', split_axis=0, concat_axis=0, tiled=True)]
    pallas_call x3 -> x4, Pallas kernels: 17.4 us -> 19.8 us  [pair_gather(): pl.pallas_call(_pair_gather_kernel, out_shape=jax.ShapeDtypeStruct((a.sha...]
    concatenate x3 -> x2, other arithmetic: 5.94 us -> 4.03 us  [ends(): jnp.concatenate([field, field], axis=1).reshape(VERT_DEV, 1, 2 * width)]
  transfers between devices with their start and end apart: 2 -> 3, of which waited for: 2 -> 3; matrix products, arithmetic and copies ran while one was open for 3% -> 5% of each run, Pallas kernels for 3% -> 5%
where the time goes in v7:
time: 255 us; the launch traced here: 254 us
  Pallas kernels  73.8 us (29%)
  other arithmetic  48.3 us (19%)
  waiting for transfers between devices  47 us (18%)
  blocking collectives  44.6 us (17%)
  starting transfers between devices  30.3 us (12%)
  local copies, waits for them, and re-layouts  8.65 us (3%)
    pallas_call x6, Pallas kernels, sorted_sum(): pl.pallas_call(_runs_kernel, out_shape=jax.ShapeDtypeStruct((rows,) + val...  54 us
    all_to_all x3, waiting for transfers between devices, a2a(): return lax.all_to_all(x, 'dom', split_axis=0, concat_axis=0, tiled=True)  47 us
    all_to_all x1, blocking collectives, a2a(): return lax.all_to_all(x, 'dom', split_axis=0, concat_axis=0, tiled=True)  35 us
    all_to_all x3, starting transfers between devices, a2a(): return lax.all_to_all(x, 'dom', split_axis=0, concat_axis=0, tiled=True)  30.3 us
    pallas_call x4, Pallas kernels, pair_gather(): pl.pallas_call(_pair_gather_kernel, out_shape=jax.ShapeDtypeStruct((a.sha...  19.8 us
    psum x1, blocking collectives, local(): resistance = lax.psum(partial_sum, 'col') / SKETCH  9.53 us
    add x1, other arithmetic, local(): solution = solution + direction  6.18 us
  transfers between devices with their start and end apart: 3, of which 3 were waited for; matrix products, arithmetic and copies ran while one was open for 5% of the time, Pallas kernels for 5%

profile of v7, /device:TPU:1, one launch (start us, length us, event | category | flops | bytes accessed | tf_op | source)
XLA Modules:
  0.0 253.6 jit_solution(8197036457074064136)
XLA Ops:
  0.6 0.8 iota_compare_fusion
  1.6 0.8 reshape.144
  2.3 0.7 fusion.15
  3.0 1.2 copy.39
  4.3 0.3 multiply_bitcast_fusion
  5.3 1.2 maximum_maximum_fusion
  6.4 16.3 %all-to-all-start = ((f32[128,9,128]{2,1,0:T(8,128)}), f32[128,9,128]{2,1,0:T(8,128)S(1)}, u32[]{:S(2)}, u32[]{:S(2)}) async-start(f32[128,9,128]{2,1,0:T(8,128)} %maximum_maximum_fusion), calls=%async_computation | async-start | bytes 2097152 | tf_op jit(solution)/shard_map/all_to_all | solution.py:95
  22.8 5.0 %sort.30 = (s32[2048]{0:T(1024)}, s32[2048]{0:T(1024)}) sort(s32[2048]{0:T(1024)S(1)} %copy-done.9, s32[2048]{0:T(1024)S(1)} %iota.14), dimensions={0}, to_apply=%region_0.0 | sort | flops 22528 | bytes 32768 | tf_op jit(solution)/shard_map/sort | solution.py:104
  28.2 1.3 pad_maximum_fusion.3
  29.5 9.0 %shard_map.68 = f32[4096,1,128]{2,1,0:T(1,128)} custom-call(s32[2048]{0:T(1024)} %get-tuple-element.6.key_ref, s32[2048]{0:T(1024)} %get-tuple-element.7.slot_ref, f32[2048,1,128]{2,1,0:T(1,128)} %bitcast.60), custom_call_target="tpu_custom_call" | custom-call | tf_op jit(solution)/shard_map/pallas_call | solution.py:76
  38.5 14.6 %all-to-all-done = f32[128,9,128]{2,1,0:T(8,128)S(1)} async-done(((f32[128,9,128]{2,1,0:T(8,128)}), f32[128,9,128]{2,1,0:T(8,128)S(1)}, u32[]{:S(2)}, u32[]{:S(2)}) %all-to-all-start) | async-done | bytes 589856 | tf_op jit(solution)/shard_map/all_to_all | solution.py:95
  53.9 0.3 mul.122
  54.2 1.3 pad_maximum_fusion.4
  55.5 5.0 %sort.31 = (s32[2048]{0:T(1024)}, s32[2048]{0:T(1024)}) sort(s32[2048]{0:T(1024)S(1)} %convert_element_type.16.b_ref, s32[2048]{0:T(1024)S(1)} %iota.15), dimensions={0}, to_apply=%region_1.0 | sort | flops 22528 | bytes 32768 | tf_op jit(solution)/shard_map/sort | solution.py:126
  60.6 9.0 %shard_map.69 = f32[4096,1,128]{2,1,0:T(1,128)} custom-call(s32[2048]{0:T(1024)} %get-tuple-element.8.key_ref, s32[2048]{0:T(1024)} %get-tuple-element.9.slot_ref, f32[2048,1,128]{2,1,0:T(1,128)} %bitcast.59), custom_call_target="tpu_custom_call" | custom-call | tf_op jit(solution)/shard_map/pallas_call | solution.py:76
  69.6 4.0 %add_reduce_fusion = (f32[4096]{0:T(1024)S(1)}, f32[4096]{0:T(1024)S(1)}) fusion(f32[4096,128]{1,0:T(8,128)} %bitcast.37, f32[4096,128]{1,0:T(8,128)S(1)} %bitcast.33), kind=kLoop, calls=%fused_computation.16 | loop fusion | flops 20480 | bytes 65536 | tf_op jit(solution)/shard_map/add | solution.py:138
  73.6 0.7 broadcast_divide_fusion
  74.3 2.0 pad_maximum_fusion
  76.4 5.8 %shard_map.70 = f32[2048,1,128]{2,1,0:T(1,128)} custom-call(s32[2048]{0:T(1024)} %a_ref.3, s32[2048]{0:T(1024)} %copy-done.7, f32[4096,1,128]{2,1,0:T(1,128)} %bitcast.56), custom_call_target="tpu_custom_call" | custom-call | tf_op jit(solution)/shard_map/pallas_call | solution.py:35
  82.2 35.0 %all_to_all.20 = f32[2048,1,128]{2,1,0:T(1,128)S(1)} all-to-all(f32[2048,1,128]{2,1,0:T(1,128)} %shard_map.70), channel_id=1, replica_groups=mesh['dom'=128,'col'=2] {'dom'}, dimensions={0} | all-to-all | bytes 2097152 | tf_op jit(solution)/shard_map/all_to_all | solution.py:95
  117.2 1.2 fusion.13
  118.5 1.3 pad_maximum_fusion.5
  119.8 9.0 %shard_map.71 = f32[4096,1,128]{2,1,0:T(1,128)} custom-call(s32[2048]{0:T(1024)} %get-tuple-element.6.key_ref, s32[2048]{0:T(1024)} %get-tuple-element.7.slot_ref, f32[2048,1,128]{2,1,0:T(1,128)} %bitcast.52), custom_call_target="tpu_custom_call" | custom-call | tf_op jit(solution)/shard_map/pallas_call | solution.py:76
  128.8 9.0 %shard_map.72 = f32[4096,1,128]{2,1,0:T(1,128)} custom-call(s32[2048]{0:T(1024)} %get-tuple-element.8.key_ref, s32[2048]{0:T(1024)} %get-tuple-element.9.slot_ref, f32[2048,1,128]{2,1,0:T(1,128)} %bitcast.53), custom_call_target="tpu_custom_call" | custom-call | tf_op jit(solution)/shard_map/pallas_call | solution.py:76
  137.8 5.0 %divide_add_fusion = f32[4096,64]{1,0:T(8,128)S(1)} fusion(f32[4096,64]{1,0:T(8,128)} %copy-done.2, f32[4096]{0:T(1024)S(1)} %get-tuple-element.19, f32[4096]{0:T(1024)S(1)} %get-tuple-element.18, f32[4096,128]{1,0:T(8,128)} %bitcast.46, f32[4096,128]{1,0:T(8,128)} %bitcast.44, f32[4096,128]{1,0:T(8,128)} %bitcast.38, f32[4096,128]{1,0:T(8,128)S(1)} %bitcast.35), kind=kLoop, calls=%fused_computation.15 | loop fusion | flops 2359296 | bytes 6324224 | tf_op jit(solution)/shard_map/add | solution.py:166
  142.8 2.0 pad_maximum_fusion.1
  144.8 5.8 %shard_map.73 = f32[2048,1,128]{2,1,0:T(1,128)} custom-call(s32[2048]{0:T(1024)} %a_ref.3, s32[2048]{0:T(1024)} %copy-done.7, f32[4096,1,128]{2,1,0:T(1,128)} %bitcast.55), custom_call_target="tpu_custom_call" | custom-call | tf_op jit(solution)/shard_map/pallas_call | solution.py:35
  150.7 7.4 %all-to-all-start.2 = ((f32[2048,1,128]{2,1,0:T(1,128)}), f32[2048,1,128]{2,1,0:T(1,128)}, u32[]{:S(2)}, u32[]{:S(2)}) async-start(f32[2048,1,128]{2,1,0:T(1,128)} %shard_map.73), calls=%async_computation.2 | async-start | bytes 2097152 | tf_op jit(solution)/shard_map/all_to_all | solution.py:95
  158.1 0.8 slice.90.a_ref
  158.9 0.8 slice.91.b_ref
  159.7 24.5 %all-to-all-done.2 = f32[2048,1,128]{2,1,0:T(1,128)} async-done(((f32[2048,1,128]{2,1,0:T(1,128)}), f32[2048,1,128]{2,1,0:T(1,128)}, u32[]{:S(2)}, u32[]{:S(2)}) %all-to-all-start.2) | async-done | bytes 1048608 | tf_op jit(solution)/shard_map/all_to_all | solution.py:95
  184.2 2.7 %fusion.10 = (f32[2048,64]{1,0:T(8,128)S(1)}, f32[2048,64]{1,0:T(8,128)S(1)}) fusion(f32[2048,128]{1,0:T(8,128)} %bitcast.22, f32[2048,128]{1,0:T(8,128)S(1)} %bitcast.48, f32[2048]{0:T(1024)S(1)} %get-tuple-element.21, f32[2048]{0:T(1024)S(1)} %mul.121), kind=kLoop, calls=%fused_computation.22 | loop fusion | flops 655360 | bytes 3162112 | tf_op jit(solution)/shard_map/mul | solution.py:148
  187.0 1.3 pad_maximum_fusion.6
  188.3 9.1 %shard_map.74 = f32[4096,1,128]{2,1,0:T(1,128)} custom-call(s32[2048]{0:T(1024)} %get-tuple-element.6.key_ref, s32[2048]{0:T(1024)} %get-tuple-element.7.slot_ref, f32[2048,1,128]{2,1,0:T(1,128)} %bitcast.50), custom_call_target="tpu_custom_call" | custom-call | tf_op jit(solution)/shard_map/pallas_call | solution.py:76
  197.3 9.0 %shard_map.75 = f32[4096,1,128]{2,1,0:T(1,128)} custom-call(s32[2048]{0:T(1024)} %get-tuple-element.8.key_ref, s32[2048]{0:T(1024)} %get-tuple-element.9.slot_ref, f32[2048,1,128]{2,1,0:T(1,128)} %bitcast.51), custom_call_target="tpu_custom_call" | custom-call | tf_op jit(solution)/shard_map/pallas_call | solution.py:76
  206.3 6.2 %fusion.5 = f32[4096,64]{1,0:T(8,128)S(1)} fusion(f32[4096,128]{1,0:T(8,128)} %bitcast.58, f32[4096,128]{1,0:T(8,128)} %bitcast.57, f32[4096,64]{1,0:T(8,128)} %copy-done.2, f32[4096]{0:T(1024)S(1)} %get-tuple-element.18, f32[4096]{0:T(1024)S(1)} %get-tuple-element.19, f32[4096,128]{1,0:T(8,128)} %bitcast.47, f32[4096,128]{1,0:T(8,128)} %bitcast.45, ...), kind=kLoop, calls=%fused_computation.6 | loop fusion | flops 4980736 | bytes 8421376 | tf_op jit(solution)/shard_map/add | solution.py:162
  212.5 2.0 pad_maximum_fusion.2
  214.5 4.2 %shard_map.77 = f32[1024,1,128]{2,1,0:T(1,128)} custom-call(s32[1024]{0:T(1024)} %slice.90.a_ref, s32[1024]{0:T(1024)} %slice.91.b_ref, f32[4096,1,128]{2,1,0:T(1,128)} %bitcast.41), custom_call_target="tpu_custom_call" | custom-call | tf_op jit(solution)/shard_map/pallas_call | solution.py:35
  218.6 6.5 %all-to-all-start.3 = ((f32[1024,1,128]{2,1,0:T(1,128)}), f32[1024,1,128]{2,1,0:T(1,128)S(1)}, u32[]{:S(2)}, u32[]{:S(2)}) async-start(f32[1024,1,128]{2,1,0:T(1,128)} %shard_map.77), calls=%async_computation.3 | async-start | bytes 1048576 | tf_op jit(solution)/shard_map/all_to_all | solution.py:95
  225.2 0.8 slice.88.a_ref
  226.0 0.8 slice.89.b_ref
  226.8 1.6 copy.49
  228.3 4.0 %shard_map.76 = f32[1024,1,128]{2,1,0:T(1,128)} custom-call(s32[1024]{0:T(1024)} %slice.88.a_ref, s32[1024]{0:T(1024)} %slice.89.b_ref, f32[4096,1,128]{2,1,0:T(1,128)} %bitcast.42), custom_call_target="tpu_custom_call" | custom-call | tf_op jit(solution)/shard_map/pallas_call | solution.py:35
  232.3 7.9 %all-to-all-done.3 = f32[1024,1,128]{2,1,0:T(1,128)S(1)} async-done(((f32[1024,1,128]{2,1,0:T(1,128)}), f32[1024,1,128]{2,1,0:T(1,128)S(1)}, u32[]{:S(2)}, u32[]{:S(2)}) %all-to-all-start.3) | async-done | bytes 524320 | tf_op jit(solution)/shard_map/all_to_all | solution.py:95
  240.3 2.6 %multiply_reduce_fusion = f32[1024,128]{1,0:T(8,128)S(1)} fusion(f32[1024,1,128]{2,1,0:T(1,128)} %shard_map.76, f32[1024,1,128]{2,1,0:T(1,128)S(1)} %all-to-all-done.3), kind=kLoop, calls=%fused_computation.36 | loop fusion | flops 262144 | bytes 1572864 | tf_op jit(solution)/shard_map/mul | solution.py:172
  243.1 0.3 reduce_sum.9
  243.4 9.5 %psum.7 = f32[2048]{0:T(1024)S(1)} all-reduce(f32[2048]{0:T(1024)S(1)} %broadcast_select_fusion), channel_id=1, replica_groups=mesh['dom'=128,'col'=2] {'col'}, use_global_device_ids=true, to_apply=%region_3.0 | all-reduce | flops 2048 | bytes 16384 | tf_op jit(solution)/shard_map/psum | solution.py:173
  253.0 0.6 broadcast_multiply_fusion
  (44 shorter events, 2.1 us)
Async XLA Ops:
  0.6 4.2 %copy-start.12 = (s32[1,128]{1,0:T(1,128)S(1)}, s32[1,128]{1,0:T(1,128)}, u32[]{:S(2)}) copy-start(s32[1,128]{1,0:T(1,128)} %param.8) | copy-start | bytes 1540
  1.4 3.6 %copy-start.11 = (s32[2048]{0:T(1024)S(1)}, s32[2048]{0:T(1024)}, u32[]{:S(2)}) copy-start(s32[2048]{0:T(1024)} %param.6) | copy-start | bytes 24580
  4.8 18.0 %copy-start.9 = (s32[2048]{0:T(1024)S(1)}, s32[2048]{0:T(1024)}, u32[]{:S(2)}) copy-start(s32[2048]{0:T(1024)} %a_ref.3) | copy-start | bytes 24580
  6.4 46.6 %all-to-all-start = ((f32[128,9,128]{2,1,0:T(8,128)}), f32[128,9,128]{2,1,0:T(8,128)S(1)}, u32[]{:S(2)}, u32[]{:S(2)}) async-start(f32[128,9,128]{2,1,0:T(8,128)} %maximum_maximum_fusion), calls=%async_computation | async-start | bytes 2097152 | tf_op jit(solution)/shard_map/all_to_all | solution.py:95
  53.9 1.7 copy-start.7
  55.5 14.1 %copy-start = (f32[4096,1,128]{2,1,0:T(1,128)S(1)}, f32[4096,1,128]{2,1,0:T(1,128)}, u32[]{:S(2)}) copy-start(f32[4096,1,128]{2,1,0:T(1,128)} %shard_map.68) | copy-start | bytes 6291460
  69.6 4.0 %copy-start.1 = (f32[4096,1,128]{2,1,0:T(1,128)S(1)}, f32[4096,1,128]{2,1,0:T(1,128)}, u32[]{:S(2)}) copy-start(f32[4096,1,128]{2,1,0:T(1,128)} %shard_map.69) | copy-start | bytes 6291460
  74.3 2.0 copy-start.2
  82.2 35.1 %copy-start.6 = (f32[2048,1,128]{2,1,0:T(1,128)S(1)}, f32[2048,1,128]{2,1,0:T(1,128)}, u32[]{:S(2)}) copy-start(f32[2048,1,128]{2,1,0:T(1,128)} %shard_map.70) | copy-start | bytes 3145732
  144.8 13.3 %copy-start.8 = (s32[2048]{0:T(1024)S(1)}, s32[2048]{0:T(1024)}, u32[]{:S(2)}) copy-start(s32[2048]{0:T(1024)} %copy-done.7) | copy-start | bytes 24580
  150.7 33.5 %copy-start.5 = (f32[2048,1,128]{2,1,0:T(1,128)S(1)}, f32[2048,1,128]{2,1,0:T(1,128)}, u32[]{:S(2)}) copy-start(f32[2048,1,128]{2,1,0:T(1,128)} %shard_map.73) | copy-start | bytes 3145732
  150.7 33.5 %all-to-all-start.2 = ((f32[2048,1,128]{2,1,0:T(1,128)}), f32[2048,1,128]{2,1,0:T(1,128)}, u32[]{:S(2)}, u32[]{:S(2)}) async-start(f32[2048,1,128]{2,1,0:T(1,128)} %shard_map.73), calls=%async_computation.2 | async-start | bytes 2097152 | tf_op jit(solution)/shard_map/all_to_all | solution.py:95
  212.5 2.0 copy-start.3
  214.5 10.7 %copy-start.10 = (s32[2048]{0:T(1024)S(1)}, s32[2048]{0:T(1024)}, u32[]{:S(2)}) copy-start(s32[2048]{0:T(1024)} %a_ref.3) | copy-start | bytes 24580
  214.5 12.3 %copy-start.4 = (f32[4096,64]{1,0:T(8,128)S(1)}, f32[4096,64]{1,0:T(8,128)}, u32[]{:S(2)}) copy-start(f32[4096,64]{1,0:T(8,128)} %copy-done.3) | copy-start | bytes 3145732
  218.6 21.7 %all-to-all-start.3 = ((f32[1024,1,128]{2,1,0:T(1,128)}), f32[1024,1,128]{2,1,0:T(1,128)S(1)}, u32[]{:S(2)}, u32[]{:S(2)}) async-start(f32[1024,1,128]{2,1,0:T(1,128)} %shard_map.77), calls=%async_computation.3 | async-start | bytes 1048576 | tf_op jit(solution)/shard_map/all_to_all | solution.py:95

commit v8 on v7

--- a/solution.py
+++ b/solution.py
@@ -44,8 +44,9 @@
     )(a, b, x)
 
 
-def _runs_kernel(key_ref, slot_ref, v_ref, o_ref):
+def _runs_kernel(side, key_ref, slot_ref, v_ref, o_ref):
     lanes = o_ref.shape[2]
+    low = lax.broadcasted_iota(jnp.int32, (1, lanes), 1) < lanes // 2
     step = 64
 
     @pl.loop(0, o_ref.shape[0] // step)
@@ -53,10 +54,16 @@
         at = pl.ds(pl.multiple_of(i * step, step), step)
         o_ref[at] = jnp.zeros((step,) + o_ref.shape[1:], o_ref.dtype)
 
+    def take(row):
+        if side is None:
+            return row
+        turned = pltpu.roll(row, lanes // 2, 1)
+        return jnp.where(low, row, turned) if side == 0 else jnp.where(low, turned, row)
+
     def body(t, carry):
         run, prev = carry
         base = t * BLOCK
-        rows = [v_ref[slot_ref[base + r]] for r in range(BLOCK)]
+        rows = [take(v_ref[slot_ref[base + r]]) for r in range(BLOCK)]
         for r in range(BLOCK):
             k = key_ref[base + r]
             run = jnp.where(k == prev, run, jnp.zeros_like(run)) + rows[r]
@@ -72,9 +79,9 @@
     )
 
 
-def sorted_sum(key, slot, vals, rows):
+def sorted_sum(key, slot, vals, rows, side=None):
     return pl.pallas_call(
-        _runs_kernel,
+        functools.partial(_runs_kernel, side),
         out_shape=jax.ShapeDtypeStruct((rows,) + vals.shape[1:], vals.dtype),
         in_specs=[
             pl.BlockSpec(memory_space=pltpu.SMEM),
@@ -137,27 +144,23 @@
     diag = ((1.0 + degree_boost) * degree + ground_shift)[:, None]
     extra = (degree_boost * degree + ground_shift)[:, None]
 
-    def ends(field):
-        doubled = jnp.concatenate([field, field], axis=1).reshape(VERT_DEV, 1, 2 * width)
-        return pair_gather(src_local, wanted, doubled)
-
     def apply(field):
-        here = ends(field)
-        there = a2a(here).reshape(edges, 2 * width)
-        here = here.reshape(edges, 2 * width)
+        here = pair_gather(src_local, wanted, field.reshape(VERT_DEV, 1, lanes))
+        there = a2a(here).reshape(edges, lanes)
+        here = here.reshape(edges, lanes)
         flow_out = w_out[:, None] * (here[:, :width] - there[:, width:])
         flow_in = w_in[:, None] * (there[:, :width] - here[:, width:])
         flows = jnp.concatenate([flow_out, -flow_in], axis=1).reshape(edges, 1, lanes)
-        at_first = sorted_sum(key_0, slot_0, flows, VERT_DEV)
-        at_second = sorted_sum(key_1, slot_1, flows, VERT_DEV)
-        return (at_first[:, :width] + at_second[:, width:]) + extra * field
+        at_first = sorted_sum(key_0, slot_0, flows, VERT_DEV, side=0)
+        at_second = sorted_sum(key_1, slot_1, flows, VERT_DEV, side=1)
+        return (at_first + at_second) + extra * field
 
     sigma = 1.25
     delta = 0.8
     coeff = 1.0 / sigma
-    resid = rhs
+    resid = jnp.concatenate([rhs, rhs], axis=1)
     direction = resid / diag
-    solution = jnp.zeros((VERT_DEV, width), jnp.float32)
+    solution = jnp.zeros((VERT_DEV, lanes), jnp.float32)
     for sweep in range(SWEEPS):
         solution = solution + direction
         if sweep < SWEEPS - 1:
@@ -165,13 +168,13 @@
             newer = 1.0 / (2.0 * sigma - coeff)
             direction = newer * coeff * direction + 2.0 * newer / delta * resid / diag
             coeff = newer
-    doubled = jnp.concatenate([solution, solution], axis=1).reshape(VERT_DEV, 1, lanes)
+    doubled = solution.reshape(VERT_DEV, 1, lanes)
     far = a2a(pair_gather(wanted[0::2], wanted[1::2], doubled)).reshape(edges, width)
     near = pair_gather(src_local[0::2], src_local[1::2], doubled).reshape(edges, width)
     diff = near - far
     partial_sum = jnp.sum(diff * diff, axis=1) * live.reshape(-1)
     resistance = lax.psum(partial_sum, "col") / SKETCH
-    return (solution.T, resistance)
+    return (solution[:, :width].T, resistance)
 
 
 def solution(mesh):

time: 255 us -> 312 us (1.22)
  other arithmetic: 48.3 us -> 79.4 us
  Pallas kernels: 73.8 us -> 101 us
  waiting for transfers between devices: 47 us -> 40.5 us
  local copies, waits for them, and re-layouts: 8.65 us -> 13.8 us
    pallas_call x6, Pallas kernels: 54 us -> 81.3 us  [sorted_sum(): pl.pallas_call(functools.partial(_runs_kernel, side), out_shape=jax.Shape...]
    add x1, other arithmetic: 5.03 us -> 14.8 us  [local(): direction = newer * coeff * direction + 2.0 * newer / delta * resid / diag]
    mul x0 -> x1, other arithmetic: none -> 7.48 us  [apply(): return at_first + at_second + extra * field]
    add x1, other arithmetic: 6.18 us -> 13.3 us  [local(): solution = solution + direction]
    all_to_all x3, waiting for transfers between devices: 47 us -> 40.5 us  [a2a(): return lax.all_to_all(x, 'dom', split_axis=0, concat_axis=0, tiled=True)]
    concatenate x3 -> x0, other arithmetic: 6 us -> none  [the longest x2 4.03 us: ends(): jnp.concatenate([field, field], axis=1).reshape(VERT_DEV, 1, 2 * width)]
    div x1, other arithmetic: 0.73 us -> 5.74 us  [local(): direction = resid / diag]
    transpose x0 -> x1, other arithmetic: none -> 4.83 us  [local(): return (solution[:, :width].T, resistance)]
  transfers between devices with their start and end apart: 3 -> 3, of which waited for: 3 -> 3; matrix products, arithmetic and copies ran while one was open for 5% -> 6% of each run, Pallas kernels for 5% -> 4%
where the time goes in v8:
time: 312 us; the launch traced here: 311 us
  Pallas kernels  101 us (32%)
  other arithmetic  79.4 us (25%)
  blocking collectives  44.7 us (14%)
  waiting for transfers between devices  40.5 us (13%)
  starting transfers between devices  30.3 us (10%)
  local copies, waits for them, and re-layouts  13.8 us (4%)
    pallas_call x6, Pallas kernels, sorted_sum(): pl.pallas_call(functools.partial(_runs_kernel, side), out_shape=jax.Shape...  81.3 us
    all_to_all x3, waiting for transfers between devices, a2a(): return lax.all_to_all(x, 'dom', split_axis=0, concat_axis=0, tiled=True)  40.5 us
    all_to_all x1, blocking collectives, a2a(): return lax.all_to_all(x, 'dom', split_axis=0, concat_axis=0, tiled=True)  35.2 us
    all_to_all x3, starting transfers between devices, a2a(): return lax.all_to_all(x, 'dom', split_axis=0, concat_axis=0, tiled=True)  30.3 us
    pallas_call x4, Pallas kernels, pair_gather(): pl.pallas_call(_pair_gather_kernel, out_shape=jax.ShapeDtypeStruct((a.sha...  19.9 us
    add x1, other arithmetic, local(): direction = newer * coeff * direction + 2.0 * newer / delta * resid / diag  14.8 us
    add x1, other arithmetic, local(): solution = solution + direction  13.3 us
    psum x1, blocking collectives, local(): resistance = lax.psum(partial_sum, 'col') / SKETCH  9.52 us
  transfers between devices with their start and end apart: 3, of which 3 were waited for; matrix products, arithmetic and copies ran while one was open for 6% of the time, Pallas kernels for 4%

profile of v8, /device:TPU:1, one launch (start us, length us, event | category | flops | bytes accessed | tf_op | source)
XLA Modules:
  0.0 310.8 jit_solution(11096678031606697329)
XLA Ops:
  0.6 0.8 iota_compare_fusion
  1.6 0.8 reshape.309
  2.3 0.7 fusion.16
  3.0 1.2 copy.51
  5.3 1.2 maximum_maximum_fusion
  6.4 16.3 %all-to-all-start = ((f32[128,9,128]{2,1,0:T(8,128)}), f32[128,9,128]{2,1,0:T(8,128)S(1)}, u32[]{:S(2)}, u32[]{:S(2)}) async-start(f32[128,9,128]{2,1,0:T(8,128)} %maximum_maximum_fusion), calls=%async_computation | async-start | bytes 2097152 | tf_op jit(solution)/shard_map/all_to_all | solution.py:102
  22.8 5.0 %sort.30 = (s32[2048]{0:T(1024)}, s32[2048]{0:T(1024)}) sort(s32[2048]{0:T(1024)S(1)} %copy-done.14, s32[2048]{0:T(1024)S(1)} %iota.14), dimensions={0}, to_apply=%region_0.0 | sort | flops 22528 | bytes 32768 | tf_op jit(solution)/shard_map/sort | solution.py:111
  28.2 1.3 pad_maximum_fusion.2
  29.5 9.0 %shard_map.68 = f32[4096,1,128]{2,1,0:T(1,128)} custom-call(s32[2048]{0:T(1024)} %get-tuple-element.6.key_ref, s32[2048]{0:T(1024)} %get-tuple-element.7.slot_ref, f32[2048,1,128]{2,1,0:T(1,128)} %bitcast.61), custom_call_target="tpu_custom_call" | custom-call | tf_op jit(solution)/shard_map/pallas_call | solution.py:83
  38.5 14.5 %all-to-all-done = f32[128,9,128]{2,1,0:T(8,128)S(1)} async-done(((f32[128,9,128]{2,1,0:T(8,128)}), f32[128,9,128]{2,1,0:T(8,128)S(1)}, u32[]{:S(2)}, u32[]{:S(2)}) %all-to-all-start) | async-done | bytes 589856 | tf_op jit(solution)/shard_map/all_to_all | solution.py:102
  54.2 1.3 pad_maximum_fusion.3
  55.5 5.0 %sort.31 = (s32[2048]{0:T(1024)}, s32[2048]{0:T(1024)}) sort(s32[2048]{0:T(1024)S(1)} %convert_element_type.16.b_ref, s32[2048]{0:T(1024)S(1)} %iota.15), dimensions={0}, to_apply=%region_1.0 | sort | flops 22528 | bytes 32768 | tf_op jit(solution)/shard_map/sort | solution.py:133
  60.6 9.0 %shard_map.69 = f32[4096,1,128]{2,1,0:T(1,128)} custom-call(s32[2048]{0:T(1024)} %get-tuple-element.8.key_ref, s32[2048]{0:T(1024)} %get-tuple-element.9.slot_ref, f32[2048,1,128]{2,1,0:T(1,128)} %bitcast.60), custom_call_target="tpu_custom_call" | custom-call | tf_op jit(solution)/shard_map/pallas_call | solution.py:83
  69.5 4.0 %add_reduce_fusion = (f32[4096]{0:T(1024)S(1)}, f32[4096]{0:T(1024)S(1)}) fusion(f32[4096,128]{1,0:T(8,128)} %bitcast.44, f32[4096,128]{1,0:T(8,128)S(1)} %bitcast.42), kind=kLoop, calls=%fused_computation.18 | loop fusion | flops 20480 | bytes 65536 | tf_op jit(solution)/shard_map/add | solution.py:145
  74.5 0.7 copy-done.2
  75.1 5.7 %fusion.14.x_ref = f32[4096,1,128]{2,1,0:T(1,128)} fusion(f32[4096,1,128]{2,1,0:T(1,128)S(1)} %bitcast.37, f32[4096,1,64]{2,1,0:T(1,128)S(1)} %bitcast.40), kind=kLoop, calls=%fused_computation.48 | loop fusion | flops 1048576 | bytes 5242880 | tf_op jit(solution)/shard_map/div | solution.py:162
  80.9 5.8 %shard_map.70 = f32[2048,1,128]{2,1,0:T(1,128)} custom-call(s32[2048]{0:T(1024)} %a_ref.3, s32[2048]{0:T(1024)} %copy-done.12, f32[4096,1,128]{2,1,0:T(1,128)} %fusion.14.x_ref), custom_call_target="tpu_custom_call" | custom-call | tf_op jit(solution)/shard_map/pallas_call | solution.py:35
  86.7 35.2 %all_to_all.20 = f32[2048,1,128]{2,1,0:T(1,128)S(1)} all-to-all(f32[2048,1,128]{2,1,0:T(1,128)} %shard_map.70), channel_id=1, replica_groups=mesh['dom'=128,'col'=2] {'dom'}, dimensions={0} | all-to-all | bytes 2097152 | tf_op jit(solution)/shard_map/all_to_all | solution.py:102
  121.9 1.2 fusion.12
  123.2 1.3 pad_maximum_fusion.4
  124.5 15.8 %shard_map.72 = f32[4096,1,128]{2,1,0:T(1,128)} custom-call(s32[2048]{0:T(1024)} %get-tuple-element.8.key_ref, s32[2048]{0:T(1024)} %get-tuple-element.9.slot_ref, f32[2048,1,128]{2,1,0:T(1,128)} %bitcast.52), custom_call_target="tpu_custom_call" | custom-call | tf_op jit(solution)/shard_map/pallas_call | solution.py:83
  140.3 15.8 %shard_map.71 = f32[4096,1,128]{2,1,0:T(1,128)} custom-call(s32[2048]{0:T(1024)} %get-tuple-element.6.key_ref, s32[2048]{0:T(1024)} %get-tuple-element.7.slot_ref, f32[2048,1,128]{2,1,0:T(1,128)} %bitcast.53), custom_call_target="tpu_custom_call" | custom-call | tf_op jit(solution)/shard_map/pallas_call | solution.py:83
  156.1 7.5 %broadcast_multiply_fusion = (f32[4096,128]{1,0:T(8,128)}, f32[4096,128]{1,0:T(8,128)}, f32[4096,128]{1,0:T(8,128)}, f32[4096,1,128]{2,0,1:T(8,128)S(1)}, f32[4096,128]{1,0:T(8,128)}) fusion(f32[4096]{0:T(1024)S(1)} %get-tuple-element.18, f32[4096]{0:T(1024)S(1)} %get-tuple-element.19, f32[4096,64]{1,0:T(8,128)} %copy-done.2, f32[4096,1,128]{2,0,1:T(8,128)} %bitcast.58, ...), kind=kLoop, calls=%fused_computation.36 | loop fusion | flops 5767168 | bytes 15761408 | tf_op jit(solution)/shard_map/mul | solution.py:156
  163.6 14.8 %divide_add_fusion = (f32[4096,1,128]{2,1,0:T(1,128)}, f32[4096,1,128]{2,1,0:T(1,128)}) fusion(f32[4096,1,128]{2,1,0:T(1,128)S(1)} %bitcast.38, f32[4096,1,128]{2,1,0:T(1,128)S(1)} %copy-done, f32[4096,1,128]{2,1,0:T(1,128)S(1)} %bitcast.59, f32[4096]{0:T(1024)S(1)} %get-tuple-element.18, f32[4096,1,64]{2,1,0:T(1,128)S(1)} %bitcast.41), kind=kLoop, calls=%fused_computation.15 | loop fusion | flops 4194304 | bytes 11550720 | tf_op jit(solution)/shard_map/add | solution.py:169
  178.4 5.8 %shard_map.73 = f32[2048,1,128]{2,1,0:T(1,128)} custom-call(s32[2048]{0:T(1024)} %a_ref.3, s32[2048]{0:T(1024)} %copy-done.12, f32[4096,1,128]{2,1,0:T(1,128)} %get-tuple-element.20.x_ref), custom_call_target="tpu_custom_call" | custom-call | tf_op jit(solution)/shard_map/pallas_call | solution.py:35
  184.3 7.4 %all-to-all-start.2 = ((f32[2048,1,128]{2,1,0:T(1,128)}), f32[2048,1,128]{2,1,0:T(1,128)}, u32[]{:S(2)}, u32[]{:S(2)}) async-start(f32[2048,1,128]{2,1,0:T(1,128)} %shard_map.73), calls=%async_computation.2 | async-start | bytes 2097152 | tf_op jit(solution)/shard_map/all_to_all | solution.py:102
  191.7 0.8 slice.76.a_ref
  192.5 0.8 slice.77.b_ref
  193.3 0.8 slice.78.a_ref
  194.1 0.8 slice.79.b_ref
  194.9 22.9 %all-to-all-done.2 = f32[2048,1,128]{2,1,0:T(1,128)} async-done(((f32[2048,1,128]{2,1,0:T(1,128)}), f32[2048,1,128]{2,1,0:T(1,128)}, u32[]{:S(2)}, u32[]{:S(2)}) %all-to-all-start.2) | async-done | bytes 1048608 | tf_op jit(solution)/shard_map/all_to_all | solution.py:102
  217.8 2.7 fusion.9
  220.5 1.3 pad_maximum_fusion.5
  221.8 15.8 %shard_map.75 = f32[4096,1,128]{2,1,0:T(1,128)} custom-call(s32[2048]{0:T(1024)} %get-tuple-element.8.key_ref, s32[2048]{0:T(1024)} %get-tuple-element.9.slot_ref, f32[2048,1,128]{2,1,0:T(1,128)} %bitcast.50), custom_call_target="tpu_custom_call" | custom-call | tf_op jit(solution)/shard_map/pallas_call | solution.py:83
  237.6 15.8 %shard_map.74 = f32[4096,1,128]{2,1,0:T(1,128)} custom-call(s32[2048]{0:T(1024)} %get-tuple-element.6.key_ref, s32[2048]{0:T(1024)} %get-tuple-element.7.slot_ref, f32[2048,1,128]{2,1,0:T(1,128)} %bitcast.51), custom_call_target="tpu_custom_call" | custom-call | tf_op jit(solution)/shard_map/pallas_call | solution.py:83
  253.5 2.6 add.82
  256.1 1.3 copy-done.6
  257.4 0.9 copy-done.11
  258.3 13.3 %add_add_fusion.x_ref = f32[4096,1,128]{2,1,0:T(1,128)} fusion(f32[4096,1,128]{2,1,0:T(1,128)S(1)} %bitcast.39, f32[4096,1,128]{2,1,0:T(1,128)S(1)} %copy-done.11, f32[4096,1,128]{2,1,0:T(1,128)S(1)} %bitcast.46, f32[4096,1,128]{2,1,0:T(1,128)S(1)} %copy-done.8, f32[4096,1,128]{2,1,0:T(1,128)S(1)} %copy-done.1, f32[4096]{0:T(1024)S(1)} %get-tuple-element.18), kind=kLoop, calls=%fused_computation.14 | loop fusion | flops 4718592 | bytes 12599296 | tf_op jit(solution)/shard_map/add | solution.py:165
  271.7 4.2 %shard_map.77 = f32[1024,1,128]{2,1,0:T(1,128)} custom-call(s32[1024]{0:T(1024)} %slice.78.a_ref, s32[1024]{0:T(1024)} %slice.79.b_ref, f32[4096,1,128]{2,1,0:T(1,128)} %add_add_fusion.x_ref), custom_call_target="tpu_custom_call" | custom-call | tf_op jit(solution)/shard_map/pallas_call | solution.py:35
  275.8 6.5 %all-to-all-start.3 = ((f32[1024,1,128]{2,1,0:T(1,128)}), f32[1024,1,128]{2,1,0:T(1,128)S(1)}, u32[]{:S(2)}, u32[]{:S(2)}) async-start(f32[1024,1,128]{2,1,0:T(1,128)} %shard_map.77), calls=%async_computation.3 | async-start | bytes 1048576 | tf_op jit(solution)/shard_map/all_to_all | solution.py:102
  282.4 4.8 %fusion.1 = f32[64,4096]{0,1:T(8,128)} fusion(f32[4096,128]{1,0:T(8,128)} %get-tuple-element.28, f32[4096,128]{1,0:T(8,128)} %get-tuple-element.24, f32[4096,128]{1,0:T(8,128)} %get-tuple-element.22, f32[4096,128]{1,0:T(8,128)S(1)} %bitcast.47, f32[4096,128]{1,0:T(8,128)} %get-tuple-element.23, f32[4096]{0:T(1024)S(1)} %get-tuple-element.19), kind=kLoop, calls=%fused_computation.2 | loop fusion | flops 2097152 | bytes 6307840 | tf_op jit(solution)/shard_map/transpose | solution.py:177
  287.2 3.1 %copy.68 = f32[64,4096]{1,0:T(8,128)} copy(f32[64,4096]{0,1:T(8,128)} %fusion.1) | data formatting | bytes 2097152
  290.4 4.0 %shard_map.76 = f32[1024,1,128]{2,1,0:T(1,128)} custom-call(s32[1024]{0:T(1024)} %slice.76.a_ref, s32[1024]{0:T(1024)} %slice.77.b_ref, f32[4096,1,128]{2,1,0:T(1,128)} %add_add_fusion.x_ref), custom_call_target="tpu_custom_call" | custom-call | tf_op jit(solution)/shard_map/pallas_call | solution.py:35
  294.4 3.1 all-to-all-done.3
  297.5 2.6 multiply_reduce_fusion
  300.6 9.5 %psum.7 = f32[2048]{0:T(1024)S(1)} all-reduce(f32[2048]{0:T(1024)S(1)} %broadcast_select_fusion), channel_id=1, replica_groups=mesh['dom'=128,'col'=2] {'col'}, use_global_device_ids=true, to_apply=%region_3.0 | all-reduce | flops 2048 | bytes 16384 | tf_op jit(solution)/shard_map/psum | solution.py:176
  310.2 0.6 broadcast_multiply_fusion.1
  (56 shorter events, 4.0 us)
Async XLA Ops:
  0.6 4.2 %copy-start.17 = (s32[1,128]{1,0:T(1,128)S(1)}, s32[1,128]{1,0:T(1,128)}, u32[]{:S(2)}) copy-start(s32[1,128]{1,0:T(1,128)} %param.8) | copy-start | bytes 1540
  1.4 3.6 %copy-start.16 = (s32[2048]{0:T(1024)S(1)}, s32[2048]{0:T(1024)}, u32[]{:S(2)}) copy-start(s32[2048]{0:T(1024)} %param.6) | copy-start | bytes 24580
  4.8 18.0 %copy-start.14 = (s32[2048]{0:T(1024)S(1)}, s32[2048]{0:T(1024)}, u32[]{:S(2)}) copy-start(s32[2048]{0:T(1024)} %a_ref.3) | copy-start | bytes 24580
  6.4 46.6 %all-to-all-start = ((f32[128,9,128]{2,1,0:T(8,128)}), f32[128,9,128]{2,1,0:T(8,128)S(1)}, u32[]{:S(2)}, u32[]{:S(2)}) async-start(f32[128,9,128]{2,1,0:T(8,128)} %maximum_maximum_fusion), calls=%async_computation | async-start | bytes 2097152 | tf_op jit(solution)/shard_map/all_to_all | solution.py:102
  53.9 1.7 copy-start.12
  55.5 14.0 %copy-start.4 = (f32[4096,1,128]{2,1,0:T(1,128)S(1)}, f32[4096,1,128]{2,1,0:T(1,128)}, u32[]{:S(2)}) copy-start(f32[4096,1,128]{2,1,0:T(1,128)} %shard_map.68) | copy-start | bytes 6291460
  69.5 4.0 %copy-start.5 = (f32[4096,1,128]{2,1,0:T(1,128)S(1)}, f32[4096,1,128]{2,1,0:T(1,128)}, u32[]{:S(2)}) copy-start(f32[4096,1,128]{2,1,0:T(1,128)} %shard_map.69) | copy-start | bytes 6291460
  73.8 1.3 copy-start.2
  86.7 35.2 %copy-start.10 = (f32[2048,1,128]{2,1,0:T(1,128)S(1)}, f32[2048,1,128]{2,1,0:T(1,128)}, u32[]{:S(2)}) copy-start(f32[2048,1,128]{2,1,0:T(1,128)} %shard_map.70) | copy-start | bytes 3145732
  156.1 7.5 %copy-start = (f32[4096,1,128]{2,1,0:T(1,128)S(1)}, f32[4096,1,128]{2,1,0:T(1,128)}, u32[]{:S(2)}) copy-start(f32[4096,1,128]{2,1,0:T(1,128)} %fusion.14.x_ref) | copy-start | bytes 6291460
  156.1 7.5 %copy-start.3 = (f32[4096,64]{1,0:T(8,128)S(1)}, f32[4096,64]{1,0:T(8,128)}, u32[]{:S(2)}) copy-start(f32[4096,64]{1,0:T(8,128)} %copy-done.2) | copy-start | bytes 3145732
  178.4 13.3 %copy-start.15 = (s32[2048]{0:T(1024)S(1)}, s32[2048]{0:T(1024)}, u32[]{:S(2)}) copy-start(s32[2048]{0:T(1024)} %a_ref.3) | copy-start | bytes 24580
  178.4 14.9 %copy-start.13 = (s32[2048]{0:T(1024)S(1)}, s32[2048]{0:T(1024)}, u32[]{:S(2)}) copy-start(s32[2048]{0:T(1024)} %copy-done.12) | copy-start | bytes 24580
  184.3 33.5 %copy-start.9 = (f32[2048,1,128]{2,1,0:T(1,128)S(1)}, f32[2048,1,128]{2,1,0:T(1,128)}, u32[]{:S(2)}) copy-start(f32[2048,1,128]{2,1,0:T(1,128)} %shard_map.73) | copy-start | bytes 3145732
  184.3 33.5 %all-to-all-start.2 = ((f32[2048,1,128]{2,1,0:T(1,128)}), f32[2048,1,128]{2,1,0:T(1,128)}, u32[]{:S(2)}, u32[]{:S(2)}) async-start(f32[2048,1,128]{2,1,0:T(1,128)} %shard_map.73), calls=%async_computation.2 | async-start | bytes 2097152 | tf_op jit(solution)/shard_map/all_to_all | solution.py:102
  253.5 3.9 %copy-start.1 = (f32[4096,1,128]{2,1,0:T(1,128)S(1)}, f32[4096,1,128]{2,1,0:T(1,128)}, u32[]{:S(2)}) copy-start(f32[4096,1,128]{2,1,0:T(1,128)} %fusion.14.x_ref) | copy-start | bytes 6291460
  253.5 3.9 %copy-start.8 = (f32[4096,1,128]{2,1,0:T(1,128)S(1)}, f32[4096,1,128]{2,1,0:T(1,128)}, u32[]{:S(2)}) copy-start(f32[4096,1,128]{2,1,0:T(1,128)} %get-tuple-element.20.x_ref) | copy-start | bytes 6291460
  253.5 4.9 %copy-start.11 = (f32[4096,1,128]{2,1,0:T(1,128)S(1)}, f32[4096,1,128]{2,1,0:T(1,128)}, u32[]{:S(2)}) copy-start(f32[4096,1,128]{2,1,0:T(1,128)} %get-tuple-element.21) | copy-start | bytes 6291460
  256.1 1.3 copy-start.6
  271.7 10.7 %copy-start.7 = (f32[4096,1,128]{2,0,1:T(8,128)S(1)}, f32[4096,1,128]{2,0,1:T(8,128)}, u32[]{:S(2)}) copy-start(f32[4096,1,128]{2,0,1:T(8,128)} %copy-done.6) | copy-start | bytes 6291460
  275.8 21.7 %all-to-all-start.3 = ((f32[1024,1,128]{2,1,0:T(1,128)}), f32[1024,1,128]{2,1,0:T(1,128)S(1)}, u32[]{:S(2)}, u32[]{:S(2)}) async-start(f32[1024,1,128]{2,1,0:T(1,128)} %shard_map.77), calls=%async_computation.3 | async-start | bytes 1048576 | tf_op jit(solution)/shard_map/all_to_all | solution.py:102

commit v9 on v7

--- a/solution.py
+++ b/solution.py
@@ -133,9 +133,9 @@
         VERT_DEV,
     )
     rhs = own[:, :width] + far[:, :width]
-    degree = own[:, width] + far[:, width]
-    diag = ((1.0 + degree_boost) * degree + ground_shift)[:, None]
-    extra = (degree_boost * degree + ground_shift)[:, None]
+    degree = own[:, width:] + far[:, width:]
+    diag = (1.0 + degree_boost) * degree + ground_shift
+    extra = degree_boost * degree + ground_shift
 
     def ends(field):
         doubled = jnp.concatenate([field, field], axis=1).reshape(VERT_DEV, 1, 2 * width)

time: 255 us -> 255 us (level)
    add x1 -> x0, other arithmetic: 3.99 us -> none  [local(): extra = (degree_boost * degree + ground_shift)[:, None]]
    div x1, other arithmetic: 0.73 us -> 3.37 us  [local(): direction = resid / diag]
where the time goes in v9:
time: 255 us; the launch traced here: 254 us
  Pallas kernels  73.8 us (29%)
  other arithmetic  49 us (19%)
  waiting for transfers between devices  47 us (18%)
  blocking collectives  44.6 us (17%)
  starting transfers between devices  30.3 us (12%)
  local copies, waits for them, and re-layouts  8.65 us (3%)
    pallas_call x6, Pallas kernels, sorted_sum(): pl.pallas_call(_runs_kernel, out_shape=jax.ShapeDtypeStruct((rows,) + val...  54 us
    all_to_all x3, waiting for transfers between devices, a2a(): return lax.all_to_all(x, 'dom', split_axis=0, concat_axis=0, tiled=True)  47 us
    all_to_all x1, blocking collectives, a2a(): return lax.all_to_all(x, 'dom', split_axis=0, concat_axis=0, tiled=True)  35 us
    all_to_all x3, starting transfers between devices, a2a(): return lax.all_to_all(x, 'dom', split_axis=0, concat_axis=0, tiled=True)  30.3 us
    pallas_call x4, Pallas kernels, pair_gather(): pl.pallas_call(_pair_gather_kernel, out_shape=jax.ShapeDtypeStruct((a.sha...  19.8 us
    psum x1, blocking collectives, local(): resistance = lax.psum(partial_sum, 'col') / SKETCH  9.53 us
    add x1, other arithmetic, local(): solution = solution + direction  7.81 us
    add x1, other arithmetic, local(): direction = newer * coeff * direction + 2.0 * newer / delta * resid / diag  5.47 us
  transfers between devices with their start and end apart: 3, of which 3 were waited for; matrix products, arithmetic and copies ran while one was open for 5% of the time, Pallas kernels for 5%

profile of v9, /device:TPU:1, one launch (start us, length us, event | category | flops | bytes accessed | tf_op | source)
XLA Modules:
  0.0 254.2 jit_solution(12593828316202811298)
XLA Ops:
  0.6 0.8 iota_compare_fusion
  1.6 0.8 reshape.144
  2.3 0.7 fusion.16
  3.0 1.2 copy.39
  4.3 0.3 multiply_bitcast_fusion
  5.3 1.2 maximum_maximum_fusion
  6.4 16.3 %all-to-all-start = ((f32[128,9,128]{2,1,0:T(8,128)}), f32[128,9,128]{2,1,0:T(8,128)S(1)}, u32[]{:S(2)}, u32[]{:S(2)}) async-start(f32[128,9,128]{2,1,0:T(8,128)} %maximum_maximum_fusion), calls=%async_computation | async-start | bytes 2097152 | tf_op jit(solution)/shard_map/all_to_all | solution.py:95
  22.8 5.0 %sort.30 = (s32[2048]{0:T(1024)}, s32[2048]{0:T(1024)}) sort(s32[2048]{0:T(1024)S(1)} %copy-done.9, s32[2048]{0:T(1024)S(1)} %iota.14), dimensions={0}, to_apply=%region_0.0 | sort | flops 22528 | bytes 32768 | tf_op jit(solution)/shard_map/sort | solution.py:104
  27.8 0.3 mul.107
  28.2 1.3 pad_maximum_fusion.3
  29.5 9.0 %shard_map.68 = f32[4096,1,128]{2,1,0:T(1,128)} custom-call(s32[2048]{0:T(1024)} %get-tuple-element.6.key_ref, s32[2048]{0:T(1024)} %get-tuple-element.7.slot_ref, f32[2048,1,128]{2,1,0:T(1,128)} %bitcast.58), custom_call_target="tpu_custom_call" | custom-call | tf_op jit(solution)/shard_map/pallas_call | solution.py:76
  38.5 14.6 %all-to-all-done = f32[128,9,128]{2,1,0:T(8,128)S(1)} async-done(((f32[128,9,128]{2,1,0:T(8,128)}), f32[128,9,128]{2,1,0:T(8,128)S(1)}, u32[]{:S(2)}, u32[]{:S(2)}) %all-to-all-start) | async-done | bytes 589856 | tf_op jit(solution)/shard_map/all_to_all | solution.py:95
  53.9 0.3 mul.110
  54.2 1.3 pad_maximum_fusion.4
  55.5 5.0 %sort.31 = (s32[2048]{0:T(1024)}, s32[2048]{0:T(1024)}) sort(s32[2048]{0:T(1024)S(1)} %convert_element_type.16.b_ref, s32[2048]{0:T(1024)S(1)} %iota.15), dimensions={0}, to_apply=%region_1.0 | sort | flops 22528 | bytes 32768 | tf_op jit(solution)/shard_map/sort | solution.py:126
  60.6 9.0 %shard_map.69 = f32[4096,1,128]{2,1,0:T(1,128)} custom-call(s32[2048]{0:T(1024)} %get-tuple-element.8.key_ref, s32[2048]{0:T(1024)} %get-tuple-element.9.slot_ref, f32[2048,1,128]{2,1,0:T(1,128)} %bitcast.57), custom_call_target="tpu_custom_call" | custom-call | tf_op jit(solution)/shard_map/pallas_call | solution.py:76
  69.6 3.4 %fusion.8 = f32[4096,64]{1,0:T(8,128)S(1)} fusion(f32[4096,128]{1,0:T(8,128)} %bitcast.36, f32[4096,128]{1,0:T(8,128)S(1)} %bitcast.33), kind=kLoop, calls=%fused_computation.18 | loop fusion | flops 1310720 | bytes 5242880 | tf_op jit(solution)/shard_map/div | solution.py:159
  73.0 2.0 pad_maximum_fusion
  75.0 5.8 %shard_map.70 = f32[2048,1,128]{2,1,0:T(1,128)} custom-call(s32[2048]{0:T(1024)} %a_ref.3, s32[2048]{0:T(1024)} %copy-done.7, f32[4096,1,128]{2,1,0:T(1,128)} %bitcast.53), custom_call_target="tpu_custom_call" | custom-call | tf_op jit(solution)/shard_map/pallas_call | solution.py:35
  80.8 35.0 %all_to_all.20 = f32[2048,1,128]{2,1,0:T(1,128)S(1)} all-to-all(f32[2048,1,128]{2,1,0:T(1,128)} %shard_map.70), channel_id=1, replica_groups=mesh['dom'=128,'col'=2] {'dom'}, dimensions={0} | all-to-all | bytes 2097152 | tf_op jit(solution)/shard_map/all_to_all | solution.py:95
  115.9 1.2 fusion.14
  117.1 1.3 pad_maximum_fusion.5
  118.4 9.0 %shard_map.71 = f32[4096,1,128]{2,1,0:T(1,128)} custom-call(s32[2048]{0:T(1024)} %get-tuple-element.6.key_ref, s32[2048]{0:T(1024)} %get-tuple-element.7.slot_ref, f32[2048,1,128]{2,1,0:T(1,128)} %bitcast.50), custom_call_target="tpu_custom_call" | custom-call | tf_op jit(solution)/shard_map/pallas_call | solution.py:76
  127.4 9.0 %shard_map.72 = f32[4096,1,128]{2,1,0:T(1,128)} custom-call(s32[2048]{0:T(1024)} %get-tuple-element.8.key_ref, s32[2048]{0:T(1024)} %get-tuple-element.9.slot_ref, f32[2048,1,128]{2,1,0:T(1,128)} %bitcast.51), custom_call_target="tpu_custom_call" | custom-call | tf_op jit(solution)/shard_map/pallas_call | solution.py:76
  136.4 5.5 %divide_add_fusion = f32[4096,64]{1,0:T(8,128)S(1)} fusion(f32[4096,64]{1,0:T(8,128)} %copy-done.1, f32[4096,128]{1,0:T(8,128)} %bitcast.44, f32[4096,128]{1,0:T(8,128)} %bitcast.42, f32[4096,128]{1,0:T(8,128)} %bitcast.37, f32[4096,128]{1,0:T(8,128)S(1)} %bitcast.34), kind=kLoop, calls=%fused_computation.15 | loop fusion | flops 3670016 | bytes 8388608 | tf_op jit(solution)/shard_map/add | solution.py:166
  141.9 2.0 pad_maximum_fusion.1
  143.9 5.8 %shard_map.73 = f32[2048,1,128]{2,1,0:T(1,128)} custom-call(s32[2048]{0:T(1024)} %a_ref.3, s32[2048]{0:T(1024)} %copy-done.7, f32[4096,1,128]{2,1,0:T(1,128)} %bitcast.54), custom_call_target="tpu_custom_call" | custom-call | tf_op jit(solution)/shard_map/pallas_call | solution.py:35
  149.7 7.4 %all-to-all-start.2 = ((f32[2048,1,128]{2,1,0:T(1,128)}), f32[2048,1,128]{2,1,0:T(1,128)}, u32[]{:S(2)}, u32[]{:S(2)}) async-start(f32[2048,1,128]{2,1,0:T(1,128)} %shard_map.73), calls=%async_computation.2 | async-start | bytes 2097152 | tf_op jit(solution)/shard_map/all_to_all | solution.py:95
  157.2 0.8 slice.90.a_ref
  158.0 0.8 slice.91.b_ref
  158.8 24.5 %all-to-all-done.2 = f32[2048,1,128]{2,1,0:T(1,128)} async-done(((f32[2048,1,128]{2,1,0:T(1,128)}), f32[2048,1,128]{2,1,0:T(1,128)}, u32[]{:S(2)}, u32[]{:S(2)}) %all-to-all-start.2) | async-done | bytes 1048608 | tf_op jit(solution)/shard_map/all_to_all | solution.py:95
  183.3 2.8 %fusion.11 = (f32[2048,64]{1,0:T(8,128)S(1)}, f32[2048,64]{1,0:T(8,128)S(1)}) fusion(f32[2048,128]{1,0:T(8,128)} %bitcast.22, f32[2048,128]{1,0:T(8,128)S(1)} %bitcast.46, f32[2048]{0:T(1024)S(1)} %get-tuple-element.19, f32[2048]{0:T(1024)S(1)} %mul.109), kind=kLoop, calls=%fused_computation.23 | loop fusion | flops 655360 | bytes 3162112 | tf_op jit(solution)/shard_map/mul | solution.py:148
  186.0 1.3 pad_maximum_fusion.6
  187.3 9.0 %shard_map.74 = f32[4096,1,128]{2,1,0:T(1,128)} custom-call(s32[2048]{0:T(1024)} %get-tuple-element.6.key_ref, s32[2048]{0:T(1024)} %get-tuple-element.7.slot_ref, f32[2048,1,128]{2,1,0:T(1,128)} %bitcast.48), custom_call_target="tpu_custom_call" | custom-call | tf_op jit(solution)/shard_map/pallas_call | solution.py:76
  196.3 9.0 %shard_map.75 = f32[4096,1,128]{2,1,0:T(1,128)} custom-call(s32[2048]{0:T(1024)} %get-tuple-element.8.key_ref, s32[2048]{0:T(1024)} %get-tuple-element.9.slot_ref, f32[2048,1,128]{2,1,0:T(1,128)} %bitcast.49), custom_call_target="tpu_custom_call" | custom-call | tf_op jit(solution)/shard_map/pallas_call | solution.py:76
  205.3 7.8 %fusion.5 = f32[4096,64]{1,0:T(8,128)S(1)} fusion(f32[4096,128]{1,0:T(8,128)} %bitcast.56, f32[4096,128]{1,0:T(8,128)} %bitcast.55, f32[4096,64]{1,0:T(8,128)} %copy-done.4, f32[4096,64]{1,0:T(8,128)} %copy-done.1, f32[4096,128]{1,0:T(8,128)} %bitcast.45, f32[4096,128]{1,0:T(8,128)} %bitcast.43, f32[4096,128]{1,0:T(8,128)} %bitcast.38, ...), kind=kLoop, calls=%fused_computation.6 | loop fusion | flops 5242880 | bytes 11534336 | tf_op jit(solution)/shard_map/add | solution.py:162
  213.2 2.0 pad_maximum_fusion.2
  215.1 4.2 %shard_map.77 = f32[1024,1,128]{2,1,0:T(1,128)} custom-call(s32[1024]{0:T(1024)} %slice.90.a_ref, s32[1024]{0:T(1024)} %slice.91.b_ref, f32[4096,1,128]{2,1,0:T(1,128)} %bitcast.39), custom_call_target="tpu_custom_call" | custom-call | tf_op jit(solution)/shard_map/pallas_call | solution.py:35
  219.3 6.5 %all-to-all-start.3 = ((f32[1024,1,128]{2,1,0:T(1,128)}), f32[1024,1,128]{2,1,0:T(1,128)S(1)}, u32[]{:S(2)}, u32[]{:S(2)}) async-start(f32[1024,1,128]{2,1,0:T(1,128)} %shard_map.77), calls=%async_computation.3 | async-start | bytes 1048576 | tf_op jit(solution)/shard_map/all_to_all | solution.py:95
  225.8 0.8 slice.88.a_ref
  226.6 0.8 slice.89.b_ref
  227.4 1.6 copy.49
  229.0 4.0 %shard_map.76 = f32[1024,1,128]{2,1,0:T(1,128)} custom-call(s32[1024]{0:T(1024)} %slice.88.a_ref, s32[1024]{0:T(1024)} %slice.89.b_ref, f32[4096,1,128]{2,1,0:T(1,128)} %bitcast.40), custom_call_target="tpu_custom_call" | custom-call | tf_op jit(solution)/shard_map/pallas_call | solution.py:35
  233.0 7.9 %all-to-all-done.3 = f32[1024,1,128]{2,1,0:T(1,128)S(1)} async-done(((f32[1024,1,128]{2,1,0:T(1,128)}), f32[1024,1,128]{2,1,0:T(1,128)S(1)}, u32[]{:S(2)}, u32[]{:S(2)}) %all-to-all-start.3) | async-done | bytes 524320 | tf_op jit(solution)/shard_map/all_to_all | solution.py:95
  241.0 2.6 %multiply_reduce_fusion = f32[1024,128]{1,0:T(8,128)S(1)} fusion(f32[1024,1,128]{2,1,0:T(1,128)} %shard_map.76, f32[1024,1,128]{2,1,0:T(1,128)S(1)} %all-to-all-done.3), kind=kLoop, calls=%fused_computation.36 | loop fusion | flops 262144 | bytes 1572864 | tf_op jit(solution)/shard_map/mul | solution.py:172
  243.7 0.3 reduce_sum.9
  244.1 9.5 %psum.7 = f32[2048]{0:T(1024)S(1)} all-reduce(f32[2048]{0:T(1024)S(1)} %broadcast_select_fusion), channel_id=1, replica_groups=mesh['dom'=128,'col'=2] {'col'}, use_global_device_ids=true, to_apply=%region_3.0 | all-reduce | flops 2048 | bytes 16384 | tf_op jit(solution)/shard_map/psum | solution.py:173
  253.6 0.6 broadcast_multiply_fusion
  (43 shorter events, 1.8 us)
Async XLA Ops:
  0.6 4.2 %copy-start.12 = (s32[1,128]{1,0:T(1,128)S(1)}, s32[1,128]{1,0:T(1,128)}, u32[]{:S(2)}) copy-start(s32[1,128]{1,0:T(1,128)} %param.8) | copy-start | bytes 1540
  1.4 3.6 %copy-start.11 = (s32[2048]{0:T(1024)S(1)}, s32[2048]{0:T(1024)}, u32[]{:S(2)}) copy-start(s32[2048]{0:T(1024)} %param.6) | copy-start | bytes 24580
  4.8 18.0 %copy-start.9 = (s32[2048]{0:T(1024)S(1)}, s32[2048]{0:T(1024)}, u32[]{:S(2)}) copy-start(s32[2048]{0:T(1024)} %a_ref.3) | copy-start | bytes 24580
  6.4 46.6 %all-to-all-start = ((f32[128,9,128]{2,1,0:T(8,128)}), f32[128,9,128]{2,1,0:T(8,128)S(1)}, u32[]{:S(2)}, u32[]{:S(2)}) async-start(f32[128,9,128]{2,1,0:T(8,128)} %maximum_maximum_fusion), calls=%async_computation | async-start | bytes 2097152 | tf_op jit(solution)/shard_map/all_to_all | solution.py:95
  53.9 1.7 copy-start.7
  55.5 14.1 %copy-start = (f32[4096,1,128]{2,1,0:T(1,128)S(1)}, f32[4096,1,128]{2,1,0:T(1,128)}, u32[]{:S(2)}) copy-start(f32[4096,1,128]{2,1,0:T(1,128)} %shard_map.68) | copy-start | bytes 6291460
  73.0 2.0 copy-start.1
  80.8 35.1 %copy-start.6 = (f32[2048,1,128]{2,1,0:T(1,128)S(1)}, f32[2048,1,128]{2,1,0:T(1,128)}, u32[]{:S(2)}) copy-start(f32[2048,1,128]{2,1,0:T(1,128)} %shard_map.70) | copy-start | bytes 3145732
  141.9 2.0 copy-start.4
  143.9 13.3 %copy-start.8 = (s32[2048]{0:T(1024)S(1)}, s32[2048]{0:T(1024)}, u32[]{:S(2)}) copy-start(s32[2048]{0:T(1024)} %copy-done.7) | copy-start | bytes 24580
  149.7 33.5 %copy-start.5 = (f32[2048,1,128]{2,1,0:T(1,128)S(1)}, f32[2048,1,128]{2,1,0:T(1,128)}, u32[]{:S(2)}) copy-start(f32[2048,1,128]{2,1,0:T(1,128)} %shard_map.73) | copy-start | bytes 3145732
  149.7 33.5 %all-to-all-start.2 = ((f32[2048,1,128]{2,1,0:T(1,128)}), f32[2048,1,128]{2,1,0:T(1,128)}, u32[]{:S(2)}, u32[]{:S(2)}) async-start(f32[2048,1,128]{2,1,0:T(1,128)} %shard_map.73), calls=%async_computation.2 | async-start | bytes 2097152 | tf_op jit(solution)/shard_map/all_to_all | solution.py:95
  213.2 2.0 copy-start.2
  215.1 10.7 %copy-start.10 = (s32[2048]{0:T(1024)S(1)}, s32[2048]{0:T(1024)}, u32[]{:S(2)}) copy-start(s32[2048]{0:T(1024)} %a_ref.3) | copy-start | bytes 24580
  215.1 12.3 %copy-start.3 = (f32[4096,64]{1,0:T(8,128)S(1)}, f32[4096,64]{1,0:T(8,128)}, u32[]{:S(2)}) copy-start(f32[4096,64]{1,0:T(8,128)} %copy-done.2) | copy-start | bytes 3145732
  219.3 21.7 %all-to-all-start.3 = ((f32[1024,1,128]{2,1,0:T(1,128)}), f32[1024,1,128]{2,1,0:T(1,128)S(1)}, u32[]{:S(2)}, u32[]{:S(2)}) async-start(f32[1024,1,128]{2,1,0:T(1,128)} %shard_map.77), calls=%async_computation.3 | async-start | bytes 1048576 | tf_op jit(solution)/shard_map/all_to_all | solution.py:95

commit v10 on v7

--- a/solution.py
+++ b/solution.py
@@ -137,6 +137,8 @@
     diag = ((1.0 + degree_boost) * degree + ground_shift)[:, None]
     extra = (degree_boost * degree + ground_shift)[:, None]
 
+    weights = jnp.concatenate([w_out[:, None] * ones, w_in[:, None] * ones], axis=1)
+
     def ends(field):
         doubled = jnp.concatenate([field, field], axis=1).reshape(VERT_DEV, 1, 2 * width)
         return pair_gather(src_local, wanted, doubled)
@@ -145,9 +147,8 @@
         here = ends(field)
         there = a2a(here).reshape(edges, 2 * width)
         here = here.reshape(edges, 2 * width)
-        flow_out = w_out[:, None] * (here[:, :width] - there[:, width:])
-        flow_in = w_in[:, None] * (there[:, :width] - here[:, width:])
-        flows = jnp.concatenate([flow_out, -flow_in], axis=1).reshape(edges, 1, lanes)
+        swapped = jnp.concatenate([there[:, width:], there[:, :width]], axis=1)
+        flows = (weights * (here - swapped)).reshape(edges, 1, lanes)
         at_first = sorted_sum(key_0, slot_0, flows, VERT_DEV)
         at_second = sorted_sum(key_1, slot_1, flows, VERT_DEV)
         return (at_first[:, :width] + at_second[:, width:]) + extra * field

time: 255 us -> 272 us (1.067)
  local copies, waits for them, and re-layouts: 8.65 us -> 23.3 us
  other arithmetic: 48.3 us -> 52.2 us
    mul x2, other arithmetic: 3.98 us -> 10.5 us  [apply(): flows = (weights * (here - swapped)).reshape(edges, 1, lanes)]
    mul x1 -> x2, local copies, waits for them, and re-layouts: 0.32 us -> 6.05 us  [local(): w_out[:, None] * ones]
    mul x2 -> x3, local copies, waits for them, and re-layouts: 0.41 us -> 6.14 us  [local(): w_in[:, None] * ones]
  transfers between devices with their start and end apart: 3 -> 3, of which waited for: 3 -> 3; matrix products, arithmetic and copies ran while one was open for 5% -> 4% of each run, Pallas kernels for 5% -> 5%
where the time goes in v10:
time: 272 us; the launch traced here: 271 us
  Pallas kernels  73.8 us (27%)
  other arithmetic  52.2 us (19%)
  waiting for transfers between devices  47.4 us (17%)
  blocking collectives  44.4 us (16%)
  starting transfers between devices  29.1 us (11%)
  local copies, waits for them, and re-layouts  23.3 us (9%)
    pallas_call x6, Pallas kernels, sorted_sum(): pl.pallas_call(_runs_kernel, out_shape=jax.ShapeDtypeStruct((rows,) + val...  54 us
    all_to_all x3, waiting for transfers between devices, a2a(): return lax.all_to_all(x, 'dom', split_axis=0, concat_axis=0, tiled=True)  47.4 us
    all_to_all x1, blocking collectives, a2a(): return lax.all_to_all(x, 'dom', split_axis=0, concat_axis=0, tiled=True)  34.9 us
    all_to_all x3, starting transfers between devices, a2a(): return lax.all_to_all(x, 'dom', split_axis=0, concat_axis=0, tiled=True)  29.1 us
    pallas_call x4, Pallas kernels, pair_gather(): pl.pallas_call(_pair_gather_kernel, out_shape=jax.ShapeDtypeStruct((a.sha...  19.8 us
    mul x2, other arithmetic, apply(): flows = (weights * (here - swapped)).reshape(edges, 1, lanes)  10.5 us
    psum x1, blocking collectives, local(): resistance = lax.psum(partial_sum, 'col') / SKETCH  9.53 us
    add x1, other arithmetic, local(): solution = solution + direction  6.18 us
  transfers between devices with their start and end apart: 3, of which 3 were waited for; matrix products, arithmetic and copies ran while one was open for 4% of the time, Pallas kernels for 5%

profile of v10, /device:TPU:1, one launch (start us, length us, event | category | flops | bytes accessed | tf_op | source)
XLA Modules:
  0.0 271.2 jit_solution(9605302881627802312)
XLA Ops:
  0.6 0.8 iota_compare_fusion
  1.6 0.8 reshape.162
  2.3 0.7 fusion.11
  3.0 1.2 copy.33
  5.3 1.2 maximum_maximum_fusion
  6.4 16.3 %all-to-all-start = ((f32[128,9,128]{2,1,0:T(8,128)}), f32[128,9,128]{2,1,0:T(8,128)S(1)}, u32[]{:S(2)}, u32[]{:S(2)}) async-start(f32[128,9,128]{2,1,0:T(8,128)} %maximum_maximum_fusion), calls=%async_computation | async-start | bytes 2097152 | tf_op jit(solution)/shard_map/all_to_all | solution.py:95
  22.8 5.0 %sort.30 = (s32[2048]{0:T(1024)}, s32[2048]{0:T(1024)}) sort(s32[2048]{0:T(1024)S(1)} %copy-done.13, s32[2048]{0:T(1024)S(1)} %iota.14), dimensions={0}, to_apply=%region_0.0 | sort | flops 22528 | bytes 32768 | tf_op jit(solution)/shard_map/sort | solution.py:104
  28.2 1.3 pad_maximum_fusion.3
  29.5 9.0 %shard_map.68 = f32[4096,1,128]{2,1,0:T(1,128)} custom-call(s32[2048]{0:T(1024)} %get-tuple-element.6.key_ref, s32[2048]{0:T(1024)} %get-tuple-element.7.slot_ref, f32[2048,1,128]{2,1,0:T(1,128)} %bitcast.53), custom_call_target="tpu_custom_call" | custom-call | tf_op jit(solution)/shard_map/pallas_call | solution.py:76
  38.5 14.6 %all-to-all-done = f32[128,9,128]{2,1,0:T(8,128)S(1)} async-done(((f32[128,9,128]{2,1,0:T(8,128)}), f32[128,9,128]{2,1,0:T(8,128)S(1)}, u32[]{:S(2)}, u32[]{:S(2)}) %all-to-all-start) | async-done | bytes 589856 | tf_op jit(solution)/shard_map/all_to_all | solution.py:95
  54.2 1.3 pad_maximum_fusion.4
  55.5 5.0 %sort.31 = (s32[2048]{0:T(1024)}, s32[2048]{0:T(1024)}) sort(s32[2048]{0:T(1024)S(1)} %convert_element_type.16.b_ref, s32[2048]{0:T(1024)S(1)} %iota.15), dimensions={0}, to_apply=%region_1.0 | sort | flops 22528 | bytes 32768 | tf_op jit(solution)/shard_map/sort | solution.py:126
  60.6 9.0 %shard_map.69 = f32[4096,1,128]{2,1,0:T(1,128)} custom-call(s32[2048]{0:T(1024)} %get-tuple-element.8.key_ref, s32[2048]{0:T(1024)} %get-tuple-element.9.slot_ref, f32[2048,1,128]{2,1,0:T(1,128)} %bitcast.52), custom_call_target="tpu_custom_call" | custom-call | tf_op jit(solution)/shard_map/pallas_call | solution.py:76
  69.6 4.0 %add_reduce_fusion = (f32[4096]{0:T(1024)S(1)}, f32[4096]{0:T(1024)S(1)}) fusion(f32[4096,128]{1,0:T(8,128)} %bitcast.35, f32[4096,128]{1,0:T(8,128)S(1)} %bitcast.31), kind=kLoop, calls=%fused_computation.16 | loop fusion | flops 20480 | bytes 65536 | tf_op jit(solution)/shard_map/add | solution.py:138
  73.6 0.7 broadcast_divide_fusion
  74.3 2.0 pad_maximum_fusion
  76.4 5.8 %shard_map.70 = f32[2048,1,128]{2,1,0:T(1,128)} custom-call(s32[2048]{0:T(1024)} %a_ref.3, s32[2048]{0:T(1024)} %copy-done.11, f32[4096,1,128]{2,1,0:T(1,128)} %bitcast.49), custom_call_target="tpu_custom_call" | custom-call | tf_op jit(solution)/shard_map/pallas_call | solution.py:35
  82.2 34.9 %all_to_all.20 = f32[2048,1,128]{2,1,0:T(1,128)S(1)} all-to-all(f32[2048,1,128]{2,1,0:T(1,128)} %shard_map.70), channel_id=1, replica_groups=mesh['dom'=128,'col'=2] {'dom'}, dimensions={0} | all-to-all | bytes 2097152 | tf_op jit(solution)/shard_map/all_to_all | solution.py:95
  117.4 5.7 %mul.122 = f32[2048,1,64]{2,1,0:T(1,128)S(1)} broadcast(f32[2048]{0:T(1024)S(1)} %mul.115), dimensions={0} | broadcast | bytes 532480 | tf_op jit(solution)/shard_map/mul | solution.py:130
  123.2 5.7 %mul.121 = f32[2048,1,64]{2,1,0:T(1,128)S(1)} broadcast(f32[2048]{0:T(1024)S(1)} %get-tuple-element.21), dimensions={0} | broadcast | bytes 532480 | tf_op jit(solution)/shard_map/mul | solution.py:108
  129.0 1.0 copy-done.9
  129.9 5.3 %fusion.8.v_ref = f32[2048,1,128]{2,1,0:T(1,128)} fusion(f32[2048,1,128]{2,1,0:T(1,128)S(1)} %copy-done.6, f32[2048,1,64]{2,1,0:T(1,128)S(1)} %bitcast.55, f32[2048,1,64]{2,1,0:T(1,128)S(1)} %bitcast.54, f32[2048,1,64]{2,1,0:T(1,128)S(1)} %mul.122, f32[2048,1,64]{2,1,0:T(1,128)S(1)} %mul.121), kind=kLoop, calls=%fused_computation.23 | loop fusion | flops 1048576 | bytes 4194304 | tf_op jit(solution)/shard_map/mul | solution.py:151
  135.2 9.0 %shard_map.71 = f32[4096,1,128]{2,1,0:T(1,128)} custom-call(s32[2048]{0:T(1024)} %get-tuple-element.6.key_ref, s32[2048]{0:T(1024)} %get-tuple-element.7.slot_ref, f32[2048,1,128]{2,1,0:T(1,128)} %fusion.8.v_ref), custom_call_target="tpu_custom_call" | custom-call | tf_op jit(solution)/shard_map/pallas_call | solution.py:76
  144.2 9.0 %shard_map.72 = f32[4096,1,128]{2,1,0:T(1,128)} custom-call(s32[2048]{0:T(1024)} %get-tuple-element.8.key_ref, s32[2048]{0:T(1024)} %get-tuple-element.9.slot_ref, f32[2048,1,128]{2,1,0:T(1,128)} %fusion.8.v_ref), custom_call_target="tpu_custom_call" | custom-call | tf_op jit(solution)/shard_map/pallas_call | solution.py:76
  153.2 5.0 %divide_add_fusion = f32[4096,64]{1,0:T(8,128)S(1)} fusion(f32[4096,64]{1,0:T(8,128)} %copy-done.2, f32[4096]{0:T(1024)S(1)} %get-tuple-element.19, f32[4096]{0:T(1024)S(1)} %get-tuple-element.18, f32[4096,128]{1,0:T(8,128)} %bitcast.44, f32[4096,128]{1,0:T(8,128)} %bitcast.42, f32[4096,128]{1,0:T(8,128)} %bitcast.36, f32[4096,128]{1,0:T(8,128)S(1)} %bitcast.33), kind=kLoop, calls=%fused_computation.15 | loop fusion | flops 2359296 | bytes 6324224 | tf_op jit(solution)/shard_map/add | solution.py:167
  158.2 2.0 pad_maximum_fusion.1
  160.2 5.8 %shard_map.73 = f32[2048,1,128]{2,1,0:T(1,128)} custom-call(s32[2048]{0:T(1024)} %a_ref.3, s32[2048]{0:T(1024)} %copy-done.11, f32[4096,1,128]{2,1,0:T(1,128)} %bitcast.48), custom_call_target="tpu_custom_call" | custom-call | tf_op jit(solution)/shard_map/pallas_call | solution.py:35
  166.1 6.4 %all-to-all-start.2 = ((f32[2048,1,128]{2,1,0:T(1,128)}), f32[2048,1,128]{2,1,0:T(1,128)S(1)}, u32[]{:S(2)}, u32[]{:S(2)}) async-start(f32[2048,1,128]{2,1,0:T(1,128)} %shard_map.73), calls=%async_computation.2 | async-start | bytes 2097152 | tf_op jit(solution)/shard_map/all_to_all | solution.py:95
  172.5 0.8 slice.74.a_ref
  173.3 0.8 slice.75.b_ref
  174.1 24.7 %all-to-all-done.2 = f32[2048,1,128]{2,1,0:T(1,128)S(1)} async-done(((f32[2048,1,128]{2,1,0:T(1,128)}), f32[2048,1,128]{2,1,0:T(1,128)S(1)}, u32[]{:S(2)}, u32[]{:S(2)}) %all-to-all-start.2) | async-done | bytes 1048608 | tf_op jit(solution)/shard_map/all_to_all | solution.py:95
  199.1 0.9 copy-done.5
  200.6 5.3 %fusion.9.v_ref = f32[2048,1,128]{2,1,0:T(1,128)} fusion(f32[2048,1,128]{2,1,0:T(1,128)S(1)} %copy-done.5, f32[2048,1,64]{2,1,0:T(1,128)S(1)} %bitcast.57, f32[2048,1,64]{2,1,0:T(1,128)S(1)} %bitcast.56, f32[2048,1,64]{2,1,0:T(1,128)S(1)} %copy-done.8, f32[2048,1,64]{2,1,0:T(1,128)S(1)} %copy-done.10), kind=kLoop, calls=%fused_computation.25 | loop fusion | flops 1048576 | bytes 4194304 | tf_op jit(solution)/shard_map/mul | solution.py:151
  205.9 9.1 %shard_map.74 = f32[4096,1,128]{2,1,0:T(1,128)} custom-call(s32[2048]{0:T(1024)} %get-tuple-element.6.key_ref, s32[2048]{0:T(1024)} %get-tuple-element.7.slot_ref, f32[2048,1,128]{2,1,0:T(1,128)} %fusion.9.v_ref), custom_call_target="tpu_custom_call" | custom-call | tf_op jit(solution)/shard_map/pallas_call | solution.py:76
  214.9 9.0 %shard_map.75 = f32[4096,1,128]{2,1,0:T(1,128)} custom-call(s32[2048]{0:T(1024)} %get-tuple-element.8.key_ref, s32[2048]{0:T(1024)} %get-tuple-element.9.slot_ref, f32[2048,1,128]{2,1,0:T(1,128)} %fusion.9.v_ref), custom_call_target="tpu_custom_call" | custom-call | tf_op jit(solution)/shard_map/pallas_call | solution.py:76
  223.9 6.2 %fusion.5 = f32[4096,64]{1,0:T(8,128)S(1)} fusion(f32[4096,128]{1,0:T(8,128)} %bitcast.51, f32[4096,128]{1,0:T(8,128)} %bitcast.50, f32[4096,64]{1,0:T(8,128)} %copy-done.2, f32[4096]{0:T(1024)S(1)} %get-tuple-element.18, f32[4096]{0:T(1024)S(1)} %get-tuple-element.19, f32[4096,128]{1,0:T(8,128)} %bitcast.45, f32[4096,128]{1,0:T(8,128)} %bitcast.43, ...), kind=kLoop, calls=%fused_computation.6 | loop fusion | flops 4980736 | bytes 8421376 | tf_op jit(solution)/shard_map/add | solution.py:163
  230.1 2.0 pad_maximum_fusion.2
  232.1 4.2 %shard_map.77 = f32[1024,1,128]{2,1,0:T(1,128)} custom-call(s32[1024]{0:T(1024)} %slice.74.a_ref, s32[1024]{0:T(1024)} %slice.75.b_ref, f32[4096,1,128]{2,1,0:T(1,128)} %bitcast.39), custom_call_target="tpu_custom_call" | custom-call | tf_op jit(solution)/shard_map/pallas_call | solution.py:35
  236.2 6.3 %all-to-all-start.3 = ((f32[1024,1,128]{2,1,0:T(1,128)}), f32[1024,1,128]{2,1,0:T(1,128)S(1)}, u32[]{:S(2)}, u32[]{:S(2)}) async-start(f32[1024,1,128]{2,1,0:T(1,128)} %shard_map.77), calls=%async_computation.3 | async-start | bytes 1048576 | tf_op jit(solution)/shard_map/all_to_all | solution.py:95
  242.6 0.8 slice.72.a_ref
  243.4 0.8 slice.73.b_ref
  244.2 1.6 copy.41
  245.7 4.0 %shard_map.76 = f32[1024,1,128]{2,1,0:T(1,128)} custom-call(s32[1024]{0:T(1024)} %slice.72.a_ref, s32[1024]{0:T(1024)} %slice.73.b_ref, f32[4096,1,128]{2,1,0:T(1,128)} %bitcast.40), custom_call_target="tpu_custom_call" | custom-call | tf_op jit(solution)/shard_map/pallas_call | solution.py:35
  249.7 8.2 %all-to-all-done.3 = f32[1024,1,128]{2,1,0:T(1,128)S(1)} async-done(((f32[1024,1,128]{2,1,0:T(1,128)}), f32[1024,1,128]{2,1,0:T(1,128)S(1)}, u32[]{:S(2)}, u32[]{:S(2)}) %all-to-all-start.3) | async-done | bytes 524320 | tf_op jit(solution)/shard_map/all_to_all | solution.py:95
  257.9 2.6 multiply_reduce_fusion
  260.7 0.3 reduce_sum.9
  261.0 9.5 %psum.7 = f32[2048]{0:T(1024)S(1)} all-reduce(f32[2048]{0:T(1024)S(1)} %broadcast_select_fusion), channel_id=1, replica_groups=mesh['dom'=128,'col'=2] {'col'}, use_global_device_ids=true, to_apply=%region_3.0 | all-reduce | flops 2048 | bytes 16384 | tf_op jit(solution)/shard_map/psum | solution.py:174
  270.6 0.6 broadcast_multiply_fusion
  (54 shorter events, 4.0 us)
Async XLA Ops:
  0.6 4.2 %copy-start.16 = (s32[1,128]{1,0:T(1,128)S(1)}, s32[1,128]{1,0:T(1,128)}, u32[]{:S(2)}) copy-start(s32[1,128]{1,0:T(1,128)} %param.8) | copy-start | bytes 1540
  1.4 3.6 %copy-start.15 = (s32[2048]{0:T(1024)S(1)}, s32[2048]{0:T(1024)}, u32[]{:S(2)}) copy-start(s32[2048]{0:T(1024)} %param.6) | copy-start | bytes 24580
  4.8 18.0 %copy-start.13 = (s32[2048]{0:T(1024)S(1)}, s32[2048]{0:T(1024)}, u32[]{:S(2)}) copy-start(s32[2048]{0:T(1024)} %a_ref.3) | copy-start | bytes 24580
  6.4 46.6 %all-to-all-start = ((f32[128,9,128]{2,1,0:T(8,128)}), f32[128,9,128]{2,1,0:T(8,128)S(1)}, u32[]{:S(2)}, u32[]{:S(2)}) async-start(f32[128,9,128]{2,1,0:T(8,128)} %maximum_maximum_fusion), calls=%async_computation | async-start | bytes 2097152 | tf_op jit(solution)/shard_map/all_to_all | solution.py:95
  53.9 1.7 copy-start.11
  55.5 14.1 %copy-start = (f32[4096,1,128]{2,1,0:T(1,128)S(1)}, f32[4096,1,128]{2,1,0:T(1,128)}, u32[]{:S(2)}) copy-start(f32[4096,1,128]{2,1,0:T(1,128)} %shard_map.68) | copy-start | bytes 6291460
  69.6 4.0 %copy-start.1 = (f32[4096,1,128]{2,1,0:T(1,128)S(1)}, f32[4096,1,128]{2,1,0:T(1,128)}, u32[]{:S(2)}) copy-start(f32[4096,1,128]{2,1,0:T(1,128)} %shard_map.69) | copy-start | bytes 6291460
  74.3 2.0 copy-start.2
  117.4 12.5 %copy-start.6 = (f32[2048,1,128]{2,1,0:T(1,128)S(1)}, f32[2048,1,128]{2,1,0:T(1,128)}, u32[]{:S(2)}) copy-start(f32[2048,1,128]{2,1,0:T(1,128)} %shard_map.70) | copy-start | bytes 3145732
  123.2 5.8 %copy-start.7 = (f32[2048,1,64]{2,1,0:T(1,128)}, f32[2048,1,64]{2,1,0:T(1,128)S(1)}, u32[]{:S(2)}) copy-start(f32[2048,1,64]{2,1,0:T(1,128)S(1)} %mul.122) | copy-start | bytes 1572868
  128.9 1.0 copy-start.9
  160.2 12.2 %copy-start.12 = (s32[2048]{0:T(1024)S(1)}, s32[2048]{0:T(1024)}, u32[]{:S(2)}) copy-start(s32[2048]{0:T(1024)} %copy-done.11) | copy-start | bytes 24580
  166.1 32.7 %all-to-all-start.2 = ((f32[2048,1,128]{2,1,0:T(1,128)}), f32[2048,1,128]{2,1,0:T(1,128)S(1)}, u32[]{:S(2)}, u32[]{:S(2)}) async-start(f32[2048,1,128]{2,1,0:T(1,128)} %shard_map.73), calls=%async_computation.2 | async-start | bytes 2097152 | tf_op jit(solution)/shard_map/all_to_all | solution.py:95
  198.8 1.2 copy-start.5
  198.8 1.5 copy-start.8
  198.8 1.9 copy-start.10
  230.1 2.0 copy-start.3
  232.1 10.5 %copy-start.14 = (s32[2048]{0:T(1024)S(1)}, s32[2048]{0:T(1024)}, u32[]{:S(2)}) copy-start(s32[2048]{0:T(1024)} %a_ref.3) | copy-start | bytes 24580
  232.1 12.1 %copy-start.4 = (f32[4096,64]{1,0:T(8,128)S(1)}, f32[4096,64]{1,0:T(8,128)}, u32[]{:S(2)}) copy-start(f32[4096,64]{1,0:T(8,128)} %copy-done.3) | copy-start | bytes 3145732
  236.2 21.7 %all-to-all-start.3 = ((f32[1024,1,128]{2,1,0:T(1,128)}), f32[1024,1,128]{2,1,0:T(1,128)S(1)}, u32[]{:S(2)}, u32[]{:S(2)}) async-start(f32[1024,1,128]{2,1,0:T(1,128)} %shard_map.77), calls=%async_computation.3 | async-start | bytes 1048576 | tf_op jit(solution)/shard_map/all_to_all | solution.py:95

commit v11 on v7

--- a/solution.py
+++ b/solution.py
@@ -170,7 +170,8 @@
     near = pair_gather(src_local[0::2], src_local[1::2], doubled).reshape(edges, width)
     diff = near - far
     partial_sum = jnp.sum(diff * diff, axis=1) * live.reshape(-1)
-    resistance = lax.psum(partial_sum, "col") / SKETCH
+    other = lax.ppermute(partial_sum, "col", [(0, 1), (1, 0)])
+    resistance = (partial_sum + other) / SKETCH
     return (solution.T, resistance)
 
 

time: 255 us -> 256 us (level)
  blocking collectives: 44.6 us -> 35 us
  starting transfers between devices: 30.3 us -> 37.6 us
    psum x1 -> x0, blocking collectives: 9.53 us -> none  [local(): resistance = lax.psum(partial_sum, 'col') / SKETCH]
    ppermute x0 -> x1, starting transfers between devices: none -> 7.46 us  [local(): other = lax.ppermute(partial_sum, 'col', [(0, 1), (1, 0)])]
  transfers between devices with their start and end apart: 3 -> 4, of which waited for: 3 -> 3; matrix products, arithmetic and copies ran while one was open for 5% -> 4% of each run, Pallas kernels for 5% -> 5%
where the time goes in v11:
time: 256 us; the launch traced here: 255 us
  Pallas kernels  73.7 us (29%)
  other arithmetic  49 us (19%)
  waiting for transfers between devices  48.8 us (19%)
  starting transfers between devices  37.6 us (15%)
  blocking collectives  35 us (14%)
  local copies, waits for them, and re-layouts  9.69 us (4%)
    pallas_call x6, Pallas kernels, sorted_sum(): pl.pallas_call(_runs_kernel, out_shape=jax.ShapeDtypeStruct((rows,) + val...  54 us
    all_to_all x3, waiting for transfers between devices, a2a(): return lax.all_to_all(x, 'dom', split_axis=0, concat_axis=0, tiled=True)  48.7 us
    all_to_all x1, blocking collectives, a2a(): return lax.all_to_all(x, 'dom', split_axis=0, concat_axis=0, tiled=True)  35 us
    all_to_all x3, starting transfers between devices, a2a(): return lax.all_to_all(x, 'dom', split_axis=0, concat_axis=0, tiled=True)  30.1 us
    pallas_call x4, Pallas kernels, pair_gather(): pl.pallas_call(_pair_gather_kernel, out_shape=jax.ShapeDtypeStruct((a.sha...  19.7 us
    ppermute x1, starting transfers between devices, local(): other = lax.ppermute(partial_sum, 'col', [(0, 1), (1, 0)])  7.46 us
    add x1, other arithmetic, local(): solution = solution + direction  6.18 us
  transfers between devices with their start and end apart: 4, of which 3 were waited for; matrix products, arithmetic and copies ran while one was open for 4% of the time, Pallas kernels for 5%

profile of v11, /device:TPU:1, one launch (start us, length us, event | category | flops | bytes accessed | tf_op | source)
XLA Modules:
  0.0 254.7 jit_solution(9487471920920830964)
XLA Ops:
  0.6 0.8 iota_compare_fusion
  1.6 0.8 reshape.144
  2.3 0.7 fusion.15
  3.0 1.2 copy.39
  4.3 0.3 multiply_bitcast_fusion
  5.3 1.2 maximum_maximum_fusion
  6.4 16.3 %all-to-all-start = ((f32[128,9,128]{2,1,0:T(8,128)}), f32[128,9,128]{2,1,0:T(8,128)S(1)}, u32[]{:S(2)}, u32[]{:S(2)}) async-start(f32[128,9,128]{2,1,0:T(8,128)} %maximum_maximum_fusion), calls=%async_computation | async-start | bytes 2097152 | tf_op jit(solution)/shard_map/all_to_all | solution.py:95
  22.8 5.0 %sort.30 = (s32[2048]{0:T(1024)}, s32[2048]{0:T(1024)}) sort(s32[2048]{0:T(1024)S(1)} %copy-done.9, s32[2048]{0:T(1024)S(1)} %iota.14), dimensions={0}, to_apply=%region_0.0 | sort | flops 22528 | bytes 32768 | tf_op jit(solution)/shard_map/sort | solution.py:104
  28.2 1.3 pad_maximum_fusion.3
  29.5 9.0 %shard_map.68 = f32[4096,1,128]{2,1,0:T(1,128)} custom-call(s32[2048]{0:T(1024)} %get-tuple-element.6.key_ref, s32[2048]{0:T(1024)} %get-tuple-element.7.slot_ref, f32[2048,1,128]{2,1,0:T(1,128)} %bitcast.60), custom_call_target="tpu_custom_call" | custom-call | tf_op jit(solution)/shard_map/pallas_call | solution.py:76
  38.5 14.6 %all-to-all-done = f32[128,9,128]{2,1,0:T(8,128)S(1)} async-done(((f32[128,9,128]{2,1,0:T(8,128)}), f32[128,9,128]{2,1,0:T(8,128)S(1)}, u32[]{:S(2)}, u32[]{:S(2)}) %all-to-all-start) | async-done | bytes 589856 | tf_op jit(solution)/shard_map/all_to_all | solution.py:95
  54.2 1.3 pad_maximum_fusion.4
  55.5 5.0 %sort.31 = (s32[2048]{0:T(1024)}, s32[2048]{0:T(1024)}) sort(s32[2048]{0:T(1024)S(1)} %convert_element_type.16.b_ref, s32[2048]{0:T(1024)S(1)} %iota.15), dimensions={0}, to_apply=%region_1.0 | sort | flops 22528 | bytes 32768 | tf_op jit(solution)/shard_map/sort | solution.py:126
  60.6 9.0 %shard_map.69 = f32[4096,1,128]{2,1,0:T(1,128)} custom-call(s32[2048]{0:T(1024)} %get-tuple-element.8.key_ref, s32[2048]{0:T(1024)} %get-tuple-element.9.slot_ref, f32[2048,1,128]{2,1,0:T(1,128)} %bitcast.59), custom_call_target="tpu_custom_call" | custom-call | tf_op jit(solution)/shard_map/pallas_call | solution.py:76
  69.6 4.0 %add_reduce_fusion = (f32[4096]{0:T(1024)S(1)}, f32[4096]{0:T(1024)S(1)}) fusion(f32[4096,128]{1,0:T(8,128)} %bitcast.37, f32[4096,128]{1,0:T(8,128)S(1)} %bitcast.33), kind=kLoop, calls=%fused_computation.16 | loop fusion | flops 20480 | bytes 65536 | tf_op jit(solution)/shard_map/add | solution.py:138
  73.6 0.7 broadcast_divide_fusion
  74.3 2.0 pad_maximum_fusion
  76.4 5.8 %shard_map.70 = f32[2048,1,128]{2,1,0:T(1,128)} custom-call(s32[2048]{0:T(1024)} %a_ref.3, s32[2048]{0:T(1024)} %copy-done.7, f32[4096,1,128]{2,1,0:T(1,128)} %bitcast.56), custom_call_target="tpu_custom_call" | custom-call | tf_op jit(solution)/shard_map/pallas_call | solution.py:35
  82.2 35.0 %all_to_all.20 = f32[2048,1,128]{2,1,0:T(1,128)S(1)} all-to-all(f32[2048,1,128]{2,1,0:T(1,128)} %shard_map.70), channel_id=1, replica_groups=mesh['dom'=128,'col'=2] {'dom'}, dimensions={0} | all-to-all | bytes 2097152 | tf_op jit(solution)/shard_map/all_to_all | solution.py:95
  117.2 1.2 fusion.13
  118.5 1.3 pad_maximum_fusion.5
  119.8 9.0 %shard_map.71 = f32[4096,1,128]{2,1,0:T(1,128)} custom-call(s32[2048]{0:T(1024)} %get-tuple-element.6.key_ref, s32[2048]{0:T(1024)} %get-tuple-element.7.slot_ref, f32[2048,1,128]{2,1,0:T(1,128)} %bitcast.52), custom_call_target="tpu_custom_call" | custom-call | tf_op jit(solution)/shard_map/pallas_call | solution.py:76
  128.8 9.0 %shard_map.72 = f32[4096,1,128]{2,1,0:T(1,128)} custom-call(s32[2048]{0:T(1024)} %get-tuple-element.8.key_ref, s32[2048]{0:T(1024)} %get-tuple-element.9.slot_ref, f32[2048,1,128]{2,1,0:T(1,128)} %bitcast.53), custom_call_target="tpu_custom_call" | custom-call | tf_op jit(solution)/shard_map/pallas_call | solution.py:76
  137.8 5.0 %divide_add_fusion = f32[4096,64]{1,0:T(8,128)S(1)} fusion(f32[4096,64]{1,0:T(8,128)} %copy-done.2, f32[4096]{0:T(1024)S(1)} %get-tuple-element.19, f32[4096]{0:T(1024)S(1)} %get-tuple-element.18, f32[4096,128]{1,0:T(8,128)} %bitcast.46, f32[4096,128]{1,0:T(8,128)} %bitcast.44, f32[4096,128]{1,0:T(8,128)} %bitcast.38, f32[4096,128]{1,0:T(8,128)S(1)} %bitcast.35), kind=kLoop, calls=%fused_computation.15 | loop fusion | flops 2359296 | bytes 6324224 | tf_op jit(solution)/shard_map/add | solution.py:166
  142.8 2.0 pad_maximum_fusion.1
  144.8 5.8 %shard_map.73 = f32[2048,1,128]{2,1,0:T(1,128)} custom-call(s32[2048]{0:T(1024)} %a_ref.3, s32[2048]{0:T(1024)} %copy-done.7, f32[4096,1,128]{2,1,0:T(1,128)} %bitcast.55), custom_call_target="tpu_custom_call" | custom-call | tf_op jit(solution)/shard_map/pallas_call | solution.py:35
  150.7 7.4 %all-to-all-start.2 = ((f32[2048,1,128]{2,1,0:T(1,128)}), f32[2048,1,128]{2,1,0:T(1,128)}, u32[]{:S(2)}, u32[]{:S(2)}) async-start(f32[2048,1,128]{2,1,0:T(1,128)} %shard_map.73), calls=%async_computation.2 | async-start | bytes 2097152 | tf_op jit(solution)/shard_map/all_to_all | solution.py:95
  158.1 0.8 slice.90.a_ref
  158.9 0.8 slice.91.b_ref
  159.7 24.5 %all-to-all-done.2 = f32[2048,1,128]{2,1,0:T(1,128)} async-done(((f32[2048,1,128]{2,1,0:T(1,128)}), f32[2048,1,128]{2,1,0:T(1,128)}, u32[]{:S(2)}, u32[]{:S(2)}) %all-to-all-start.2) | async-done | bytes 1048608 | tf_op jit(solution)/shard_map/all_to_all | solution.py:95
  184.2 2.7 %fusion.10 = (f32[2048,64]{1,0:T(8,128)S(1)}, f32[2048,64]{1,0:T(8,128)S(1)}) fusion(f32[2048,128]{1,0:T(8,128)} %bitcast.22, f32[2048,128]{1,0:T(8,128)S(1)} %bitcast.48, f32[2048]{0:T(1024)S(1)} %get-tuple-element.21, f32[2048]{0:T(1024)S(1)} %mul.121), kind=kLoop, calls=%fused_computation.22 | loop fusion | flops 655360 | bytes 3162112 | tf_op jit(solution)/shard_map/mul | solution.py:148
  187.0 1.3 pad_maximum_fusion.6
  188.3 9.1 %shard_map.74 = f32[4096,1,128]{2,1,0:T(1,128)} custom-call(s32[2048]{0:T(1024)} %get-tuple-element.6.key_ref, s32[2048]{0:T(1024)} %get-tuple-element.7.slot_ref, f32[2048,1,128]{2,1,0:T(1,128)} %bitcast.50), custom_call_target="tpu_custom_call" | custom-call | tf_op jit(solution)/shard_map/pallas_call | solution.py:76
  197.3 9.0 %shard_map.75 = f32[4096,1,128]{2,1,0:T(1,128)} custom-call(s32[2048]{0:T(1024)} %get-tuple-element.8.key_ref, s32[2048]{0:T(1024)} %get-tuple-element.9.slot_ref, f32[2048,1,128]{2,1,0:T(1,128)} %bitcast.51), custom_call_target="tpu_custom_call" | custom-call | tf_op jit(solution)/shard_map/pallas_call | solution.py:76
  206.3 6.2 %fusion.5 = f32[4096,64]{1,0:T(8,128)S(1)} fusion(f32[4096,128]{1,0:T(8,128)} %bitcast.58, f32[4096,128]{1,0:T(8,128)} %bitcast.57, f32[4096,64]{1,0:T(8,128)} %copy-done.2, f32[4096]{0:T(1024)S(1)} %get-tuple-element.18, f32[4096]{0:T(1024)S(1)} %get-tuple-element.19, f32[4096,128]{1,0:T(8,128)} %bitcast.47, f32[4096,128]{1,0:T(8,128)} %bitcast.45, ...), kind=kLoop, calls=%fused_computation.6 | loop fusion | flops 4980736 | bytes 8421376 | tf_op jit(solution)/shard_map/add | solution.py:162
  212.5 1.9 pad_maximum_fusion.2
  214.4 4.0 %shard_map.77 = f32[1024,1,128]{2,1,0:T(1,128)} custom-call(s32[1024]{0:T(1024)} %slice.90.a_ref, s32[1024]{0:T(1024)} %slice.91.b_ref, f32[4096,1,128]{2,1,0:T(1,128)} %bitcast.41), custom_call_target="tpu_custom_call" | custom-call | tf_op jit(solution)/shard_map/pallas_call | solution.py:35
  218.4 6.3 %all-to-all-start.3 = ((f32[1024,1,128]{2,1,0:T(1,128)}), f32[1024,1,128]{2,1,0:T(1,128)S(1)}, u32[]{:S(2)}, u32[]{:S(2)}) async-start(f32[1024,1,128]{2,1,0:T(1,128)} %shard_map.77), calls=%async_computation.3 | async-start | bytes 1048576 | tf_op jit(solution)/shard_map/all_to_all | solution.py:95
  224.8 0.8 slice.88.a_ref
  225.6 0.8 slice.89.b_ref
  226.4 4.0 %shard_map.76 = f32[1024,1,128]{2,1,0:T(1,128)} custom-call(s32[1024]{0:T(1024)} %slice.88.a_ref, s32[1024]{0:T(1024)} %slice.89.b_ref, f32[4096,1,128]{2,1,0:T(1,128)} %bitcast.42), custom_call_target="tpu_custom_call" | custom-call | tf_op jit(solution)/shard_map/pallas_call | solution.py:35
  230.4 9.7 %all-to-all-done.3 = f32[1024,1,128]{2,1,0:T(1,128)S(1)} async-done(((f32[1024,1,128]{2,1,0:T(1,128)}), f32[1024,1,128]{2,1,0:T(1,128)S(1)}, u32[]{:S(2)}, u32[]{:S(2)}) %all-to-all-start.3) | async-done | bytes 524320 | tf_op jit(solution)/shard_map/all_to_all | solution.py:95
  240.1 3.4 %multiply_reduce_fusion = f32[1024,128]{1,0:T(8,128)} fusion(f32[1024,1,128]{2,1,0:T(1,128)} %shard_map.76, f32[1024,1,128]{2,1,0:T(1,128)S(1)} %all-to-all-done.3), kind=kLoop, calls=%fused_computation.36 | loop fusion | flops 262144 | bytes 1572864 | tf_op jit(solution)/shard_map/mul | solution.py:172
  243.5 1.2 mul.144
  244.7 0.3 reduce_sum.9
  245.1 7.5 %collective-permute-start = (f32[2048]{0:T(1024)S(1)}, f32[2048]{0:T(1024)S(1)}, u32[]{:S(2)}, u32[]{:S(2)}) collective-permute-start(f32[2048]{0:T(1024)S(1)} %broadcast_select_fusion), channel_id=1, source_target_pairs={{0,1},{1,0},{2,3},{3,2},{4,5},{5,4},{6,7},{7,6},{8,9},{9,8},{10,11... | collective-permute-start | bytes 24584 | tf_op jit(solution)/shard_map/ppermute | solution.py:173
  252.5 1.6 copy.49
  254.1 0.6 add_multiply_fusion
  (45 shorter events, 2.2 us)
Async XLA Ops:
  0.6 4.2 %copy-start.12 = (s32[1,128]{1,0:T(1,128)S(1)}, s32[1,128]{1,0:T(1,128)}, u32[]{:S(2)}) copy-start(s32[1,128]{1,0:T(1,128)} %param.8) | copy-start | bytes 1540
  1.4 3.6 %copy-start.11 = (s32[2048]{0:T(1024)S(1)}, s32[2048]{0:T(1024)}, u32[]{:S(2)}) copy-start(s32[2048]{0:T(1024)} %param.6) | copy-start | bytes 24580
  4.8 18.0 %copy-start.9 = (s32[2048]{0:T(1024)S(1)}, s32[2048]{0:T(1024)}, u32[]{:S(2)}) copy-start(s32[2048]{0:T(1024)} %a_ref.3) | copy-start | bytes 24580
  6.4 46.6 %all-to-all-start = ((f32[128,9,128]{2,1,0:T(8,128)}), f32[128,9,128]{2,1,0:T(8,128)S(1)}, u32[]{:S(2)}, u32[]{:S(2)}) async-start(f32[128,9,128]{2,1,0:T(8,128)} %maximum_maximum_fusion), calls=%async_computation | async-start | bytes 2097152 | tf_op jit(solution)/shard_map/all_to_all | solution.py:95
  53.9 1.7 copy-start.7
  55.5 14.1 %copy-start = (f32[4096,1,128]{2,1,0:T(1,128)S(1)}, f32[4096,1,128]{2,1,0:T(1,128)}, u32[]{:S(2)}) copy-start(f32[4096,1,128]{2,1,0:T(1,128)} %shard_map.68) | copy-start | bytes 6291460
  69.6 4.0 %copy-start.1 = (f32[4096,1,128]{2,1,0:T(1,128)S(1)}, f32[4096,1,128]{2,1,0:T(1,128)}, u32[]{:S(2)}) copy-start(f32[4096,1,128]{2,1,0:T(1,128)} %shard_map.69) | copy-start | bytes 6291460
  74.3 2.0 copy-start.2
  82.2 35.1 %copy-start.6 = (f32[2048,1,128]{2,1,0:T(1,128)S(1)}, f32[2048,1,128]{2,1,0:T(1,128)}, u32[]{:S(2)}) copy-start(f32[2048,1,128]{2,1,0:T(1,128)} %shard_map.70) | copy-start | bytes 3145732
  144.8 13.3 %copy-start.8 = (s32[2048]{0:T(1024)S(1)}, s32[2048]{0:T(1024)}, u32[]{:S(2)}) copy-start(s32[2048]{0:T(1024)} %copy-done.7) | copy-start | bytes 24580
  150.7 33.5 %copy-start.5 = (f32[2048,1,128]{2,1,0:T(1,128)S(1)}, f32[2048,1,128]{2,1,0:T(1,128)}, u32[]{:S(2)}) copy-start(f32[2048,1,128]{2,1,0:T(1,128)} %shard_map.73) | copy-start | bytes 3145732
  150.7 33.5 %all-to-all-start.2 = ((f32[2048,1,128]{2,1,0:T(1,128)}), f32[2048,1,128]{2,1,0:T(1,128)}, u32[]{:S(2)}, u32[]{:S(2)}) async-start(f32[2048,1,128]{2,1,0:T(1,128)} %shard_map.73), calls=%async_computation.2 | async-start | bytes 2097152 | tf_op jit(solution)/shard_map/all_to_all | solution.py:95
  212.5 1.9 copy-start.3
  214.4 10.3 %copy-start.10 = (s32[2048]{0:T(1024)S(1)}, s32[2048]{0:T(1024)}, u32[]{:S(2)}) copy-start(s32[2048]{0:T(1024)} %a_ref.3) | copy-start | bytes 24580
  218.4 21.7 %all-to-all-start.3 = ((f32[1024,1,128]{2,1,0:T(1,128)}), f32[1024,1,128]{2,1,0:T(1,128)S(1)}, u32[]{:S(2)}, u32[]{:S(2)}) async-start(f32[1024,1,128]{2,1,0:T(1,128)} %shard_map.77), calls=%async_computation.3 | async-start | bytes 1048576 | tf_op jit(solution)/shard_map/all_to_all | solution.py:95
  230.4 22.2 %copy-start.4 = (f32[4096,64]{1,0:T(8,128)S(1)}, f32[4096,64]{1,0:T(8,128)}, u32[]{:S(2)}) copy-start(f32[4096,64]{1,0:T(8,128)} %copy-done.3) | copy-start | bytes 3145732
  245.1 9.0 %collective-permute-start = (f32[2048]{0:T(1024)S(1)}, f32[2048]{0:T(1024)S(1)}, u32[]{:S(2)}, u32[]{:S(2)}) collective-permute-start(f32[2048]{0:T(1024)S(1)} %broadcast_select_fusion), channel_id=1, source_target_pairs={{0,1},{1,0},{2,3},{3,2},{4,5},{5,4},{6,7},{7,6},{8,9},{9,8},{10,11... | collective-permute-start | bytes 24584 | tf_op jit(solution)/shard_map/ppermute | solution.py:173
